TPU v7x, 128 devices: a whole 4x4x4 slice. The times are simulated.
128 devices in a mesh: blk: 8 (over z, x_lo), rep: 16 (over x_hi, y, core).
Axes of the slice: x: 4 (x_hi: 2, x_lo: 2; x = x_hi * 2 + x_lo), y: 4, z: 4, core: 2. Of those that a mesh axis runs over, the one named last changes fastest.
Arguments:
- raw_features: bfloat16 [131072, 512], P(('blk', 'rep')), may hold values from -6 to 6
- move_plan: int32 [8, 16, 16], P('blk'), may hold values from 8 to 64, as said below
- weight: bfloat16 [512, 512], replicated, may hold values from -0.25 to 0.25
- bias_vector: float32 [512], replicated, may hold values from -3 to 3
- tile_rows: int32 [8, 16, 16, 6], P('blk', 'rep'), may hold values from 0 to 31, as said below
- tile_values: bfloat16 [8, 16, 16, 6, 256, 256], P('blk', 'rep'), may hold values from -0.0546875 to 0.0546875
- grad_out: bfloat16 [65536, 512], P(('blk', 'rep')), may hold values from -6 to 6
Outputs:
- projected: bfloat16 [65536, 512], P(('blk', 'rep'))
- activated: bfloat16 [65536, 512], P(('blk', 'rep'))
- feature_grad: bfloat16 [65536, 512], P(('blk', 'rep'))
- weight_grad: float32 [512, 512], replicated
- bias_grad: float32 [512], replicated
Inputs may be any that keep to these rules, and one draw needn't show every extreme that they name: For every partition p and destination e the counts move_plan[p, s, e] over sources s sum to 512; the counts of one source over destinations sum to at most 1024, and some source of every partition sends 64 rows to every destination. `tile_rows`: the 6 row tiles listed for one column tile of a device are distinct.
All inputs are finite; a program needn't handle non-finite values.
Results may differ from a plain program's by a relative error of at most 0.018.
Values may be sent and summed in bfloat16 or wider, within the bound.
No kernel may reach another device: no remote copies, remote signals or barrier semaphores. Data moves between devices by JAX's collectives and lax.ppermute only.
A program may use at most 192 MiB of HBM per device.

v0:
```python
import math

import jax
import jax.numpy as jnp
from jax import lax
from jax.sharding import PartitionSpec as P


def silu_slope(values):
    sigma = jax.nn.sigmoid(values)
    return sigma * (1.0 + values * (1.0 - sigma))


def per_device(raw_features, move_plan, weight, bias_vector, tile_rows, tile_values, grad_out):
    rep_size = lax.axis_size("rep")
    own_index = lax.axis_index("rep")
    dev_rows, feature_width = grad_out.shape
    raw_rows = raw_features.shape[0]
    capacity = 4 * (dev_rows // (2 * rep_size))
    counts = move_plan[0]
    tile_stack = tile_values[0, 0]
    row_lists = tile_rows[0, 0]
    tile_size = tile_stack.shape[2]
    row_tiles = rep_size * dev_rows // tile_size
    root_count = math.sqrt(dev_rows * lax.axis_size("blk") * rep_size)
    sent_counts = lax.dynamic_index_in_dim(counts, own_index, 0, keepdims=False)
    first_rows = jnp.cumsum(sent_counts) - sent_counts
    slot_rows = first_rows[:, None] + jnp.arange(capacity, dtype=jnp.int32)[None, :]
    outgoing = raw_features[jnp.minimum(slot_rows, raw_rows - 1)]
    incoming = lax.all_to_all(outgoing, "rep", split_axis=0, concat_axis=0, tiled=True)
    recv_counts = lax.dynamic_index_in_dim(counts, own_index, 1, keepdims=False)
    inclusive = jnp.cumsum(recv_counts)
    exclusive = inclusive - recv_counts
    positions = jnp.arange(dev_rows, dtype=jnp.int32)
    sources = jnp.sum((inclusive[None, :] <= positions[:, None]).astype(jnp.int32), axis=1)
    selector = sources[:, None] == jnp.arange(rep_size, dtype=jnp.int32)[None, :]
    offsets = jnp.sum(jnp.where(selector, exclusive[None, :], 0), axis=1)
    features = incoming.reshape(rep_size * capacity, feature_width)[
        sources * capacity + positions - offsets
    ]
    projected = jnp.dot(features, weight, preferred_element_type=jnp.float32).astype(jnp.bfloat16)
    zero_rows = jnp.zeros((row_tiles, tile_size, feature_width), jnp.float32)
    shard_rows = lax.all_gather(projected, "blk", axis=0, tiled=True)

    def column_step(step_index, running):
        adjacency_tile = lax.dynamic_index_in_dim(tile_stack, step_index, 0, keepdims=False)
        targets = lax.dynamic_index_in_dim(row_lists, step_index, 0, keepdims=False)
        inputs = lax.dynamic_slice_in_dim(shard_rows, step_index * tile_size, tile_size, 0)
        matmul_result = jnp.einsum(
            "jab,bf->jaf", adjacency_tile, inputs, preferred_element_type=jnp.float32
        )
        return running.at[targets].add(matmul_result)

    partial_value = lax.fori_loop(0, shard_rows.shape[0] // tile_size, column_step, zero_rows)
    partial_value = partial_value.reshape(row_tiles * tile_size, feature_width)
    preact = (
        lax.psum_scatter(
            partial_value.astype(jnp.bfloat16), "rep", scatter_dimension=0, tiled=True
        ).astype(jnp.float32)
        + bias_vector
    )
    own_grad = (grad_out.astype(jnp.float32) * silu_slope(preact)).astype(jnp.bfloat16)
    pre_grad = lax.all_gather(own_grad, "rep", axis=0, tiled=True)
    activated = jax.nn.silu(preact).astype(jnp.bfloat16)
    grad_tiles = pre_grad.reshape(row_tiles, tile_size, feature_width)
    column_indices = lax.axis_size("blk") * dev_rows // tile_size
    adjacency_tile = tile_stack
    targets = row_lists
    selected_rows = grad_tiles[targets]
    column_contribution = jnp.einsum(
        "nzqm,nzqg->nmg", adjacency_tile, selected_rows, preferred_element_type=jnp.float32
    )
    proj_grad = lax.psum_scatter(
        column_contribution.reshape(column_indices * tile_size, feature_width).astype(jnp.bfloat16),
        "blk",
        scatter_dimension=0,
        tiled=True,
    )
    local_weight = jnp.einsum("nf,ng->fg", features, proj_grad, preferred_element_type=jnp.float32)
    local_bias = jnp.sum(own_grad.astype(jnp.float32), axis=0)
    weight_sum, bias_sum = lax.psum((local_weight, local_bias), ("blk", "rep"))
    feature_grad = jnp.einsum(
        "ng,fg->nf", proj_grad, weight, preferred_element_type=jnp.float32
    ).astype(jnp.bfloat16)
    return (projected, activated, feature_grad, weight_sum / root_count, bias_sum / root_count)


def solution(mesh):
    return jax.shard_map(
        per_device,
        mesh=mesh,
        in_specs=(
            P(("blk", "rep"), None),
            P("blk", None, None),
            P(),
            P(),
            P("blk", "rep", None, None),
            P("blk", "rep", None, None, None, None),
            P(("blk", "rep"), None),
        ),
        out_specs=(
            P(("blk", "rep"), None),
            P(("blk", "rep"), None),
            P(("blk", "rep"), None),
            P(),
            P(),
        ),
        check_vma=False,
    )
```

profile of v0, /device:TPU:1, one launch (start us, length us, event | category | flops | bytes accessed | tf_op | source)
XLA Modules:
  0.0 759.5 jit_solution(11965677881912372824)
XLA Ops:
  9.1 5.1 gather_fusion
  14.2 8.4 %all-to-all-start = ((bf16[16,64,512]{2,1,0:T(8,128)(2,1)}), bf16[16,64,512]{2,1,0:T(8,128)(2,1)S(1)}, u32[]{:S(2)}, u32[]{:S(2)}) async-start(bf16[16,64,512]{2,1,0:T(8,128)(2,1)} %bitcast.6), calls=%async_computation | async-start | bytes 2097152 | tf_op jit(solution)/shard_map/all_to_all | solution.py:30
  23.9 15.8 %all-to-all-done = bf16[16,64,512]{2,1,0:T(8,128)(2,1)S(1)} async-done(((bf16[16,64,512]{2,1,0:T(8,128)(2,1)}), bf16[16,64,512]{2,1,0:T(8,128)(2,1)S(1)}, u32[]{:S(2)}, u32[]{:S(2)}) %all-to-all-start) | async-done | bytes 1048608 | tf_op jit(solution)/shard_map/all_to_all | solution.py:30
  43.1 89.0 %all-gather.3.cloned.1.call-done = bf16[4096,512]{1,0:T(8,128)(2,1)} async-done(((bf16[512,512]{1,0:T(8,128)(2,1)}), bf16[4096,512]{1,0:T(8,128)(2,1)}) %all-gather.3.cloned.1.call-update) | async-done | bytes 4194320 | tf_op jit(solution)/shard_map/all_gather | solution.py:43
  132.1 7.9 %broadcast_in_dim.18 = f32[32,256,512]{2,1,0:T(8,128)} broadcast(f32[]{:T(128)} %constant.89.clone.1), dimensions={} | broadcast | bytes 16777220 | tf_op jit(solution)/shard_map/broadcast_in_dim | solution.py:42
  139.9 150.5 %while.13 = (s32[]{:T(128)}, f32[32,256,512]{2,1,0:T(8,128)}, s32[16,6]{1,0:T(8,128)S(1)}, bf16[16,6,256,256]{3,2,1,0:T(8,128)(2,1)}, bf16[4096,512]{1,0:T(8,128...) while((s32[]{:T(128)}, f32[32,256,512]{2,1,0:T(8,128)}, s32[16,6]{1,0:T(8,128)S(1)}, ...), condition=%wide.region_6.7_spmd, body=%wide.region_4.6_spmd.sunk | while | flops 403439648 | bytes 13632219 | solution.py:54
  141.7 7.7 %scatter_fusion = f32[32,256,512]{2,1,0:T(8,128)} fusion(f32[32,256,512]{2,1,0:T(8,128)} %get-tuple-element.171, s32[6]{0:T(128)S(1)} %fusion.24, f32[6,256,512]{2,1,0:T(8,128)S(1)} %fusion.25), kind=kCustom, calls=%fused_computation.3.clone.1 | custom fusion | flops 786432 | bytes 9437208 | tf_op jit(solution)/shard_map/while/body/eval_jaxpr/scatter-add | solution.py:52
  151.1 7.6 %scatter_fusion = f32[32,256,512]{2,1,0:T(8,128)} fusion(f32[32,256,512]{2,1,0:T(8,128)} %get-tuple-element.171, s32[6]{0:T(128)S(1)} %fusion.24, f32[6,256,512]{2,1,0:T(8,128)S(1)} %fusion.25), kind=kCustom, calls=%fused_computation.3.clone.1 | custom fusion | flops 786432 | bytes 9437208 | tf_op jit(solution)/shard_map/while/body/eval_jaxpr/scatter-add | solution.py:52
  160.5 7.6 %scatter_fusion = f32[32,256,512]{2,1,0:T(8,128)} fusion(f32[32,256,512]{2,1,0:T(8,128)} %get-tuple-element.171, s32[6]{0:T(128)S(1)} %fusion.24, f32[6,256,512]{2,1,0:T(8,128)S(1)} %fusion.25), kind=kCustom, calls=%fused_computation.3.clone.1 | custom fusion | flops 786432 | bytes 9437208 | tf_op jit(solution)/shard_map/while/body/eval_jaxpr/scatter-add | solution.py:52
  169.9 7.6 %scatter_fusion = f32[32,256,512]{2,1,0:T(8,128)} fusion(f32[32,256,512]{2,1,0:T(8,128)} %get-tuple-element.171, s32[6]{0:T(128)S(1)} %fusion.24, f32[6,256,512]{2,1,0:T(8,128)S(1)} %fusion.25), kind=kCustom, calls=%fused_computation.3.clone.1 | custom fusion | flops 786432 | bytes 9437208 | tf_op jit(solution)/shard_map/while/body/eval_jaxpr/scatter-add | solution.py:52
  179.3 7.6 scatter_fusion
  188.6 7.7 %scatter_fusion = f32[32,256,512]{2,1,0:T(8,128)} fusion(f32[32,256,512]{2,1,0:T(8,128)} %get-tuple-element.171, s32[6]{0:T(128)S(1)} %fusion.24, f32[6,256,512]{2,1,0:T(8,128)S(1)} %fusion.25), kind=kCustom, calls=%fused_computation.3.clone.1 | custom fusion | flops 786432 | bytes 9437208 | tf_op jit(solution)/shard_map/while/body/eval_jaxpr/scatter-add | solution.py:52
  198.1 7.6 %scatter_fusion = f32[32,256,512]{2,1,0:T(8,128)} fusion(f32[32,256,512]{2,1,0:T(8,128)} %get-tuple-element.171, s32[6]{0:T(128)S(1)} %fusion.24, f32[6,256,512]{2,1,0:T(8,128)S(1)} %fusion.25), kind=kCustom, calls=%fused_computation.3.clone.1 | custom fusion | flops 786432 | bytes 9437208 | tf_op jit(solution)/shard_map/while/body/eval_jaxpr/scatter-add | solution.py:52
  207.5 7.6 scatter_fusion
  216.9 7.7 %scatter_fusion = f32[32,256,512]{2,1,0:T(8,128)} fusion(f32[32,256,512]{2,1,0:T(8,128)} %get-tuple-element.171, s32[6]{0:T(128)S(1)} %fusion.24, f32[6,256,512]{2,1,0:T(8,128)S(1)} %fusion.25), kind=kCustom, calls=%fused_computation.3.clone.1 | custom fusion | flops 786432 | bytes 9437208 | tf_op jit(solution)/shard_map/while/body/eval_jaxpr/scatter-add | solution.py:52
  226.4 7.6 %scatter_fusion = f32[32,256,512]{2,1,0:T(8,128)} fusion(f32[32,256,512]{2,1,0:T(8,128)} %get-tuple-element.171, s32[6]{0:T(128)S(1)} %fusion.24, f32[6,256,512]{2,1,0:T(8,128)S(1)} %fusion.25), kind=kCustom, calls=%fused_computation.3.clone.1 | custom fusion | flops 786432 | bytes 9437208 | tf_op jit(solution)/shard_map/while/body/eval_jaxpr/scatter-add | solution.py:52
  235.8 7.7 %scatter_fusion = f32[32,256,512]{2,1,0:T(8,128)} fusion(f32[32,256,512]{2,1,0:T(8,128)} %get-tuple-element.171, s32[6]{0:T(128)S(1)} %fusion.24, f32[6,256,512]{2,1,0:T(8,128)S(1)} %fusion.25), kind=kCustom, calls=%fused_computation.3.clone.1 | custom fusion | flops 786432 | bytes 9437208 | tf_op jit(solution)/shard_map/while/body/eval_jaxpr/scatter-add | solution.py:52
  245.3 7.6 %scatter_fusion = f32[32,256,512]{2,1,0:T(8,128)} fusion(f32[32,256,512]{2,1,0:T(8,128)} %get-tuple-element.171, s32[6]{0:T(128)S(1)} %fusion.24, f32[6,256,512]{2,1,0:T(8,128)S(1)} %fusion.25), kind=kCustom, calls=%fused_computation.3.clone.1 | custom fusion | flops 786432 | bytes 9437208 | tf_op jit(solution)/shard_map/while/body/eval_jaxpr/scatter-add | solution.py:52
  254.7 7.6 %scatter_fusion = f32[32,256,512]{2,1,0:T(8,128)} fusion(f32[32,256,512]{2,1,0:T(8,128)} %get-tuple-element.171, s32[6]{0:T(128)S(1)} %fusion.24, f32[6,256,512]{2,1,0:T(8,128)S(1)} %fusion.25), kind=kCustom, calls=%fused_computation.3.clone.1 | custom fusion | flops 786432 | bytes 9437208 | tf_op jit(solution)/shard_map/while/body/eval_jaxpr/scatter-add | solution.py:52
  264.1 7.6 scatter_fusion
  273.4 7.6 %scatter_fusion = f32[32,256,512]{2,1,0:T(8,128)} fusion(f32[32,256,512]{2,1,0:T(8,128)} %get-tuple-element.171, s32[6]{0:T(128)S(1)} %fusion.24, f32[6,256,512]{2,1,0:T(8,128)S(1)} %fusion.25), kind=kCustom, calls=%fused_computation.3.clone.1 | custom fusion | flops 786432 | bytes 9437208 | tf_op jit(solution)/shard_map/while/body/eval_jaxpr/scatter-add | solution.py:52
  282.8 7.6 %scatter_fusion = f32[32,256,512]{2,1,0:T(8,128)} fusion(f32[32,256,512]{2,1,0:T(8,128)} %get-tuple-element.171, s32[6]{0:T(128)S(1)} %fusion.24, f32[6,256,512]{2,1,0:T(8,128)S(1)} %fusion.25), kind=kCustom, calls=%fused_computation.3.clone.1 | custom fusion | flops 786432 | bytes 9437208 | tf_op jit(solution)/shard_map/while/body/eval_jaxpr/scatter-add | solution.py:52
  290.4 9.1 %convert_element_type.41 = bf16[32,256,512]{2,1,0:T(8,128)(2,1)} convert(f32[32,256,512]{2,1,0:T(8,128)} %get-tuple-element.99) | non-fusion elementwise | flops 4194304 | bytes 25165824 | tf_op jit(solution)/shard_map/convert_element_type | solution.py:58
  299.7 101.3 %reduce-scatter.3.cloned.1.call-done = bf16[512,512]{1,0:T(8,128)(2,1)} async-done(((bf16[8192,512]{1,0:T(8,128)(2,1)}), bf16[512,512]{1,0:T(8,128)(2,1)}) %reduce-scatter.3.cloned.1.call-update) | async-done | bytes 524304 | tf_op jit(solution)/shard_map/reduce_scatter | solution.py:57
  401.0 2.5 convert_reduce_fusion
  403.8 73.5 %all-gather.5.cloned.1.call-done = bf16[8192,512]{1,0:T(8,128)(2,1)} async-done(((bf16[512,512]{1,0:T(8,128)(2,1)}), bf16[8192,512]{1,0:T(8,128)(2,1)}) %all-gather.5.cloned.1.call-update) | async-done | bytes 8388624 | tf_op jit(solution)/shard_map/all_gather | solution.py:63
  477.3 13.6 %gather_fusion.2 = bf16[96,256,512]{2,1,0:T(8,128)(2,1)} fusion(bf16[32,256,512]{2,1,0:T(8,128)(2,1)} %bitcast.59, s32[1024]{0:T(1024)S(1)} %pad_clamp_fusion), kind=kCustom, calls=%fused_computation.2 | custom fusion | bytes 50332032 | tf_op jit(solution)/shard_map/gather | solution.py:69
  490.9 17.4 %bitcast_convert_fusion = bf16[16,512,256]{1,2,0:T(8,128)(2,1)} fusion(bf16[16,6,256,512]{3,2,1,0:T(8,128)(2,1)} %bitcast.62, bf16[1,1,16,6,256,256]{5,4,3,2,1,0:T(8,128)(2,1)} %bitcast.65), kind=kOutput, calls=%fused_computation.14 | convolution fusion | flops 6444548096 | bytes 41943040 | tf_op jit(solution)/shard_map/nzqm,nzqg->nmg/dot_general | solution.py:70
  508.4 88.7 %reduce-scatter.5.cloned.1.call-done = bf16[512,512]{1,0:T(8,128)(2,1)} async-done(((bf16[4096,512]{1,0:T(8,128)(2,1)}), bf16[512,512]{1,0:T(8,128)(2,1)}) %reduce-scatter.5.cloned.1.call-update) | async-done | bytes 524304 | tf_op jit(solution)/shard_map/reduce_scatter | solution.py:73
  597.1 2.5 fusion.10
  599.6 64.9 %psum.15 = f32[512]{0:T(512)S(1)} all-reduce(f32[512]{0:T(512)S(1)} %get-tuple-element.125), channel_id=1, replica_groups=mesh['blk'=8,'rep'=16] {'blk','rep'}, use_global_device_ids=true, to_apply=%region_11.12 | all-reduce | flops 512 | bytes 4096 | tf_op jit(solution)/shard_map/psum | solution.py:81
  667.3 83.4 %all-reduce.2.cloned.1.call-done = f32[512,512]{1,0:T(8,128)} async-done(((f32[512,512]{1,0:T(8,128)}), f32[512,512]{1,0:T(8,128)}) %all-reduce.2.cloned.1.call-update) | async-done | bytes 1048592 | tf_op jit(solution)/shard_map/psum | solution.py:81
  (87 shorter events, 40.3 us)
Async XLA Ops:
  7.2 1.9 copy-start
  7.2 34.5 %copy-start.4 = (bf16[512,512]{1,0:T(8,128)(2,1)S(1)}, bf16[512,512]{1,0:T(8,128)(2,1)}, u32[]{:S(2)}) copy-start(bf16[512,512]{1,0:T(8,128)(2,1)} %param.11) | copy-start | bytes 1572868
  7.2 35.8 %copy-start.7 = (s32[1,1,16,6]{2,1,3,0:T(1,128)S(1)}, s32[1,1,16,6]{2,1,3,0:T(1,128)}, u32[]{:S(2)}) copy-start(s32[1,1,16,6]{2,1,3,0:T(1,128)} %param.13) | copy-start | bytes 1156
  14.2 25.5 %all-to-all-start = ((bf16[16,64,512]{2,1,0:T(8,128)(2,1)}), bf16[16,64,512]{2,1,0:T(8,128)(2,1)S(1)}, u32[]{:S(2)}, u32[]{:S(2)}) async-start(bf16[16,64,512]{2,1,0:T(8,128)(2,1)} %bitcast.6), calls=%async_computation | async-start | bytes 2097152 | tf_op jit(solution)/shard_map/all_to_all | solution.py:30
  22.6 109.4 %all-gather.3.cloned.1.call-start = ((), (), s32[]{:S(2)}) async-start(), calls=%async_computation.3 | async-start | bytes 4718592 | tf_op jit(solution)/shard_map/all_gather | solution.py:43
  41.7 98.2 %copy-start.2 = (bf16[512,512]{1,0:T(8,128)(2,1)}, bf16[512,512]{1,0:T(8,128)(2,1)S(1)}, u32[]{:S(2)}) copy-start(bf16[512,512]{1,0:T(8,128)(2,1)S(1)} %gather_fusion.1) | copy-start | bytes 1572868
  43.0 358.0 %reduce-scatter.3.cloned.1.call-start = ((), (), s32[]{:S(2)}) async-start(), calls=%async_computation.4 | async-start | bytes 8912896 | tf_op jit(solution)/shard_map/reduce_scatter | solution.py:57
  290.4 110.6 %copy-start.6 = (bf16[512,512]{1,0:T(8,128)(2,1)S(1)}, bf16[512,512]{1,0:T(8,128)(2,1)}, u32[]{:S(2)}) copy-start(bf16[512,512]{1,0:T(8,128)(2,1)} %param.15) | copy-start | bytes 1572868
  290.4 110.6 %copy-start.8 = (f32[512]{0:T(512)S(1)}, f32[512]{0:T(512)}, u32[]{:S(2)}) copy-start(f32[512]{0:T(512)} %param.12) | copy-start | bytes 6148
  299.6 177.7 %all-gather.5.cloned.1.call-start = ((), (), s32[]{:S(2)}) async-start(), calls=%async_computation.5 | async-start | bytes 8912896 | tf_op jit(solution)/shard_map/all_gather | solution.py:63
  403.6 193.5 %reduce-scatter.5.cloned.1.call-start = ((), (), s32[]{:S(2)}) async-start(), calls=%async_computation.6 | async-start | bytes 4718592 | tf_op jit(solution)/shard_map/reduce_scatter | solution.py:73
  490.9 106.1 %copy-start.3 = (bf16[512,512]{1,0:T(8,128)(2,1)S(1)}, bf16[512,512]{1,0:T(8,128)(2,1)}, u32[]{:S(2)}) copy-start(bf16[512,512]{1,0:T(8,128)(2,1)} %copy-done.2) | copy-start | bytes 1572868
  490.9 174.1 %copy-start.5 = (bf16[512,512]{1,0:T(8,128)(2,1)S(1)}, bf16[512,512]{1,0:T(8,128)(2,1)}, u32[]{:S(2)}) copy-start(bf16[512,512]{1,0:T(8,128)(2,1)} %param.11) | copy-start | bytes 1572868
  490.9 262.1 %copy-start.1 = (bf16[1024,512]{1,0:T(8,128)(2,1)S(1)}, bf16[1024,512]{1,0:T(8,128)(2,1)}, u32[]{:S(2)}) copy-start(bf16[1024,512]{1,0:T(8,128)(2,1)} %param.9) | copy-start | bytes 3145732
  508.3 242.4 %all-reduce.2.cloned.1.call-start = ((), (), s32[]{:S(2)}) async-start(), calls=%async_computation.7 | async-start | bytes 2097152 | tf_op jit(solution)/shard_map/psum | solution.py:81
Sparse Core Ops, SparseCore 0:
  43.1 88.9 all-gather.2
  299.7 101.2 reduce-scatter.2
  404.0 73.2 all-gather.4
  508.4 88.5 reduce-scatter.4
  602.3 148.4 all-reduce.1
where the time goes:
time: 761 us; the launch traced here: 760 us
  waiting for transfers between devices  452 us (59%)
  other arithmetic  138 us (18%)
  blocking collectives  64.9 us (9%)
  matrix products  51.4 us (7%)
  local copies, waits for them, and re-layouts  30.7 us (4%)
  between operations  13.9 us (2%)
  starting transfers between devices  8.64 us (1%)
    scatter-add x16, other arithmetic, column_step(): return running.at[targets].add(matmul_result)  122 us
    reduce_scatter x1, waiting for transfers between devices, per_device(): lax.psum_scatter(partial_value.astype(jnp.bfloat16), 'rep', scatter_dimen...  101 us
    all_gather x1, waiting for transfers between devices, per_device(): shard_rows = lax.all_gather(projected, 'blk', axis=0, tiled=True)  89 us
    reduce_scatter x1, waiting for transfers between devices, per_device(): lax.psum_scatter(column_contribution.reshape(column_indices * tile_size,...  88.7 us
    psum x1, waiting for transfers between devices, per_device(): weight_sum, bias_sum = lax.psum((local_weight, local_bias), ('blk', 'rep'))  83.4 us
    all_gather x1, waiting for transfers between devices, per_device(): pre_grad = lax.all_gather(own_grad, 'rep', axis=0, tiled=True)  73.5 us
    psum x1, blocking collectives, per_device(): weight_sum, bias_sum = lax.psum((local_weight, local_bias), ('blk', 'rep'))  64.9 us
    dot_general x16, matrix products, column_step(): jnp.einsum('jab,bf->jaf', adjacency_tile, inputs, preferred_element_type=...  28 us
  transfers between devices with their start and end apart: 6, of which 6 were waited for; matrix products, arithmetic and copies ran while one was open for 1% of the time, Pallas kernels for 0%

commit v1 on v0

--- a/solution.py
+++ b/solution.py
@@ -1,14 +1,98 @@
+import functools
 import math
 
 import jax
 import jax.numpy as jnp
 from jax import lax
+from jax.experimental import pallas as pl
+from jax.experimental.pallas import tpu as pltpu
 from jax.sharding import PartitionSpec as P
 
 
 def silu_slope(values):
     sigma = jax.nn.sigmoid(values)
     return sigma * (1.0 + values * (1.0 - sigma))
+
+
+def _forward_kernel(rows_ref, tiles_ref, cols_ref, out_ref, acc_ref):
+    step = pl.program_id(0)
+    fill = tiles_ref.shape[1]
+
+    @pl.when(step == 0)
+    def _():
+        acc_ref[...] = jnp.zeros_like(acc_ref)
+
+    inputs = cols_ref[...]
+    for j in range(fill):
+        target = rows_ref[step, j]
+        acc_ref[target] += jnp.dot(tiles_ref[0, j], inputs, preferred_element_type=jnp.float32)
+
+    @pl.when(step == pl.num_programs(0) - 1)
+    def _():
+        out_ref[...] = acc_ref[...].astype(out_ref.dtype)
+
+
+def forward_spmm(row_lists, tile_stack, shard_rows, row_tiles, interpret=False):
+    col_tiles, fill, tile_size, _ = tile_stack.shape
+    width = shard_rows.shape[1]
+    grid_spec = pltpu.PrefetchScalarGridSpec(
+        num_scalar_prefetch=1,
+        grid=(col_tiles,),
+        in_specs=[
+            pl.BlockSpec((1, fill, tile_size, tile_size), lambda c, rows: (c, 0, 0, 0)),
+            pl.BlockSpec((tile_size, width), lambda c, rows: (c, 0)),
+        ],
+        out_specs=pl.BlockSpec((row_tiles, tile_size, width), lambda c, rows: (0, 0, 0)),
+        scratch_shapes=[pltpu.VMEM((row_tiles, tile_size, width), jnp.float32)],
+    )
+    return pl.pallas_call(
+        _forward_kernel,
+        grid_spec=grid_spec,
+        out_shape=jax.ShapeDtypeStruct((row_tiles, tile_size, width), jnp.bfloat16),
+        compiler_params=pltpu.CompilerParams(
+            dimension_semantics=("arbitrary",), vmem_limit_bytes=56 * 1024 * 1024
+        ),
+        interpret=interpret,
+    )(row_lists, tile_stack, shard_rows)
+
+
+def _backward_kernel(rows_ref, tiles_ref, grad_ref, out_ref):
+    step = pl.program_id(0)
+    fill = tiles_ref.shape[1]
+    total = None
+    for j in range(fill):
+        source = rows_ref[step, j]
+        part = lax.dot_general(
+            tiles_ref[0, j],
+            grad_ref[source],
+            (((0,), (0,)), ((), ())),
+            preferred_element_type=jnp.float32,
+        )
+        total = part if total is None else total + part
+    out_ref[...] = total.astype(out_ref.dtype)
+
+
+def backward_spmm(row_lists, tile_stack, grad_tiles, interpret=False):
+    col_tiles, fill, tile_size, _ = tile_stack.shape
+    row_tiles, _, width = grad_tiles.shape
+    grid_spec = pltpu.PrefetchScalarGridSpec(
+        num_scalar_prefetch=1,
+        grid=(col_tiles,),
+        in_specs=[
+            pl.BlockSpec((1, fill, tile_size, tile_size), lambda c, rows: (c, 0, 0, 0)),
+            pl.BlockSpec((row_tiles, tile_size, width), lambda c, rows: (0, 0, 0)),
+        ],
+        out_specs=pl.BlockSpec((tile_size, width), lambda c, rows: (c, 0)),
+    )
+    return pl.pallas_call(
+        _backward_kernel,
+        grid_spec=grid_spec,
+        out_shape=jax.ShapeDtypeStruct((col_tiles * tile_size, width), jnp.bfloat16),
+        compiler_params=pltpu.CompilerParams(
+            dimension_semantics=("arbitrary",), vmem_limit_bytes=56 * 1024 * 1024
+        ),
+        interpret=interpret,
+    )(row_lists, tile_stack, grad_tiles)
 
 
 def per_device(raw_features, move_plan, weight, bias_vector, tile_rows, tile_values, grad_out):
@@ -39,46 +123,27 @@
         sources * capacity + positions - offsets
     ]
     projected = jnp.dot(features, weight, preferred_element_type=jnp.float32).astype(jnp.bfloat16)
-    zero_rows = jnp.zeros((row_tiles, tile_size, feature_width), jnp.float32)
     shard_rows = lax.all_gather(projected, "blk", axis=0, tiled=True)
 
-    def column_step(step_index, running):
-        adjacency_tile = lax.dynamic_index_in_dim(tile_stack, step_index, 0, keepdims=False)
-        targets = lax.dynamic_index_in_dim(row_lists, step_index, 0, keepdims=False)
-        inputs = lax.dynamic_slice_in_dim(shard_rows, step_index * tile_size, tile_size, 0)
-        matmul_result = jnp.einsum(
-            "jab,bf->jaf", adjacency_tile, inputs, preferred_element_type=jnp.float32
-        )
-        return running.at[targets].add(matmul_result)
-
-    partial_value = lax.fori_loop(0, shard_rows.shape[0] // tile_size, column_step, zero_rows)
+    partial_value = forward_spmm(row_lists, tile_stack, shard_rows, row_tiles)
     partial_value = partial_value.reshape(row_tiles * tile_size, feature_width)
     preact = (
-        lax.psum_scatter(
-            partial_value.astype(jnp.bfloat16), "rep", scatter_dimension=0, tiled=True
-        ).astype(jnp.float32)
+        lax.psum_scatter(partial_value, "rep", scatter_dimension=0, tiled=True).astype(jnp.float32)
         + bias_vector
     )
     own_grad = (grad_out.astype(jnp.float32) * silu_slope(preact)).astype(jnp.bfloat16)
     pre_grad = lax.all_gather(own_grad, "rep", axis=0, tiled=True)
     activated = jax.nn.silu(preact).astype(jnp.bfloat16)
     grad_tiles = pre_grad.reshape(row_tiles, tile_size, feature_width)
-    column_indices = lax.axis_size("blk") * dev_rows // tile_size
-    adjacency_tile = tile_stack
-    targets = row_lists
-    selected_rows = grad_tiles[targets]
-    column_contribution = jnp.einsum(
-        "nzqm,nzqg->nmg", adjacency_tile, selected_rows, preferred_element_type=jnp.float32
-    )
-    proj_grad = lax.psum_scatter(
-        column_contribution.reshape(column_indices * tile_size, feature_width).astype(jnp.bfloat16),
-        "blk",
-        scatter_dimension=0,
-        tiled=True,
-    )
+    column_contribution = backward_spmm(row_lists, tile_stack, grad_tiles)
+    proj_grad = lax.psum_scatter(column_contribution, "blk", scatter_dimension=0, tiled=True)
     local_weight = jnp.einsum("nf,ng->fg", features, proj_grad, preferred_element_type=jnp.float32)
     local_bias = jnp.sum(own_grad.astype(jnp.float32), axis=0)
-    weight_sum, bias_sum = lax.psum((local_weight, local_bias), ("blk", "rep"))
+    pad_rows = jnp.zeros((7, feature_width), jnp.float32)
+    stacked = jnp.concatenate([local_weight, local_bias[None, :], pad_rows], axis=0)
+    stacked_sum = lax.psum(stacked, ("blk", "rep"))
+    weight_sum = stacked_sum[:feature_width]
+    bias_sum = stacked_sum[feature_width]
     feature_grad = jnp.einsum(
         "ng,fg->nf", proj_grad, weight, preferred_element_type=jnp.float32
     ).astype(jnp.bfloat16)

time: 761 us -> 604 us (0.79)
  other arithmetic: 138 us -> 8.58 us
  waiting for transfers between devices: 452 us -> 517 us
  blocking collectives: 64.9 us -> 0 us
  matrix products: 51.4 us -> 4 us
  Pallas kernels: 0 us -> 40.9 us
  local copies, waits for them, and re-layouts: 30.7 us -> 8.96 us
    scatter-add x16 -> x0, other arithmetic: 122 us -> none  [column_step(): return running.at[targets].add(matmul_result)]
    psum x1, waiting for transfers between devices: 83.4 us -> 149 us  [per_device(): stacked_sum = lax.psum(stacked, ('blk', 'rep'))]
    psum x1 -> x0, blocking collectives: 64.9 us -> none  [per_device(): weight_sum, bias_sum = lax.psum((local_weight, local_bias), ('blk', 'rep'))]
    dot_general x17 -> x0, matrix products: 45.4 us -> none  [the longest x16 28 us: column_step(): jnp.einsum('jab,bf->jaf', adjacency_tile, inputs, preferred_element_type=...]
    pallas_call x0 -> x2, Pallas kernels: none -> 40.9 us  [the longest x1 21.2 us: forward_spmm(): pl.pallas_call(_forward_kernel, grid_spec=grid_spec, out_shape=jax.ShapeD...]
    gather x1 -> x0, local copies, waits for them, and re-layouts: 13.6 us -> none  [per_device(): selected_rows = grad_tiles[targets]]
    convert_element_type x1 -> x0, other arithmetic: 9.14 us -> none  [per_device(): partial_value.astype(jnp.bfloat16)]
    broadcast_in_dim x1, local copies, waits for them, and re-layouts: 7.87 us -> 0.01 us  [per_device(): pad_rows = jnp.zeros((7, feature_width), jnp.float32)]
  transfers between devices with their start and end apart: 6 -> 6, of which waited for: 6 -> 6; matrix products, arithmetic and copies ran while one was open for 1% -> 0% of each run, Pallas kernels for 0% -> 0%
where the time goes in v1:
time: 604 us; the launch traced here: 602 us
  waiting for transfers between devices  517 us (86%)
  Pallas kernels  40.9 us (7%)
  between operations  13.9 us (2%)
  local copies, waits for them, and re-layouts  8.96 us (1%)
  starting transfers between devices  8.77 us (1%)
  other arithmetic  8.58 us (1%)
    psum x1, waiting for transfers between devices, per_device(): stacked_sum = lax.psum(stacked, ('blk', 'rep'))  149 us
    reduce_scatter x1, waiting for transfers between devices, per_device(): lax.psum_scatter(partial_value, 'rep', scatter_dimension=0, tiled=True)  101 us
    reduce_scatter x1, waiting for transfers between devices, per_device(): lax.psum_scatter(column_contribution, 'blk', scatter_dimension=0, tiled=T...  88.6 us
    all_gather x1, waiting for transfers between devices, per_device(): shard_rows = lax.all_gather(projected, 'blk', axis=0, tiled=True)  88.4 us
    all_gather x1, waiting for transfers between devices, per_device(): pre_grad = lax.all_gather(own_grad, 'rep', axis=0, tiled=True)  73.7 us
    pallas_call x1, Pallas kernels, forward_spmm(): pl.pallas_call(_forward_kernel, grid_spec=grid_spec, out_shape=jax.ShapeD...  21.2 us
    pallas_call x1, Pallas kernels, backward_spmm(): pl.pallas_call(_backward_kernel, grid_spec=grid_spec, out_shape=jax.Shape...  19.7 us
    all_to_all x1, waiting for transfers between devices, per_device(): lax.all_to_all(outgoing, 'rep', split_axis=0, concat_axis=0, tiled=True)  16.5 us
  transfers between devices with their start and end apart: 6, of which 6 were waited for; matrix products, arithmetic and copies ran while one was open for 0% of the time, Pallas kernels for 0%

profile of v1, /device:TPU:1, one launch (start us, length us, event | category | flops | bytes accessed | tf_op | source)
XLA Modules:
  0.0 602.4 jit_solution(2006747058370754225)
XLA Ops:
  7.2 0.8 fusion
  8.0 0.1 copy.20
  8.1 0.1 reduce
  8.2 0.7 bitcast_subtract_fusion
  8.9 0.1 compare_select_fusion
  9.0 0.1 reshape.170
  9.1 5.1 gather_fusion
  14.1 8.6 %all-to-all-start = ((bf16[16,64,512]{2,1,0:T(8,128)(2,1)}), bf16[16,64,512]{2,1,0:T(8,128)(2,1)S(1)}, u32[]{:S(2)}, u32[]{:S(2)}) async-start(bf16[16,64,512]{2,1,0:T(8,128)(2,1)} %bitcast.2), calls=%async_computation | async-start | bytes 2097152 | tf_op jit(solution)/shard_map/all_to_all | solution.py:114
  22.8 0.2 dynamic-slice_reduce_fusion
  23.0 0.1 reduce.1
  23.1 0.1 convert_reduce_fusion.1
  23.2 0.1 select_reduce_fusion
  23.3 16.5 %all-to-all-done = bf16[16,64,512]{2,1,0:T(8,128)(2,1)S(1)} async-done(((bf16[16,64,512]{2,1,0:T(8,128)(2,1)}), bf16[16,64,512]{2,1,0:T(8,128)(2,1)S(1)}, u32[]{:S(2)}, u32[]{:S(2)}) %all-to-all-start) | async-done | bytes 1048608 | tf_op jit(solution)/shard_map/all_to_all | solution.py:114
  39.8 2.0 gather_fusion.1
  41.8 1.2 convolution_convert_fusion.1
  43.0 0.0 reduce-scatter.3.cloned.1.call-start
  43.1 0.7 copy.24
  43.8 88.4 %all-gather.3.cloned.1.call-done.cols_ref = bf16[4096,512]{1,0:T(8,128)(2,1)} async-done(((bf16[512,512]{1,0:T(8,128)(2,1)}), bf16[4096,512]{1,0:T(8,128)(2,1)}) %all-gather.3.cloned.1.call-update) | async-done | bytes 4194320 | tf_op jit(solution)/shard_map/all_gather | solution.py:126
  132.2 21.2 %shard_map.110 = bf16[32,256,512]{2,1,0:T(8,128)(2,1)} custom-call(s32[16,6]{1,0:T(8,128)} %bitcast.30, bf16[16,6,256,256]{3,2,1,0:T(8,128)(2,1)} %bitcast.25, bf16[4096,512]{1,0:T(8,128)(2,1)} %all-gather.3.cloned.1.call-done.cols_ref), custom_call_target="tpu_custom_call" | custom-call | tf_op jit(solution)/shard_map/pallas_call | solution.py:48
  153.4 101.0 %reduce-scatter.3.cloned.1.call-done = bf16[512,512]{1,0:T(8,128)(2,1)} async-done(((bf16[8192,512]{1,0:T(8,128)(2,1)}), bf16[512,512]{1,0:T(8,128)(2,1)}) %reduce-scatter.3.cloned.1.call-update) | async-done | bytes 524304 | tf_op jit(solution)/shard_map/reduce_scatter | solution.py:131
  254.4 2.5 convert_reduce_fusion
  257.0 73.7 %all-gather.5.cloned.1.call-done = bf16[8192,512]{1,0:T(8,128)(2,1)} async-done(((bf16[512,512]{1,0:T(8,128)(2,1)}), bf16[8192,512]{1,0:T(8,128)(2,1)}) %all-gather.5.cloned.1.call-update) | async-done | bytes 8388624 | tf_op jit(solution)/shard_map/all_gather | solution.py:135
  330.7 19.7 %shard_map.111 = bf16[4096,512]{1,0:T(8,128)(2,1)} custom-call(s32[16,6]{1,0:T(8,128)} %bitcast.31, bf16[16,6,256,256]{3,2,1,0:T(8,128)(2,1)} %bitcast.26, bf16[32,256,512]{2,1,0:T(8,128)(2,1)} %bitcast.29), custom_call_target="tpu_custom_call" | custom-call | tf_op jit(solution)/shard_map/pallas_call | solution.py:87
  350.4 0.0 all-reduce.2.cloned.1.call-start
  350.5 0.1 pad.2.clone
  350.6 88.6 %reduce-scatter.5.cloned.1.call-done = bf16[512,512]{1,0:T(8,128)(2,1)} async-done(((bf16[4096,512]{1,0:T(8,128)(2,1)}), bf16[512,512]{1,0:T(8,128)(2,1)}) %reduce-scatter.5.cloned.1.call-update) | async-done | bytes 524304 | tf_op jit(solution)/shard_map/reduce_scatter | solution.py:139
  439.2 1.5 fusion.1
  440.7 1.2 maximum_maximum_fusion
  441.9 1.3 convolution_convert_fusion
  443.2 149.1 %all-reduce.2.cloned.1.call-done = f32[520,512]{1,0:T(8,128)} async-done(((f32[520,512]{1,0:T(8,128)}), f32[520,512]{1,0:T(8,128)}) %all-reduce.2.cloned.1.call-update) | async-done | bytes 1064976 | tf_op jit(solution)/shard_map/psum | solution.py:144
  592.3 2.3 slice_multiply_fusion
  594.6 1.3 slice_multiply_fusion.1
  (30 shorter events, 0.3 us)
Async XLA Ops:
  7.2 1.9 copy-start
  14.1 8.6 %copy-start.4 = (s32[1,16,16]{2,1,0:T(8,128)S(1)}, s32[1,16,16]{2,1,0:T(8,128)}, u32[]{:S(2)}) copy-start(s32[1,16,16]{2,1,0:T(8,128)} %param.8) | copy-start | bytes 3076
  14.1 25.6 %all-to-all-start = ((bf16[16,64,512]{2,1,0:T(8,128)(2,1)}), bf16[16,64,512]{2,1,0:T(8,128)(2,1)S(1)}, u32[]{:S(2)}, u32[]{:S(2)}) async-start(bf16[16,64,512]{2,1,0:T(8,128)(2,1)} %bitcast.2), calls=%async_computation | async-start | bytes 2097152 | tf_op jit(solution)/shard_map/all_to_all | solution.py:114
  22.7 109.4 %all-gather.3.cloned.1.call-start = ((), (), s32[]{:S(2)}) async-start(), calls=%async_computation.3 | async-start | bytes 4718592 | tf_op jit(solution)/shard_map/all_gather | solution.py:126
  39.8 2.0 copy-start.1
  41.8 1.3 copy-start.5
  43.0 211.4 %reduce-scatter.3.cloned.1.call-start = ((), (), s32[]{:S(2)}) async-start(), calls=%async_computation.4 | async-start | bytes 8912896 | tf_op jit(solution)/shard_map/reduce_scatter | solution.py:131
  153.4 101.0 %copy-start.3 = (bf16[512,512]{1,0:T(8,128)(2,1)S(1)}, bf16[512,512]{1,0:T(8,128)(2,1)}, u32[]{:S(2)}) copy-start(bf16[512,512]{1,0:T(8,128)(2,1)} %param.13) | copy-start | bytes 1572868
  153.4 101.0 %copy-start.6 = (f32[512]{0:T(512)S(1)}, f32[512]{0:T(512)}, u32[]{:S(2)}) copy-start(f32[512]{0:T(512)} %param.10) | copy-start | bytes 6148
  153.4 177.3 %all-gather.5.cloned.1.call-start = ((), (), s32[]{:S(2)}) async-start(), calls=%async_computation.5 | async-start | bytes 8912896 | tf_op jit(solution)/shard_map/all_gather | solution.py:135
  257.0 182.2 %reduce-scatter.5.cloned.1.call-start = ((), (), s32[]{:S(2)}) async-start(), calls=%async_computation.6 | async-start | bytes 4718592 | tf_op jit(solution)/shard_map/reduce_scatter | solution.py:139
  350.4 241.9 %all-reduce.2.cloned.1.call-start = ((), (), s32[]{:S(2)}) async-start(), calls=%async_computation.7 | async-start | bytes 2129920 | tf_op jit(solution)/shard_map/psum | solution.py:144
  440.7 1.2 copy-start.2
Sparse Core Ops, SparseCore 0:
  43.2 88.9 all-gather.2
  153.5 100.8 reduce-scatter.2
  257.4 73.2 all-gather.4
  350.6 88.5 reduce-scatter.4
  443.8 148.4 all-reduce.1

commit v2 on v1

--- a/solution.py
+++ b/solution.py
@@ -95,6 +95,17 @@
     )(row_lists, tile_stack, grad_tiles)
 
 
+def gather_by_exchange(values, axis, count):
+    stacked = jnp.broadcast_to(values[None], (count,) + values.shape)
+    return lax.all_to_all(stacked, axis, 0, 0, tiled=True)
+
+
+def reduce_by_exchange(values, axis, count):
+    chunks = values.reshape((count, values.shape[0] // count) + values.shape[1:])
+    received = lax.all_to_all(chunks, axis, 0, 0, tiled=True)
+    return jnp.sum(received.astype(jnp.float32), axis=0)
+
+
 def per_device(raw_features, move_plan, weight, bias_vector, tile_rows, tile_values, grad_out):
     rep_size = lax.axis_size("rep")
     own_index = lax.axis_index("rep")
@@ -123,7 +134,8 @@
         sources * capacity + positions - offsets
     ]
     projected = jnp.dot(features, weight, preferred_element_type=jnp.float32).astype(jnp.bfloat16)
-    shard_rows = lax.all_gather(projected, "blk", axis=0, tiled=True)
+    blk_size = lax.axis_size("blk")
+    shard_rows = gather_by_exchange(projected, "blk", blk_size).reshape(-1, feature_width)
 
     partial_value = forward_spmm(row_lists, tile_stack, shard_rows, row_tiles)
     partial_value = partial_value.reshape(row_tiles * tile_size, feature_width)
@@ -136,12 +148,17 @@
     activated = jax.nn.silu(preact).astype(jnp.bfloat16)
     grad_tiles = pre_grad.reshape(row_tiles, tile_size, feature_width)
     column_contribution = backward_spmm(row_lists, tile_stack, grad_tiles)
-    proj_grad = lax.psum_scatter(column_contribution, "blk", scatter_dimension=0, tiled=True)
+    proj_grad = reduce_by_exchange(column_contribution, "blk", blk_size).astype(jnp.bfloat16)
     local_weight = jnp.einsum("nf,ng->fg", features, proj_grad, preferred_element_type=jnp.float32)
     local_bias = jnp.sum(own_grad.astype(jnp.float32), axis=0)
-    pad_rows = jnp.zeros((7, feature_width), jnp.float32)
+    device_count = blk_size * rep_size
+    chunk_rows = feature_width // device_count + 1
+    pad_rows = jnp.zeros((device_count * chunk_rows - feature_width - 1, feature_width), jnp.float32)
     stacked = jnp.concatenate([local_weight, local_bias[None, :], pad_rows], axis=0)
-    stacked_sum = lax.psum(stacked, ("blk", "rep"))
+    reduced = reduce_by_exchange(stacked, ("blk", "rep"), device_count)
+    stacked_sum = gather_by_exchange(reduced, ("blk", "rep"), device_count).reshape(
+        -1, feature_width
+    )
     weight_sum = stacked_sum[:feature_width]
     bias_sum = stacked_sum[feature_width]
     feature_grad = jnp.einsum(

time: 604 us -> 459 us (0.76)
  waiting for transfers between devices: 517 us -> 314 us
  blocking collectives: 0 us -> 35.3 us
  starting transfers between devices: 8.77 us -> 23.2 us
  local copies, waits for them, and re-layouts: 8.96 us -> 15.9 us
    psum x1 -> x0, waiting for transfers between devices: 149 us -> none  [per_device(): stacked_sum = lax.psum(stacked, ('blk', 'rep'))]
    all_to_all x0 -> x3, waiting for transfers between devices: none -> 124 us  [the longest x2 75 us: gather_by_exchange(): return lax.all_to_all(stacked, axis, 0, 0, tiled=True)]
    reduce_scatter x1 -> x0, waiting for transfers between devices: 88.6 us -> none  [per_device(): lax.psum_scatter(column_contribution, 'blk', scatter_dimension=0, tiled=T...]
    all_gather x1 -> x0, waiting for transfers between devices: 88.4 us -> none  [per_device(): shard_rows = lax.all_gather(projected, 'blk', axis=0, tiled=True)]
    all_to_all x0 -> x1, blocking collectives: none -> 35.3 us  [reduce_by_exchange(): received = lax.all_to_all(chunks, axis, 0, 0, tiled=True)]
    all_to_all x0 -> x3, starting transfers between devices: none -> 14.6 us  [the longest x2 10 us: gather_by_exchange(): return lax.all_to_all(stacked, axis, 0, 0, tiled=True)]
  transfers between devices with their start and end apart: 6 -> 6, of which waited for: 6 -> 6; matrix products, arithmetic and copies ran while one was open for 0% -> 1% of each run, Pallas kernels for 0% -> 0%
where the time goes in v2:
time: 459 us; the launch traced here: 457 us
  waiting for transfers between devices  314 us (68%)
  Pallas kernels  40.9 us (9%)
  blocking collectives  35.3 us (8%)
  starting transfers between devices  23.2 us (5%)
  local copies, waits for them, and re-layouts  15.9 us (3%)
  between operations  14.2 us (3%)
  other arithmetic  10.8 us (2%)
    reduce_scatter x1, waiting for transfers between devices, per_device(): lax.psum_scatter(partial_value, 'rep', scatter_dimension=0, tiled=True)  99.1 us
    all_to_all x2, waiting for transfers between devices, gather_by_exchange(): return lax.all_to_all(stacked, axis, 0, 0, tiled=True)  75 us
    all_gather x1, waiting for transfers between devices, per_device(): pre_grad = lax.all_gather(own_grad, 'rep', axis=0, tiled=True)  73.7 us
    all_to_all x1, waiting for transfers between devices, reduce_by_exchange(): received = lax.all_to_all(chunks, axis, 0, 0, tiled=True)  49.2 us
    all_to_all x1, blocking collectives, reduce_by_exchange(): received = lax.all_to_all(chunks, axis, 0, 0, tiled=True)  35.3 us
    pallas_call x1, Pallas kernels, forward_spmm(): pl.pallas_call(_forward_kernel, grid_spec=grid_spec, out_shape=jax.ShapeD...  21.2 us
    pallas_call x1, Pallas kernels, backward_spmm(): pl.pallas_call(_backward_kernel, grid_spec=grid_spec, out_shape=jax.Shape...  19.7 us
    all_to_all x1, waiting for transfers between devices, per_device(): lax.all_to_all(outgoing, 'rep', split_axis=0, concat_axis=0, tiled=True)  16.5 us
  transfers between devices with their start and end apart: 6, of which 6 were waited for; matrix products, arithmetic and copies ran while one was open for 1% of the time, Pallas kernels for 0%

profile of v2, /device:TPU:1, one launch (start us, length us, event | category | flops | bytes accessed | tf_op | source)
XLA Modules:
  0.0 457.4 jit_solution(12890287143325892435)
XLA Ops:
  7.2 0.8 fusion
  8.2 0.7 bitcast_subtract_fusion
  9.1 5.1 %gather_fusion = bf16[1024,512]{1,0:T(8,128)(2,1)} fusion(bf16[1024,512]{1,0:T(8,128)(2,1)S(1)} %copy-done, s32[1024]{0:T(1024)S(1)} %broadcast_clamp_fusion), kind=kCustom, calls=%fused_computation | custom fusion | bytes 2101248 | tf_op jit(solution)/shard_map/gather | solution.py:124
  14.1 8.6 %all-to-all-start = ((bf16[16,64,512]{2,1,0:T(8,128)(2,1)}), bf16[16,64,512]{2,1,0:T(8,128)(2,1)S(1)}, u32[]{:S(2)}, u32[]{:S(2)}) async-start(bf16[16,64,512]{2,1,0:T(8,128)(2,1)} %bitcast.2), calls=%async_computation | async-start | bytes 2097152 | tf_op jit(solution)/shard_map/all_to_all | solution.py:125
  22.7 0.2 dynamic-slice_reduce_fusion
  23.3 16.5 %all-to-all-done = bf16[16,64,512]{2,1,0:T(8,128)(2,1)S(1)} async-done(((bf16[16,64,512]{2,1,0:T(8,128)(2,1)}), bf16[16,64,512]{2,1,0:T(8,128)(2,1)S(1)}, u32[]{:S(2)}, u32[]{:S(2)}) %all-to-all-start) | async-done | bytes 1048608 | tf_op jit(solution)/shard_map/all_to_all | solution.py:125
  39.8 2.0 gather_fusion.1
  41.8 0.4 convolution_convert_fusion.1
  42.2 2.3 broadcast_in_dim.22
  44.5 5.2 %all-to-all-start.1 = ((bf16[8,512,512]{2,1,0:T(8,128)(2,1)}), bf16[8,512,512]{2,1,0:T(8,128)(2,1)}, u32[]{:S(2)}, u32[]{:S(2)}) async-start(bf16[8,512,512]{2,1,0:T(8,128)(2,1)} %broadcast_in_dim.22), calls=%async_computation.1 | async-start | bytes 8388608 | tf_op jit(solution)/shard_map/all_to_all | solution.py:100
  49.8 0.7 copy.24
  50.5 47.6 %all-to-all-done.1 = bf16[8,512,512]{2,1,0:T(8,128)(2,1)} async-done(((bf16[8,512,512]{2,1,0:T(8,128)(2,1)}), bf16[8,512,512]{2,1,0:T(8,128)(2,1)}, u32[]{:S(2)}, u32[]{:S(2)}) %all-to-all-start.1) | async-done | bytes 4194336 | tf_op jit(solution)/shard_map/all_to_all | solution.py:100
  98.1 21.2 %shard_map.110 = bf16[32,256,512]{2,1,0:T(8,128)(2,1)} custom-call(s32[16,6]{1,0:T(8,128)} %bitcast.33, bf16[16,6,256,256]{3,2,1,0:T(8,128)(2,1)} %bitcast.27, bf16[4096,512]{1,0:T(8,128)(2,1)} %bitcast.9.cols_ref), custom_call_target="tpu_custom_call" | custom-call | tf_op jit(solution)/shard_map/pallas_call | solution.py:48
  119.4 99.1 %reduce-scatter.2.cloned.1.call-done = bf16[512,512]{1,0:T(8,128)(2,1)} async-done(((bf16[8192,512]{1,0:T(8,128)(2,1)}), bf16[512,512]{1,0:T(8,128)(2,1)}) %reduce-scatter.2.cloned.1.call-update) | async-done | bytes 524304 | tf_op jit(solution)/shard_map/reduce_scatter | solution.py:143
  218.5 2.5 convert_reduce_fusion
  221.1 73.7 %all-gather.2.cloned.1.call-done = bf16[8192,512]{1,0:T(8,128)(2,1)} async-done(((bf16[512,512]{1,0:T(8,128)(2,1)}), bf16[8192,512]{1,0:T(8,128)(2,1)}) %all-gather.2.cloned.1.call-update) | async-done | bytes 8388624 | tf_op jit(solution)/shard_map/all_gather | solution.py:147
  294.8 19.7 %shard_map.111 = bf16[4096,512]{1,0:T(8,128)(2,1)} custom-call(s32[16,6]{1,0:T(8,128)} %bitcast.34, bf16[16,6,256,256]{3,2,1,0:T(8,128)(2,1)} %bitcast.28, bf16[32,256,512]{2,1,0:T(8,128)(2,1)} %bitcast.32), custom_call_target="tpu_custom_call" | custom-call | tf_op jit(solution)/shard_map/pallas_call | solution.py:87
  314.5 4.5 all-to-all-start.2
  319.1 49.2 %all-to-all-done.2 = bf16[8,512,512]{2,1,0:T(8,128)(2,1)} async-done(((bf16[8,512,512]{2,1,0:T(8,128)(2,1)}), bf16[8,512,512]{2,1,0:T(8,128)(2,1)}, u32[]{:S(2)}, u32[]{:S(2)}) %all-to-all-start.2) | async-done | bytes 4194336 | tf_op jit(solution)/shard_map/all_to_all | solution.py:105
  368.4 3.1 reduce_sum.53
  371.4 0.5 fusion.1
  372.1 0.2 copy-done.2
  372.2 1.6 reshape.184
  373.8 35.3 %all_to_all.25 = f32[128,5,512]{2,1,0:T(8,128)S(1)} all-to-all(f32[128,5,512]{2,1,0:T(8,128)} %reshape.184), channel_id=1, replica_groups=mesh['blk'=8,'rep'=16] {'blk','rep'}, dimensions={0} | all-to-all | bytes 2621440 | tf_op jit(solution)/shard_map/all_to_all | solution.py:105
  409.1 0.2 reduce_sum.55
  409.3 1.6 broadcast_in_dim.25
  410.9 4.8 %all-to-all-start.4 = ((f32[128,5,512]{2,1,0:T(8,128)}), f32[128,5,512]{2,1,0:T(8,128)S(1)}, u32[]{:S(2)}, u32[]{:S(2)}) async-start(f32[128,5,512]{2,1,0:T(8,128)} %broadcast_in_dim.25), calls=%async_computation.5 | async-start | bytes 4194304 | tf_op jit(solution)/shard_map/all_to_all | solution.py:100
  415.7 2.5 convolution_convert_fusion
  418.3 27.4 %all-to-all-done.4 = f32[128,5,512]{2,1,0:T(8,128)S(1)} async-done(((f32[128,5,512]{2,1,0:T(8,128)}), f32[128,5,512]{2,1,0:T(8,128)S(1)}, u32[]{:S(2)}, u32[]{:S(2)}) %all-to-all-start.4) | async-done | bytes 1310752 | tf_op jit(solution)/shard_map/all_to_all | solution.py:100
  445.7 1.3 reshape.185
  447.0 2.3 slice_multiply_fusion
  449.3 1.3 slice_multiply_fusion.1
  (38 shorter events, 1.1 us)
Async XLA Ops:
  7.2 1.9 copy-start
  14.1 8.6 %copy-start.6 = (s32[1,16,16]{2,1,0:T(8,128)S(1)}, s32[1,16,16]{2,1,0:T(8,128)}, u32[]{:S(2)}) copy-start(s32[1,16,16]{2,1,0:T(8,128)} %param.8) | copy-start | bytes 3076
  14.1 25.6 %all-to-all-start = ((bf16[16,64,512]{2,1,0:T(8,128)(2,1)}), bf16[16,64,512]{2,1,0:T(8,128)(2,1)S(1)}, u32[]{:S(2)}, u32[]{:S(2)}) async-start(bf16[16,64,512]{2,1,0:T(8,128)(2,1)} %bitcast.2), calls=%async_computation | async-start | bytes 2097152 | tf_op jit(solution)/shard_map/all_to_all | solution.py:125
  39.8 2.0 copy-start.3
  42.2 2.3 copy-start.4
  44.5 5.3 %copy-start.7 = (s32[1,1,16,6]{2,1,3,0:T(1,128)S(1)}, s32[1,1,16,6]{2,1,3,0:T(1,128)}, u32[]{:S(2)}) copy-start(s32[1,1,16,6]{2,1,3,0:T(1,128)} %param.11) | copy-start | bytes 1156
  44.5 53.6 %all-to-all-start.1 = ((bf16[8,512,512]{2,1,0:T(8,128)(2,1)}), bf16[8,512,512]{2,1,0:T(8,128)(2,1)}, u32[]{:S(2)}, u32[]{:S(2)}) async-start(bf16[8,512,512]{2,1,0:T(8,128)(2,1)} %broadcast_in_dim.22), calls=%async_computation.1 | async-start | bytes 8388608 | tf_op jit(solution)/shard_map/all_to_all | solution.py:100
  49.7 168.8 %reduce-scatter.2.cloned.1.call-start = ((), (), s32[]{:S(2)}) async-start(), calls=%async_computation.6 | async-start | bytes 8912896 | tf_op jit(solution)/shard_map/reduce_scatter | solution.py:143
  119.3 99.2 %copy-start.5 = (bf16[512,512]{1,0:T(8,128)(2,1)S(1)}, bf16[512,512]{1,0:T(8,128)(2,1)}, u32[]{:S(2)}) copy-start(bf16[512,512]{1,0:T(8,128)(2,1)} %param.13) | copy-start | bytes 1572868
  119.3 99.2 %copy-start.8 = (f32[512]{0:T(512)S(1)}, f32[512]{0:T(512)}, u32[]{:S(2)}) copy-start(f32[512]{0:T(512)} %param.10) | copy-start | bytes 6148
  119.3 175.5 %all-gather.2.cloned.1.call-start = ((), (), s32[]{:S(2)}) async-start(), calls=%async_computation.7 | async-start | bytes 8912896 | tf_op jit(solution)/shard_map/all_gather | solution.py:147
  314.5 53.8 %all-to-all-start.2 = ((bf16[8,512,512]{2,1,0:T(8,128)(2,1)}), bf16[8,512,512]{2,1,0:T(8,128)(2,1)}, u32[]{:S(2)}, u32[]{:S(2)}) async-start(bf16[8,512,512]{2,1,0:T(8,128)(2,1)} %bitcast.31), calls=%async_computation.3 | async-start | bytes 8388608 | tf_op jit(solution)/shard_map/all_to_all | solution.py:105
  371.4 0.8 copy-start.2
  410.9 34.8 %all-to-all-start.4 = ((f32[128,5,512]{2,1,0:T(8,128)}), f32[128,5,512]{2,1,0:T(8,128)S(1)}, u32[]{:S(2)}, u32[]{:S(2)}) async-start(f32[128,5,512]{2,1,0:T(8,128)} %broadcast_in_dim.25), calls=%async_computation.5 | async-start | bytes 4194304 | tf_op jit(solution)/shard_map/all_to_all | solution.py:100
  415.7 34.9 %copy-start.1 = (bf16[1024,512]{1,0:T(8,128)(2,1)S(1)}, bf16[1024,512]{1,0:T(8,128)(2,1)}, u32[]{:S(2)}) copy-start(bf16[1024,512]{1,0:T(8,128)(2,1)} %param.7) | copy-start | bytes 3145732
Sparse Core Ops, SparseCore 0:
  119.4 99.0 reduce-scatter.1
  221.6 73.2 all-gather.1

commit v3 on v2

--- a/solution.py
+++ b/solution.py
@@ -135,22 +135,39 @@
     ]
     projected = jnp.dot(features, weight, preferred_element_type=jnp.float32).astype(jnp.bfloat16)
     blk_size = lax.axis_size("blk")
-    shard_rows = gather_by_exchange(projected, "blk", blk_size).reshape(-1, feature_width)
-
-    partial_value = forward_spmm(row_lists, tile_stack, shard_rows, row_tiles)
-    partial_value = partial_value.reshape(row_tiles * tile_size, feature_width)
-    preact = (
-        lax.psum_scatter(partial_value, "rep", scatter_dimension=0, tiled=True).astype(jnp.float32)
-        + bias_vector
-    )
-    own_grad = (grad_out.astype(jnp.float32) * silu_slope(preact)).astype(jnp.bfloat16)
-    pre_grad = lax.all_gather(own_grad, "rep", axis=0, tiled=True)
-    activated = jax.nn.silu(preact).astype(jnp.bfloat16)
-    grad_tiles = pre_grad.reshape(row_tiles, tile_size, feature_width)
-    column_contribution = backward_spmm(row_lists, tile_stack, grad_tiles)
-    proj_grad = reduce_by_exchange(column_contribution, "blk", blk_size).astype(jnp.bfloat16)
+    chunks = 2
+    chunk_width = feature_width // chunks
+    activated_parts = []
+    grad_parts = []
+    bias_parts = []
+    for chunk in range(chunks):
+        columns = slice(chunk * chunk_width, (chunk + 1) * chunk_width)
+        shard_rows = gather_by_exchange(projected[:, columns], "blk", blk_size).reshape(
+            -1, chunk_width
+        )
+        partial_value = forward_spmm(row_lists, tile_stack, shard_rows, row_tiles)
+        partial_value = partial_value.reshape(row_tiles * tile_size, chunk_width)
+        preact = (
+            lax.psum_scatter(partial_value, "rep", scatter_dimension=0, tiled=True).astype(
+                jnp.float32
+            )
+            + bias_vector[columns]
+        )
+        own_grad = (grad_out[:, columns].astype(jnp.float32) * silu_slope(preact)).astype(
+            jnp.bfloat16
+        )
+        pre_grad = lax.all_gather(own_grad, "rep", axis=0, tiled=True)
+        activated_parts.append(jax.nn.silu(preact).astype(jnp.bfloat16))
+        bias_parts.append(jnp.sum(own_grad.astype(jnp.float32), axis=0))
+        grad_tiles = pre_grad.reshape(row_tiles, tile_size, chunk_width)
+        column_contribution = backward_spmm(row_lists, tile_stack, grad_tiles)
+        grad_parts.append(
+            reduce_by_exchange(column_contribution, "blk", blk_size).astype(jnp.bfloat16)
+        )
+    activated = jnp.concatenate(activated_parts, axis=1)
+    proj_grad = jnp.concatenate(grad_parts, axis=1)
+    local_bias = jnp.concatenate(bias_parts, axis=0)
     local_weight = jnp.einsum("nf,ng->fg", features, proj_grad, preferred_element_type=jnp.float32)
-    local_bias = jnp.sum(own_grad.astype(jnp.float32), axis=0)
     device_count = blk_size * rep_size
     chunk_rows = feature_width // device_count + 1
     pad_rows = jnp.zeros((device_count * chunk_rows - feature_width - 1, feature_width), jnp.float32)

time: 459 us -> 517 us (1.13)
  blocking collectives: 35.3 us -> 66.1 us
  Pallas kernels: 40.9 us -> 67.2 us
  waiting for transfers between devices: 314 us -> 308 us
    all_to_all x0 -> x1, blocking collectives: none -> 29.7 us  [gather_by_exchange(): return lax.all_to_all(stacked, axis, 0, 0, tiled=True)]
    all_gather x1 -> x2, waiting for transfers between devices: 73.7 us -> 99.8 us  [per_device(): pre_grad = lax.all_gather(own_grad, 'rep', axis=0, tiled=True)]
    all_to_all x2, waiting for transfers between devices: 75 us -> 51.7 us  [gather_by_exchange(): return lax.all_to_all(stacked, axis, 0, 0, tiled=True)]
    all_to_all x1 -> x2, waiting for transfers between devices: 49.2 us -> 26.2 us  [reduce_by_exchange(): received = lax.all_to_all(chunks, axis, 0, 0, tiled=True)]
    reduce_scatter x1 -> x2, waiting for transfers between devices: 99.1 us -> 114 us  [per_device(): lax.psum_scatter(partial_value, 'rep', scatter_dimension=0, tiled=True)]
    pallas_call x1 -> x2, Pallas kernels: 19.7 us -> 33.2 us  [backward_spmm(): pl.pallas_call(_backward_kernel, grid_spec=grid_spec, out_shape=jax.Shape...]
    pallas_call x1 -> x2, Pallas kernels: 21.2 us -> 34.1 us  [forward_spmm(): pl.pallas_call(_forward_kernel, grid_spec=grid_spec, out_shape=jax.ShapeD...]
  transfers between devices with their start and end apart: 6 -> 9, of which waited for: 6 -> 8; matrix products, arithmetic and copies ran while one was open for 1% -> 1% of each run, Pallas kernels for 0% -> 10%
where the time goes in v3:
time: 517 us; the launch traced here: 515 us
  waiting for transfers between devices  308 us (60%)
  Pallas kernels  67.2 us (13%)
  blocking collectives  66.1 us (13%)
  starting transfers between devices  27.5 us (5%)
  local copies, waits for them, and re-layouts  17.3 us (3%)
  between operations  13.9 us (3%)
  other arithmetic  10.8 us (2%)
    reduce_scatter x2, waiting for transfers between devices, per_device(): lax.psum_scatter(partial_value, 'rep', scatter_dimension=0, tiled=True)  114 us
    all_gather x2, waiting for transfers between devices, per_device(): pre_grad = lax.all_gather(own_grad, 'rep', axis=0, tiled=True)  99.8 us
    all_to_all x2, waiting for transfers between devices, gather_by_exchange(): return lax.all_to_all(stacked, axis, 0, 0, tiled=True)  51.7 us
    all_to_all x1, blocking collectives, reduce_by_exchange(): received = lax.all_to_all(chunks, axis, 0, 0, tiled=True)  36.5 us
    pallas_call x2, Pallas kernels, forward_spmm(): pl.pallas_call(_forward_kernel, grid_spec=grid_spec, out_shape=jax.ShapeD...  34.1 us
    pallas_call x2, Pallas kernels, backward_spmm(): pl.pallas_call(_backward_kernel, grid_spec=grid_spec, out_shape=jax.Shape...  33.2 us
    all_to_all x1, blocking collectives, gather_by_exchange(): return lax.all_to_all(stacked, axis, 0, 0, tiled=True)  29.7 us
    all_to_all x2, waiting for transfers between devices, reduce_by_exchange(): received = lax.all_to_all(chunks, axis, 0, 0, tiled=True)  26.2 us
  transfers between devices with their start and end apart: 9, of which 8 were waited for; matrix products, arithmetic and copies ran while one was open for 1% of the time, Pallas kernels for 10%

profile of v3, /device:TPU:1, one launch (start us, length us, event | category | flops | bytes accessed | tf_op | source)
XLA Modules:
  0.0 514.5 jit_solution(4092229630071286645)
XLA Ops:
  9.1 5.1 gather_fusion
  14.1 8.6 %all-to-all-start = ((bf16[16,64,512]{2,1,0:T(8,128)(2,1)}), bf16[16,64,512]{2,1,0:T(8,128)(2,1)S(1)}, u32[]{:S(2)}, u32[]{:S(2)}) async-start(bf16[16,64,512]{2,1,0:T(8,128)(2,1)} %bitcast.2), calls=%async_computation | async-start | bytes 2097152 | tf_op jit(solution)/shard_map/all_to_all | solution.py:125
  23.3 16.5 %all-to-all-done = bf16[16,64,512]{2,1,0:T(8,128)(2,1)S(1)} async-done(((bf16[16,64,512]{2,1,0:T(8,128)(2,1)}), bf16[16,64,512]{2,1,0:T(8,128)(2,1)S(1)}, u32[]{:S(2)}, u32[]{:S(2)}) %all-to-all-start) | async-done | bytes 1048608 | tf_op jit(solution)/shard_map/all_to_all | solution.py:125
  39.8 2.0 gather_fusion.1
  42.3 1.5 broadcast_in_dim.24
  43.8 5.2 %all-to-all-start.1 = ((bf16[8,512,256]{2,1,0:T(8,128)(2,1)}), bf16[8,512,256]{2,1,0:T(8,128)(2,1)S(1)}, u32[]{:S(2)}, u32[]{:S(2)}) async-start(bf16[8,512,256]{2,1,0:T(8,128)(2,1)} %broadcast_in_dim.24), calls=%async_computation.1 | async-start | bytes 4194304 | tf_op jit(solution)/shard_map/all_to_all | solution.py:100
  49.7 25.0 %all-to-all-done.1 = bf16[8,512,256]{2,1,0:T(8,128)(2,1)S(1)} async-done(((bf16[8,512,256]{2,1,0:T(8,128)(2,1)}), bf16[8,512,256]{2,1,0:T(8,128)(2,1)S(1)}, u32[]{:S(2)}, u32[]{:S(2)}) %all-to-all-start.1) | async-done | bytes 2097184 | tf_op jit(solution)/shard_map/all_to_all | solution.py:100
  74.8 1.3 copy-done.2
  76.1 16.9 %shard_map.110 = bf16[32,256,256]{2,1,0:T(8,128)(2,1)} custom-call(s32[16,6]{1,0:T(8,128)} %bitcast.42, bf16[16,6,256,256]{3,2,1,0:T(8,128)(2,1)} %bitcast.29, bf16[4096,256]{1,0:T(8,128)(2,1)} %bitcast.37), custom_call_target="tpu_custom_call" | custom-call | tf_op jit(solution)/shard_map/pallas_call | solution.py:48
  93.3 29.7 %all_to_all.35 = bf16[8,512,256]{2,1,0:T(8,128)(2,1)} all-to-all(bf16[8,512,256]{2,1,0:T(8,128)(2,1)S(1)} %broadcast_in_dim.25), channel_id=1, replica_groups=mesh['blk'=8,'rep'=16] {'blk'}, dimensions={0} | all-to-all | bytes 4194304 | tf_op jit(solution)/shard_map/all_to_all | solution.py:100
  122.9 17.1 %shard_map.111 = bf16[32,256,256]{2,1,0:T(8,128)(2,1)} custom-call(s32[16,6]{1,0:T(8,128)} %bitcast.43, bf16[16,6,256,256]{3,2,1,0:T(8,128)(2,1)} %bitcast.30, bf16[4096,256]{1,0:T(8,128)(2,1)} %bitcast.39), custom_call_target="tpu_custom_call" | custom-call | tf_op jit(solution)/shard_map/pallas_call | solution.py:48
  140.7 30.0 %reduce-scatter.3.cloned.1.call-done = bf16[512,256]{1,0:T(8,128)(2,1)} async-done(((bf16[8192,256]{1,0:T(8,128)(2,1)}), bf16[512,256]{1,0:T(8,128)(2,1)}) %reduce-scatter.3.cloned.1.call-update) | async-done | bytes 262160 | tf_op jit(solution)/shard_map/reduce_scatter | solution.py:151
  170.8 83.5 %reduce-scatter.5.cloned.1.call-done = bf16[512,256]{1,0:T(8,128)(2,1)} async-done(((bf16[8192,256]{1,0:T(8,128)(2,1)}), bf16[512,256]{1,0:T(8,128)(2,1)}) %reduce-scatter.5.cloned.1.call-update) | async-done | bytes 262160 | tf_op jit(solution)/shard_map/reduce_scatter | solution.py:151
  254.3 2.3 convert_reduce_fusion.1
  257.3 55.5 %all-gather.3.cloned.1.call-done = bf16[8192,256]{1,0:T(8,128)(2,1)} async-done(((bf16[512,256]{1,0:T(8,128)(2,1)}), bf16[8192,256]{1,0:T(8,128)(2,1)}) %all-gather.3.cloned.1.call-update) | async-done | bytes 4194320 | tf_op jit(solution)/shard_map/all_gather | solution.py:159
  312.8 16.6 %shard_map.112 = bf16[4096,256]{1,0:T(8,128)(2,1)} custom-call(s32[16,6]{1,0:T(8,128)} %bitcast.44, bf16[16,6,256,256]{3,2,1,0:T(8,128)(2,1)} %bitcast.31, bf16[32,256,256]{2,1,0:T(8,128)(2,1)} %bitcast.41), custom_call_target="tpu_custom_call" | custom-call | tf_op jit(solution)/shard_map/pallas_call | solution.py:87
  329.4 4.1 all-to-all-start.3
  333.6 44.3 %all-gather.5.cloned.1.call-done = bf16[8192,256]{1,0:T(8,128)(2,1)} async-done(((bf16[512,256]{1,0:T(8,128)(2,1)}), bf16[8192,256]{1,0:T(8,128)(2,1)}) %all-gather.5.cloned.1.call-update) | async-done | bytes 4194320 | tf_op jit(solution)/shard_map/all_gather | solution.py:159
  377.9 16.5 %shard_map.113 = bf16[4096,256]{1,0:T(8,128)(2,1)} custom-call(s32[16,6]{1,0:T(8,128)} %bitcast.45, bf16[16,6,256,256]{3,2,1,0:T(8,128)(2,1)} %bitcast.32, bf16[32,256,256]{2,1,0:T(8,128)(2,1)} %bitcast.40), custom_call_target="tpu_custom_call" | custom-call | tf_op jit(solution)/shard_map/pallas_call | solution.py:87
  394.4 4.6 all-to-all-start.4
  399.5 26.2 %all-to-all-done.4 = bf16[8,512,256]{2,1,0:T(8,128)(2,1)} async-done(((bf16[8,512,256]{2,1,0:T(8,128)(2,1)}), bf16[8,512,256]{2,1,0:T(8,128)(2,1)}, u32[]{:S(2)}, u32[]{:S(2)}) %all-to-all-start.4) | async-done | bytes 2097184 | tf_op jit(solution)/shard_map/all_to_all | solution.py:105
  425.6 2.0 reduce_sum.75
  428.5 1.6 reshape.202
  430.0 36.5 %all_to_all.36 = f32[128,5,512]{2,1,0:T(8,128)S(1)} all-to-all(f32[128,5,512]{2,1,0:T(8,128)} %reshape.202), channel_id=1, replica_groups=mesh['blk'=8,'rep'=16] {'blk','rep'}, dimensions={0} | all-to-all | bytes 2621440 | tf_op jit(solution)/shard_map/all_to_all | solution.py:105
  466.7 1.6 broadcast_in_dim.28
  468.3 4.8 all-to-all-start.6
  473.1 0.8 pad_maximum_fusion
  474.0 2.5 convolution_convert_fusion
  476.4 26.7 %all-to-all-done.6 = f32[128,5,512]{2,1,0:T(8,128)S(1)} async-done(((f32[128,5,512]{2,1,0:T(8,128)}), f32[128,5,512]{2,1,0:T(8,128)S(1)}, u32[]{:S(2)}, u32[]{:S(2)}) %all-to-all-start.6) | async-done | bytes 1310752 | tf_op jit(solution)/shard_map/all_to_all | solution.py:100
  503.1 1.3 reshape.203
  504.4 2.3 slice_multiply_fusion
  506.7 1.3 slice_multiply_fusion.1
  (61 shorter events, 6.6 us)
Async XLA Ops:
  7.2 1.9 copy-start
  14.1 8.6 %copy-start.9 = (s32[1,16,16]{2,1,0:T(8,128)S(1)}, s32[1,16,16]{2,1,0:T(8,128)}, u32[]{:S(2)}) copy-start(s32[1,16,16]{2,1,0:T(8,128)} %param.8) | copy-start | bytes 3076
  14.1 25.6 %all-to-all-start = ((bf16[16,64,512]{2,1,0:T(8,128)(2,1)}), bf16[16,64,512]{2,1,0:T(8,128)(2,1)S(1)}, u32[]{:S(2)}, u32[]{:S(2)}) async-start(bf16[16,64,512]{2,1,0:T(8,128)(2,1)} %bitcast.2), calls=%async_computation | async-start | bytes 2097152 | tf_op jit(solution)/shard_map/all_to_all | solution.py:125
  39.8 2.0 copy-start.6
  41.8 2.0 copy-start.3
  42.2 1.6 copy-start.5
  43.8 5.3 %copy-start.10 = (s32[1,1,16,6]{2,1,3,0:T(1,128)S(1)}, s32[1,1,16,6]{2,1,3,0:T(1,128)}, u32[]{:S(2)}) copy-start(s32[1,1,16,6]{2,1,3,0:T(1,128)} %param.11) | copy-start | bytes 1156
  43.8 31.0 %all-to-all-start.1 = ((bf16[8,512,256]{2,1,0:T(8,128)(2,1)}), bf16[8,512,256]{2,1,0:T(8,128)(2,1)S(1)}, u32[]{:S(2)}, u32[]{:S(2)}) async-start(bf16[8,512,256]{2,1,0:T(8,128)(2,1)} %broadcast_in_dim.24), calls=%async_computation.1 | async-start | bytes 4194304 | tf_op jit(solution)/shard_map/all_to_all | solution.py:100
  49.0 121.8 %reduce-scatter.3.cloned.1.call-start = ((), (), s32[]{:S(2)}) async-start(), calls=%async_computation.9 | async-start | bytes 4456448 | tf_op jit(solution)/shard_map/reduce_scatter | solution.py:151
  74.8 1.3 copy-start.2
  93.1 161.2 %reduce-scatter.5.cloned.1.call-start = ((), (), s32[]{:S(2)}) async-start(), calls=%async_computation.10 | async-start | bytes 4456448 | tf_op jit(solution)/shard_map/reduce_scatter | solution.py:151
  140.1 0.7 copy-start.11
  140.1 114.3 %copy-start.7 = (bf16[512,512]{1,0:T(8,128)(2,1)S(1)}, bf16[512,512]{1,0:T(8,128)(2,1)}, u32[]{:S(2)}) copy-start(bf16[512,512]{1,0:T(8,128)(2,1)} %param.13) | copy-start | bytes 1572868
  140.1 172.7 %all-gather.3.cloned.1.call-start = ((), (), s32[]{:S(2)}) async-start(), calls=%async_computation.11 | async-start | bytes 4456448 | tf_op jit(solution)/shard_map/all_gather | solution.py:159
  256.7 121.2 %all-gather.5.cloned.1.call-start = ((), (), s32[]{:S(2)}) async-start(), calls=%async_computation.12 | async-start | bytes 4456448 | tf_op jit(solution)/shard_map/all_gather | solution.py:159
  329.4 65.0 %all-to-all-start.3 = ((bf16[8,512,256]{2,1,0:T(8,128)(2,1)}), bf16[8,512,256]{2,1,0:T(8,128)(2,1)S(1)}, u32[]{:S(2)}, u32[]{:S(2)}) async-start(bf16[8,512,256]{2,1,0:T(8,128)(2,1)} %bitcast.38), calls=%async_computation.5 | async-start | bytes 4194304 | tf_op jit(solution)/shard_map/all_to_all | solution.py:105
  394.4 31.2 %all-to-all-start.4 = ((bf16[8,512,256]{2,1,0:T(8,128)(2,1)}), bf16[8,512,256]{2,1,0:T(8,128)(2,1)}, u32[]{:S(2)}, u32[]{:S(2)}) async-start(bf16[8,512,256]{2,1,0:T(8,128)(2,1)} %bitcast.36), calls=%async_computation.6 | async-start | bytes 4194304 | tf_op jit(solution)/shard_map/all_to_all | solution.py:105
  399.1 28.5 %copy-start.4 = (bf16[512,512]{1,0:T(8,128)(2,1)S(1)}, bf16[512,512]{1,0:T(8,128)(2,1)}, u32[]{:S(2)}) copy-start(bf16[512,512]{1,0:T(8,128)(2,1)} %copy-done.3) | copy-start | bytes 1572868
  427.6 0.7 copy-start.8
  468.3 34.8 %all-to-all-start.6 = ((f32[128,5,512]{2,1,0:T(8,128)}), f32[128,5,512]{2,1,0:T(8,128)S(1)}, u32[]{:S(2)}, u32[]{:S(2)}) async-start(f32[128,5,512]{2,1,0:T(8,128)} %broadcast_in_dim.28), calls=%async_computation.8 | async-start | bytes 4194304 | tf_op jit(solution)/shard_map/all_to_all | solution.py:100
  474.0 34.0 %copy-start.1 = (bf16[1024,512]{1,0:T(8,128)(2,1)S(1)}, bf16[1024,512]{1,0:T(8,128)(2,1)}, u32[]{:S(2)}) copy-start(bf16[1024,512]{1,0:T(8,128)(2,1)} %param.7) | copy-start | bytes 3145732
Sparse Core Ops, SparseCore 0:
  93.2 77.5 reduce-scatter.2
  174.8 79.4 reduce-scatter.4
  257.4 55.3 all-gather.2
  315.7 62.1 all-gather.4

commit v4 on v2

--- a/solution.py
+++ b/solution.py
@@ -6,6 +6,7 @@
 from jax import lax
 from jax.experimental import pallas as pl
 from jax.experimental.pallas import tpu as pltpu
+from jax.sharding import Mesh
 from jax.sharding import PartitionSpec as P
 
 
@@ -107,14 +108,16 @@
 
 
 def per_device(raw_features, move_plan, weight, bias_vector, tile_rows, tile_values, grad_out):
-    rep_size = lax.axis_size("rep")
-    own_index = lax.axis_index("rep")
+    core_size = lax.axis_size("core")
+    chip_size = lax.axis_size("rh")
+    rep_size = chip_size * core_size
+    own_index = lax.axis_index("rh") * core_size + lax.axis_index("core")
     dev_rows, feature_width = grad_out.shape
     raw_rows = raw_features.shape[0]
     capacity = 4 * (dev_rows // (2 * rep_size))
     counts = move_plan[0]
     tile_stack = tile_values[0, 0]
-    row_lists = tile_rows[0, 0]
+    tile_lists = tile_rows[0, 0]
     tile_size = tile_stack.shape[2]
     row_tiles = rep_size * dev_rows // tile_size
     root_count = math.sqrt(dev_rows * lax.axis_size("blk") * rep_size)
@@ -122,7 +125,14 @@
     first_rows = jnp.cumsum(sent_counts) - sent_counts
     slot_rows = first_rows[:, None] + jnp.arange(capacity, dtype=jnp.int32)[None, :]
     outgoing = raw_features[jnp.minimum(slot_rows, raw_rows - 1)]
-    incoming = lax.all_to_all(outgoing, "rep", split_axis=0, concat_axis=0, tiled=True)
+    incoming = lax.all_to_all(outgoing, ("rh", "core"), split_axis=0, concat_axis=0, tiled=True)
+    block_tiles = dev_rows // tile_size
+    block_of = tile_lists // block_tiles
+    row_lists = (
+        (block_of % core_size) * (chip_size * block_tiles)
+        + (block_of // core_size) * block_tiles
+        + tile_lists % block_tiles
+    )
     recv_counts = lax.dynamic_index_in_dim(counts, own_index, 1, keepdims=False)
     inclusive = jnp.cumsum(recv_counts)
     exclusive = inclusive - recv_counts
@@ -138,13 +148,12 @@
     shard_rows = gather_by_exchange(projected, "blk", blk_size).reshape(-1, feature_width)
 
     partial_value = forward_spmm(row_lists, tile_stack, shard_rows, row_tiles)
-    partial_value = partial_value.reshape(row_tiles * tile_size, feature_width)
-    preact = (
-        lax.psum_scatter(partial_value, "rep", scatter_dimension=0, tiled=True).astype(jnp.float32)
-        + bias_vector
-    )
+    by_core = partial_value.reshape(row_tiles * tile_size, feature_width)
+    core_sum = reduce_by_exchange(by_core, "core", core_size).astype(jnp.bfloat16)
+    preact = reduce_by_exchange(core_sum, "rh", chip_size) + bias_vector
     own_grad = (grad_out.astype(jnp.float32) * silu_slope(preact)).astype(jnp.bfloat16)
-    pre_grad = lax.all_gather(own_grad, "rep", axis=0, tiled=True)
+    chip_grad = gather_by_exchange(own_grad, "rh", chip_size).reshape(-1, feature_width)
+    pre_grad = gather_by_exchange(chip_grad, "core", core_size)
     activated = jax.nn.silu(preact).astype(jnp.bfloat16)
     grad_tiles = pre_grad.reshape(row_tiles, tile_size, feature_width)
     column_contribution = backward_spmm(row_lists, tile_stack, grad_tiles)
@@ -155,8 +164,9 @@
     chunk_rows = feature_width // device_count + 1
     pad_rows = jnp.zeros((device_count * chunk_rows - feature_width - 1, feature_width), jnp.float32)
     stacked = jnp.concatenate([local_weight, local_bias[None, :], pad_rows], axis=0)
-    reduced = reduce_by_exchange(stacked, ("blk", "rep"), device_count)
-    stacked_sum = gather_by_exchange(reduced, ("blk", "rep"), device_count).reshape(
+    every = ("blk", "rh", "core")
+    reduced = reduce_by_exchange(stacked, every, device_count)
+    stacked_sum = gather_by_exchange(reduced, every, device_count).reshape(
         -1, feature_width
     )
     weight_sum = stacked_sum[:feature_width]
@@ -168,22 +178,24 @@
 
 
 def solution(mesh):
+    blk_count, rep_count = mesh.devices.shape
+    chip_mesh = Mesh(mesh.devices.reshape(blk_count, rep_count // 2, 2), ("blk", "rh", "core"))
     return jax.shard_map(
         per_device,
-        mesh=mesh,
+        mesh=chip_mesh,
         in_specs=(
-            P(("blk", "rep"), None),
+            P(("blk", "rh", "core"), None),
             P("blk", None, None),
             P(),
             P(),
-            P("blk", "rep", None, None),
-            P("blk", "rep", None, None, None, None),
-            P(("blk", "rep"), None),
+            P("blk", ("rh", "core"), None, None),
+            P("blk", ("rh", "core"), None, None, None, None),
+            P(("blk", "rh", "core"), None),
         ),
         out_specs=(
-            P(("blk", "rep"), None),
-            P(("blk", "rep"), None),
-            P(("blk", "rep"), None),
+            P(("blk", "rh", "core"), None),
+            P(("blk", "rh", "core"), None),
+            P(("blk", "rh", "core"), None),
             P(),
             P(),
         ),

time: 459 us -> 432 us (0.941)
  waiting for transfers between devices: 314 us -> 141 us
  blocking collectives: 35.3 us -> 182 us
  between operations: 14.2 us -> 0.79 us
  other arithmetic: 10.8 us -> 18.9 us
    reduce_scatter x1 -> x0, waiting for transfers between devices: 99.1 us -> none  [per_device(): lax.psum_scatter(partial_value, 'rep', scatter_dimension=0, tiled=True)]
    all_gather x1 -> x0, waiting for transfers between devices: 73.7 us -> none  [per_device(): pre_grad = lax.all_gather(own_grad, 'rep', axis=0, tiled=True)]
    all_to_all x0 -> x2, blocking collectives: none -> 73.6 us  [gather_by_exchange(): return lax.all_to_all(stacked, axis, 0, 0, tiled=True)]
    all_to_all x1 -> x3, blocking collectives: 35.3 us -> 108 us  [reduce_by_exchange(): received = lax.all_to_all(chunks, axis, 0, 0, tiled=True)]
    reduce_sum x2 -> x4, other arithmetic: 3.26 us -> 11.9 us  [reduce_by_exchange(): return jnp.sum(received.astype(jnp.float32), axis=0)]
  transfers between devices with their start and end apart: 6 -> 4, of which waited for: 6 -> 4; matrix products, arithmetic and copies ran while one was open for 1% -> 1% of each run, Pallas kernels for 0% -> 0%
where the time goes in v4:
time: 432 us; the launch traced here: 430 us
  blocking collectives  182 us (42%)
  waiting for transfers between devices  141 us (33%)
  Pallas kernels  40.9 us (9%)
  starting transfers between devices  23.3 us (5%)
  local copies, waits for them, and re-layouts  20 us (5%)
  other arithmetic  18.9 us (4%)
    all_to_all x3, blocking collectives, reduce_by_exchange(): received = lax.all_to_all(chunks, axis, 0, 0, tiled=True)  108 us
    all_to_all x2, waiting for transfers between devices, gather_by_exchange(): return lax.all_to_all(stacked, axis, 0, 0, tiled=True)  75 us
    all_to_all x2, blocking collectives, gather_by_exchange(): return lax.all_to_all(stacked, axis, 0, 0, tiled=True)  73.6 us
    all_to_all x1, waiting for transfers between devices, reduce_by_exchange(): received = lax.all_to_all(chunks, axis, 0, 0, tiled=True)  48.9 us
    pallas_call x1, Pallas kernels, forward_spmm(): pl.pallas_call(_forward_kernel, grid_spec=grid_spec, out_shape=jax.ShapeD...  21.2 us
    pallas_call x1, Pallas kernels, backward_spmm(): pl.pallas_call(_backward_kernel, grid_spec=grid_spec, out_shape=jax.Shape...  19.7 us
    all_to_all x1, waiting for transfers between devices, per_device(): lax.all_to_all(outgoing, ('rh', 'core'), split_axis=0, concat_axis=0, til...  16.5 us
    reduce_sum x4, other arithmetic, reduce_by_exchange(): return jnp.sum(received.astype(jnp.float32), axis=0)  11.9 us
  transfers between devices with their start and end apart: 4, of which 4 were waited for; matrix products, arithmetic and copies ran while one was open for 1% of the time, Pallas kernels for 0%

profile of v4, /device:TPU:1, one launch (start us, length us, event | category | flops | bytes accessed | tf_op | source)
XLA Modules:
  0.0 429.6 jit_solution(16612482417546382356)
XLA Ops:
  0.7 0.8 fusion.11
  1.7 0.7 bitcast_subtract_fusion
  2.5 5.1 %gather_fusion = bf16[1024,512]{1,0:T(8,128)(2,1)} fusion(bf16[1024,512]{1,0:T(8,128)(2,1)S(1)} %copy-done, s32[1024]{0:T(1024)S(1)} %broadcast_clamp_fusion), kind=kCustom, calls=%fused_computation | custom fusion | bytes 2101248 | tf_op jit(solution)/shard_map/gather | solution.py:127
  7.6 8.6 %all-to-all-start = ((bf16[16,64,512]{2,1,0:T(8,128)(2,1)}), bf16[16,64,512]{2,1,0:T(8,128)(2,1)S(1)}, u32[]{:S(2)}, u32[]{:S(2)}) async-start(bf16[16,64,512]{2,1,0:T(8,128)(2,1)} %bitcast.2), calls=%async_computation | async-start | bytes 2097152 | tf_op jit(solution)/shard_map/all_to_all | solution.py:128
  16.8 16.5 %all-to-all-done = bf16[16,64,512]{2,1,0:T(8,128)(2,1)S(1)} async-done(((bf16[16,64,512]{2,1,0:T(8,128)(2,1)}), bf16[16,64,512]{2,1,0:T(8,128)(2,1)S(1)}, u32[]{:S(2)}, u32[]{:S(2)}) %all-to-all-start) | async-done | bytes 1048608 | tf_op jit(solution)/shard_map/all_to_all | solution.py:128
  33.3 2.0 gather_fusion.1
  35.7 2.3 broadcast_in_dim.28
  38.0 5.2 %all-to-all-start.1 = ((bf16[8,512,512]{2,1,0:T(8,128)(2,1)}), bf16[8,512,512]{2,1,0:T(8,128)(2,1)}, u32[]{:S(2)}, u32[]{:S(2)}) async-start(bf16[8,512,512]{2,1,0:T(8,128)(2,1)} %broadcast_in_dim.28), calls=%async_computation.1 | async-start | bytes 8388608 | tf_op jit(solution)/shard_map/all_to_all | solution.py:101
  43.3 0.6 fusion.2.rows_ref
  43.9 47.6 %all-to-all-done.1 = bf16[8,512,512]{2,1,0:T(8,128)(2,1)} async-done(((bf16[8,512,512]{2,1,0:T(8,128)(2,1)}), bf16[8,512,512]{2,1,0:T(8,128)(2,1)}, u32[]{:S(2)}, u32[]{:S(2)}) %all-to-all-start.1) | async-done | bytes 4194336 | tf_op jit(solution)/shard_map/all_to_all | solution.py:101
  91.6 21.2 %shard_map.110 = bf16[32,256,512]{2,1,0:T(8,128)(2,1)} custom-call(s32[16,6]{1,0:T(8,128)} %fusion.2.rows_ref, bf16[16,6,256,256]{3,2,1,0:T(8,128)(2,1)} %bitcast.44, bf16[4096,512]{1,0:T(8,128)(2,1)} %bitcast.9.cols_ref), custom_call_target="tpu_custom_call" | custom-call | tf_op jit(solution)/shard_map/pallas_call | solution.py:49
  112.8 20.3 %all_to_all.45 = bf16[2,4096,512]{2,1,0:T(8,128)(2,1)} all-to-all(bf16[2,4096,512]{2,1,0:T(8,128)(2,1)} %bitcast.47), channel_id=1, replica_groups=mesh['blk'=8,'rh'=8,'core'=2] {'core'}, dimensions={0} | all-to-all | bytes 16777216 | tf_op jit(solution)/shard_map/all_to_all | solution.py:106
  133.1 8.1 %reduce_sum.74 = bf16[4096,512]{1,0:T(8,128)(2,1)} reduce(bf16[2,4096,512]{2,1,0:T(8,128)(2,1)} %all_to_all.45, bf16[]{:T(256)} %constant.84.clone.1), dimensions={0}, to_apply=%region_4.5 | reduce | flops 2097152 | bytes 12582914 | tf_op jit(solution)/shard_map/reduce_sum | solution.py:107
  141.2 53.1 %all_to_all.46 = bf16[8,512,512]{2,1,0:T(8,128)(2,1)S(1)} all-to-all(bf16[8,512,512]{2,1,0:T(8,128)(2,1)} %bitcast.50), channel_id=1, replica_groups=mesh['blk'=8,'rh'=8,'core'=2] {'rh'}, dimensions={0} | all-to-all | bytes 8388608 | tf_op jit(solution)/shard_map/all_to_all | solution.py:106
  194.2 0.6 convert_reduce_fusion
  195.3 1.3 convert_reduce_fusion.1
  196.9 52.6 %all_to_all.47 = bf16[8,512,512]{2,1,0:T(8,128)(2,1)S(1)} all-to-all(bf16[8,512,512]{2,1,0:T(8,128)(2,1)S(1)} %broadcast_in_dim.29), channel_id=1, replica_groups=mesh['blk'=8,'rh'=8,'core'=2] {'rh'}, dimensions={0} | all-to-all | bytes 8388608 | tf_op jit(solution)/shard_map/all_to_all | solution.py:101
  249.5 3.8 broadcast_in_dim.31
  253.3 21.0 %all_to_all.48 = bf16[2,4096,512]{2,1,0:T(8,128)(2,1)} all-to-all(bf16[2,4096,512]{2,1,0:T(8,128)(2,1)} %broadcast_in_dim.31), channel_id=1, replica_groups=mesh['blk'=8,'rh'=8,'core'=2] {'core'}, dimensions={0} | all-to-all | bytes 16777216 | tf_op jit(solution)/shard_map/all_to_all | solution.py:101
  274.3 19.7 %shard_map.111 = bf16[4096,512]{1,0:T(8,128)(2,1)} custom-call(s32[16,6]{1,0:T(8,128)} %fusion.2.rows_ref, bf16[16,6,256,256]{3,2,1,0:T(8,128)(2,1)} %bitcast.45, bf16[32,256,512]{2,1,0:T(8,128)(2,1)} %bitcast.46), custom_call_target="tpu_custom_call" | custom-call | tf_op jit(solution)/shard_map/pallas_call | solution.py:88
  294.0 4.7 %all-to-all-start.6 = ((bf16[8,512,512]{2,1,0:T(8,128)(2,1)}), bf16[8,512,512]{2,1,0:T(8,128)(2,1)}, u32[]{:S(2)}, u32[]{:S(2)}) async-start(bf16[8,512,512]{2,1,0:T(8,128)(2,1)} %bitcast.51), calls=%async_computation.6 | async-start | bytes 8388608 | tf_op jit(solution)/shard_map/all_to_all | solution.py:106
  298.8 48.9 %all-to-all-done.6 = bf16[8,512,512]{2,1,0:T(8,128)(2,1)} async-done(((bf16[8,512,512]{2,1,0:T(8,128)(2,1)}), bf16[8,512,512]{2,1,0:T(8,128)(2,1)}, u32[]{:S(2)}, u32[]{:S(2)}) %all-to-all-start.6) | async-done | bytes 4194336 | tf_op jit(solution)/shard_map/all_to_all | solution.py:106
  347.7 3.1 reduce_sum.76
  351.7 1.6 reshape.186
  353.3 34.9 %all_to_all.49 = f32[128,5,512]{2,1,0:T(8,128)S(1)} all-to-all(f32[128,5,512]{2,1,0:T(8,128)} %reshape.186), channel_id=1, replica_groups=mesh['blk'=8,'rh'=8,'core'=2] {'blk','rh','core'}, dimensions={0} | all-to-all | bytes 2621440 | tf_op jit(solution)/shard_map/all_to_all | solution.py:106
  388.4 1.6 broadcast_in_dim.34
  390.0 4.8 %all-to-all-start.8 = ((f32[128,5,512]{2,1,0:T(8,128)}), f32[128,5,512]{2,1,0:T(8,128)S(1)}, u32[]{:S(2)}, u32[]{:S(2)}) async-start(f32[128,5,512]{2,1,0:T(8,128)} %broadcast_in_dim.34), calls=%async_computation.8 | async-start | bytes 4194304 | tf_op jit(solution)/shard_map/all_to_all | solution.py:101
  394.8 2.5 convolution_convert_fusion
  397.4 27.4 %all-to-all-done.8 = f32[128,5,512]{2,1,0:T(8,128)S(1)} async-done(((f32[128,5,512]{2,1,0:T(8,128)}), f32[128,5,512]{2,1,0:T(8,128)S(1)}, u32[]{:S(2)}, u32[]{:S(2)}) %all-to-all-start.8) | async-done | bytes 1310752 | tf_op jit(solution)/shard_map/all_to_all | solution.py:101
  424.8 1.3 reshape.187
  426.1 2.3 slice_multiply_fusion
  428.3 1.3 slice_multiply_fusion.1
  (41 shorter events, 3.5 us)
Async XLA Ops:
  0.6 1.9 copy-start
  2.5 13.7 %copy-start.6 = (s32[1,16,16]{2,1,0:T(8,128)S(1)}, s32[1,16,16]{2,1,0:T(8,128)}, u32[]{:S(2)}) copy-start(s32[1,16,16]{2,1,0:T(8,128)} %param.8) | copy-start | bytes 3076
  7.6 27.6 %copy-start.3 = (bf16[512,512]{1,0:T(8,128)(2,1)S(1)}, bf16[512,512]{1,0:T(8,128)(2,1)}, u32[]{:S(2)}) copy-start(bf16[512,512]{1,0:T(8,128)(2,1)} %param.9) | copy-start | bytes 1572868
  7.6 25.6 %all-to-all-start = ((bf16[16,64,512]{2,1,0:T(8,128)(2,1)}), bf16[16,64,512]{2,1,0:T(8,128)(2,1)S(1)}, u32[]{:S(2)}, u32[]{:S(2)}) async-start(bf16[16,64,512]{2,1,0:T(8,128)(2,1)} %bitcast.2), calls=%async_computation | async-start | bytes 2097152 | tf_op jit(solution)/shard_map/all_to_all | solution.py:128
  35.7 2.3 copy-start.4
  38.0 5.2 %copy-start.7 = (s32[1,1,16,6]{2,1,3,0:T(1,128)S(1)}, s32[1,1,16,6]{2,1,3,0:T(1,128)}, u32[]{:S(2)}) copy-start(s32[1,1,16,6]{2,1,3,0:T(1,128)} %param.11) | copy-start | bytes 1156
  38.0 53.6 %all-to-all-start.1 = ((bf16[8,512,512]{2,1,0:T(8,128)(2,1)}), bf16[8,512,512]{2,1,0:T(8,128)(2,1)}, u32[]{:S(2)}, u32[]{:S(2)}) async-start(bf16[8,512,512]{2,1,0:T(8,128)(2,1)} %broadcast_in_dim.28), calls=%async_computation.1 | async-start | bytes 8388608 | tf_op jit(solution)/shard_map/all_to_all | solution.py:101
  194.2 1.0 copy-start.5
  194.2 1.0 copy-start.8
  294.0 53.8 %all-to-all-start.6 = ((bf16[8,512,512]{2,1,0:T(8,128)(2,1)}), bf16[8,512,512]{2,1,0:T(8,128)(2,1)}, u32[]{:S(2)}, u32[]{:S(2)}) async-start(bf16[8,512,512]{2,1,0:T(8,128)(2,1)} %bitcast.51), calls=%async_computation.6 | async-start | bytes 8388608 | tf_op jit(solution)/shard_map/all_to_all | solution.py:106
  350.8 0.8 copy-start.2
  390.0 34.8 %all-to-all-start.8 = ((f32[128,5,512]{2,1,0:T(8,128)}), f32[128,5,512]{2,1,0:T(8,128)S(1)}, u32[]{:S(2)}, u32[]{:S(2)}) async-start(f32[128,5,512]{2,1,0:T(8,128)} %broadcast_in_dim.34), calls=%async_computation.8 | async-start | bytes 4194304 | tf_op jit(solution)/shard_map/all_to_all | solution.py:101
  394.8 34.9 %copy-start.1 = (bf16[1024,512]{1,0:T(8,128)(2,1)S(1)}, bf16[1024,512]{1,0:T(8,128)(2,1)}, u32[]{:S(2)}) copy-start(bf16[1024,512]{1,0:T(8,128)(2,1)} %param.7) | copy-start | bytes 3145732

commit v5 on v4

--- a/solution.py
+++ b/solution.py
@@ -145,21 +145,36 @@
     ]
     projected = jnp.dot(features, weight, preferred_element_type=jnp.float32).astype(jnp.bfloat16)
     blk_size = lax.axis_size("blk")
-    shard_rows = gather_by_exchange(projected, "blk", blk_size).reshape(-1, feature_width)
-
-    partial_value = forward_spmm(row_lists, tile_stack, shard_rows, row_tiles)
-    by_core = partial_value.reshape(row_tiles * tile_size, feature_width)
-    core_sum = reduce_by_exchange(by_core, "core", core_size).astype(jnp.bfloat16)
-    preact = reduce_by_exchange(core_sum, "rh", chip_size) + bias_vector
-    own_grad = (grad_out.astype(jnp.float32) * silu_slope(preact)).astype(jnp.bfloat16)
-    chip_grad = gather_by_exchange(own_grad, "rh", chip_size).reshape(-1, feature_width)
-    pre_grad = gather_by_exchange(chip_grad, "core", core_size)
-    activated = jax.nn.silu(preact).astype(jnp.bfloat16)
-    grad_tiles = pre_grad.reshape(row_tiles, tile_size, feature_width)
-    column_contribution = backward_spmm(row_lists, tile_stack, grad_tiles)
-    proj_grad = reduce_by_exchange(column_contribution, "blk", blk_size).astype(jnp.bfloat16)
+    chunks = 2
+    chunk_width = feature_width // chunks
+    activated_parts = []
+    grad_parts = []
+    bias_parts = []
+    for chunk in range(chunks):
+        columns = slice(chunk * chunk_width, (chunk + 1) * chunk_width)
+        shard_rows = gather_by_exchange(projected[:, columns], "blk", blk_size).reshape(
+            -1, chunk_width
+        )
+        partial_value = forward_spmm(row_lists, tile_stack, shard_rows, row_tiles)
+        by_core = partial_value.reshape(row_tiles * tile_size, chunk_width)
+        core_sum = reduce_by_exchange(by_core, "core", core_size).astype(jnp.bfloat16)
+        preact = reduce_by_exchange(core_sum, "rh", chip_size) + bias_vector[columns]
+        own_grad = (grad_out[:, columns].astype(jnp.float32) * silu_slope(preact)).astype(
+            jnp.bfloat16
+        )
+        activated_parts.append(jax.nn.silu(preact).astype(jnp.bfloat16))
+        bias_parts.append(jnp.sum(own_grad.astype(jnp.float32), axis=0))
+        chip_grad = gather_by_exchange(own_grad, "rh", chip_size).reshape(-1, chunk_width)
+        pre_grad = gather_by_exchange(chip_grad, "core", core_size)
+        grad_tiles = pre_grad.reshape(row_tiles, tile_size, chunk_width)
+        column_contribution = backward_spmm(row_lists, tile_stack, grad_tiles)
+        grad_parts.append(
+            reduce_by_exchange(column_contribution, "blk", blk_size).astype(jnp.bfloat16)
+        )
+    activated = jnp.concatenate(activated_parts, axis=1)
+    proj_grad = jnp.concatenate(grad_parts, axis=1)
+    local_bias = jnp.concatenate(bias_parts, axis=0)
     local_weight = jnp.einsum("nf,ng->fg", features, proj_grad, preferred_element_type=jnp.float32)
-    local_bias = jnp.sum(own_grad.astype(jnp.float32), axis=0)
     device_count = blk_size * rep_size
     chunk_rows = feature_width // device_count + 1
     pad_rows = jnp.zeros((device_count * chunk_rows - feature_width - 1, feature_width), jnp.float32)

time: 432 us -> 429 us (level)
  blocking collectives: 182 us -> 119 us
  starting transfers between devices: 23.3 us -> 53.3 us
  Pallas kernels: 40.9 us -> 67 us
    all_to_all x3 -> x1, blocking collectives: 108 us -> 37.1 us  [reduce_by_exchange(): received = lax.all_to_all(chunks, axis, 0, 0, tiled=True)]
    all_to_all x1 -> x6, waiting for transfers between devices: 48.9 us -> 82.7 us  [reduce_by_exchange(): received = lax.all_to_all(chunks, axis, 0, 0, tiled=True)]
    all_to_all x2 -> x3, waiting for transfers between devices: 75 us -> 43.1 us  [gather_by_exchange(): return lax.all_to_all(stacked, axis, 0, 0, tiled=True)]
    all_to_all x1 -> x6, starting transfers between devices: 4.72 us -> 32.3 us  [reduce_by_exchange(): received = lax.all_to_all(chunks, axis, 0, 0, tiled=True)]
    pallas_call x1 -> x2, Pallas kernels: 19.7 us -> 33.1 us  [backward_spmm(): pl.pallas_call(_backward_kernel, grid_spec=grid_spec, out_shape=jax.Shape...]
    pallas_call x1 -> x2, Pallas kernels: 21.2 us -> 33.9 us  [forward_spmm(): pl.pallas_call(_forward_kernel, grid_spec=grid_spec, out_shape=jax.ShapeD...]
    all_to_all x2 -> x4, blocking collectives: 73.6 us -> 81.7 us  [gather_by_exchange(): return lax.all_to_all(stacked, axis, 0, 0, tiled=True)]
    reduce_sum x4 -> x7, other arithmetic: 11.9 us -> 14.6 us  [reduce_by_exchange(): return jnp.sum(received.astype(jnp.float32), axis=0)]
  transfers between devices with their start and end apart: 4 -> 10, of which waited for: 4 -> 8; matrix products, arithmetic and copies ran while one was open for 1% -> 4% of each run, Pallas kernels for 0% -> 16%
where the time goes in v5:
time: 429 us; the launch traced here: 426 us
  waiting for transfers between devices  142 us (33%)
  blocking collectives  119 us (28%)
  Pallas kernels  67 us (16%)
  starting transfers between devices  53.3 us (12%)
  other arithmetic  22.3 us (5%)
  local copies, waits for them, and re-layouts  18.2 us (4%)
    all_to_all x6, waiting for transfers between devices, reduce_by_exchange(): received = lax.all_to_all(chunks, axis, 0, 0, tiled=True)  82.7 us
    all_to_all x4, blocking collectives, gather_by_exchange(): return lax.all_to_all(stacked, axis, 0, 0, tiled=True)  81.7 us
    all_to_all x3, waiting for transfers between devices, gather_by_exchange(): return lax.all_to_all(stacked, axis, 0, 0, tiled=True)  43.1 us
    all_to_all x1, blocking collectives, reduce_by_exchange(): received = lax.all_to_all(chunks, axis, 0, 0, tiled=True)  37.1 us
    pallas_call x2, Pallas kernels, forward_spmm(): pl.pallas_call(_forward_kernel, grid_spec=grid_spec, out_shape=jax.ShapeD...  33.9 us
    pallas_call x2, Pallas kernels, backward_spmm(): pl.pallas_call(_backward_kernel, grid_spec=grid_spec, out_shape=jax.Shape...  33.1 us
    all_to_all x6, starting transfers between devices, reduce_by_exchange(): received = lax.all_to_all(chunks, axis, 0, 0, tiled=True)  32.3 us
    all_to_all x1, waiting for transfers between devices, per_device(): lax.all_to_all(outgoing, ('rh', 'core'), split_axis=0, concat_axis=0, til...  16.5 us
  transfers between devices with their start and end apart: 10, of which 8 were waited for; matrix products, arithmetic and copies ran while one was open for 4% of the time, Pallas kernels for 16%

profile of v5, /device:TPU:1, one launch (start us, length us, event | category | flops | bytes accessed | tf_op | source)
XLA Modules:
  0.0 426.4 jit_solution(8791058999880642109)
XLA Ops:
  2.5 5.1 %gather_fusion = bf16[1024,512]{1,0:T(8,128)(2,1)} fusion(bf16[1024,512]{1,0:T(8,128)(2,1)S(1)} %copy-done, s32[1024]{0:T(1024)S(1)} %broadcast_clamp_fusion), kind=kCustom, calls=%fused_computation | custom fusion | bytes 2101248 | tf_op jit(solution)/shard_map/gather | solution.py:127
  7.6 8.6 %all-to-all-start = ((bf16[16,64,512]{2,1,0:T(8,128)(2,1)}), bf16[16,64,512]{2,1,0:T(8,128)(2,1)S(1)}, u32[]{:S(2)}, u32[]{:S(2)}) async-start(bf16[16,64,512]{2,1,0:T(8,128)(2,1)} %bitcast.2), calls=%async_computation | async-start | bytes 2097152 | tf_op jit(solution)/shard_map/all_to_all | solution.py:128
  16.7 16.5 %all-to-all-done = bf16[16,64,512]{2,1,0:T(8,128)(2,1)S(1)} async-done(((bf16[16,64,512]{2,1,0:T(8,128)(2,1)}), bf16[16,64,512]{2,1,0:T(8,128)(2,1)S(1)}, u32[]{:S(2)}, u32[]{:S(2)}) %all-to-all-start) | async-done | bytes 1048608 | tf_op jit(solution)/shard_map/all_to_all | solution.py:128
  36.0 30.6 %all_to_all.75 = bf16[8,512,256]{2,1,0:T(8,128)(2,1)} all-to-all(bf16[8,512,256]{2,1,0:T(8,128)(2,1)S(1)} %broadcast_in_dim.37), channel_id=1, replica_groups=mesh['blk'=8,'rh'=8,'core'=2] {'blk'}, dimensions={0} | all-to-all | bytes 4194304 | tf_op jit(solution)/shard_map/all_to_all | solution.py:101
  68.1 3.7 all-to-all-start.1
  72.6 16.9 %shard_map.111 = bf16[32,256,256]{2,1,0:T(8,128)(2,1)} custom-call(s32[16,6]{1,0:T(8,128)} %fusion.3.rows_ref, bf16[16,6,256,256]{3,2,1,0:T(8,128)(2,1)} %bitcast.48, bf16[4096,256]{1,0:T(8,128)(2,1)} %bitcast.59), custom_call_target="tpu_custom_call" | custom-call | tf_op jit(solution)/shard_map/pallas_call | solution.py:49
  89.5 7.1 %all-to-all-done.1 = bf16[8,512,256]{2,1,0:T(8,128)(2,1)S(1)} async-done(((bf16[8,512,256]{2,1,0:T(8,128)(2,1)}), bf16[8,512,256]{2,1,0:T(8,128)(2,1)S(1)}, u32[]{:S(2)}, u32[]{:S(2)}) %all-to-all-start.1) | async-done | bytes 2097184 | tf_op jit(solution)/shard_map/all_to_all | solution.py:101
  98.0 8.7 %all-to-all-start.5 = ((bf16[2,4096,256]{2,1,0:T(8,128)(2,1)}), bf16[2,4096,256]{2,1,0:T(8,128)(2,1)}, u32[]{:S(2)}, u32[]{:S(2)}) async-start(bf16[2,4096,256]{2,1,0:T(8,128)(2,1)} %bitcast.53), calls=%async_computation.5 | async-start | bytes 8388608 | tf_op jit(solution)/shard_map/all_to_all | solution.py:106
  106.7 17.0 %shard_map.110 = bf16[32,256,256]{2,1,0:T(8,128)(2,1)} custom-call(s32[16,6]{1,0:T(8,128)} %fusion.3.rows_ref, bf16[16,6,256,256]{3,2,1,0:T(8,128)(2,1)} %bitcast.49, bf16[4096,256]{1,0:T(8,128)(2,1)} %bitcast.58), custom_call_target="tpu_custom_call" | custom-call | tf_op jit(solution)/shard_map/pallas_call | solution.py:49
  123.7 5.6 %all-to-all-start.2 = ((bf16[2,4096,256]{2,1,0:T(8,128)(2,1)}), bf16[2,4096,256]{2,1,0:T(8,128)(2,1)}, u32[]{:S(2)}, u32[]{:S(2)}) async-start(bf16[2,4096,256]{2,1,0:T(8,128)(2,1)} %bitcast.54), calls=%async_computation.2 | async-start | bytes 8388608 | tf_op jit(solution)/shard_map/all_to_all | solution.py:106
  129.3 4.9 %reduce_sum.118 = bf16[4096,256]{1,0:T(8,128)(2,1)} reduce(bf16[2,4096,256]{2,1,0:T(8,128)(2,1)} %all-to-all-done.5, bf16[]{:T(256)} %constant.87.clone.1), dimensions={0}, to_apply=%region_6.7 | reduce | flops 1048576 | bytes 6291458 | tf_op jit(solution)/shard_map/reduce_sum | solution.py:107
  134.3 4.7 %all-to-all-start.6 = ((bf16[8,512,256]{2,1,0:T(8,128)(2,1)}), bf16[8,512,256]{2,1,0:T(8,128)(2,1)S(1)}, u32[]{:S(2)}, u32[]{:S(2)}) async-start(bf16[8,512,256]{2,1,0:T(8,128)(2,1)} %bitcast.14), calls=%async_computation.6 | async-start | bytes 4194304 | tf_op jit(solution)/shard_map/all_to_all | solution.py:106
  139.0 4.9 %reduce_sum.116 = bf16[4096,256]{1,0:T(8,128)(2,1)} reduce(bf16[2,4096,256]{2,1,0:T(8,128)(2,1)} %all-to-all-done.2, bf16[]{:T(256)} %constant.87.clone.1), dimensions={0}, to_apply=%region_4.5 | reduce | flops 1048576 | bytes 6291458 | tf_op jit(solution)/shard_map/reduce_sum | solution.py:107
  143.9 21.3 %all-to-all-done.6 = bf16[8,512,256]{2,1,0:T(8,128)(2,1)S(1)} async-done(((bf16[8,512,256]{2,1,0:T(8,128)(2,1)}), bf16[8,512,256]{2,1,0:T(8,128)(2,1)S(1)}, u32[]{:S(2)}, u32[]{:S(2)}) %all-to-all-start.6) | async-done | bytes 2097184 | tf_op jit(solution)/shard_map/all_to_all | solution.py:106
  165.2 5.3 %all-to-all-start.3 = ((bf16[8,512,256]{2,1,0:T(8,128)(2,1)}), bf16[8,512,256]{2,1,0:T(8,128)(2,1)}, u32[]{:S(2)}, u32[]{:S(2)}) async-start(bf16[8,512,256]{2,1,0:T(8,128)(2,1)} %bitcast.11), calls=%async_computation.3 | async-start | bytes 4194304 | tf_op jit(solution)/shard_map/all_to_all | solution.py:106
  170.8 26.0 %all-to-all-done.3 = bf16[8,512,256]{2,1,0:T(8,128)(2,1)} async-done(((bf16[8,512,256]{2,1,0:T(8,128)(2,1)}), bf16[8,512,256]{2,1,0:T(8,128)(2,1)}, u32[]{:S(2)}, u32[]{:S(2)}) %all-to-all-start.3) | async-done | bytes 2097184 | tf_op jit(solution)/shard_map/all_to_all | solution.py:106
  200.1 31.8 %all_to_all.76 = bf16[8,512,256]{2,1,0:T(8,128)(2,1)S(1)} all-to-all(bf16[8,512,256]{2,1,0:T(8,128)(2,1)S(1)} %broadcast_in_dim.38), channel_id=1, replica_groups=mesh['blk'=8,'rh'=8,'core'=2] {'rh'}, dimensions={0} | all-to-all | bytes 4194304 | tf_op jit(solution)/shard_map/all_to_all | solution.py:101
  232.2 10.2 %all_to_all.77 = bf16[2,4096,256]{2,1,0:T(8,128)(2,1)} all-to-all(bf16[2,4096,256]{2,1,0:T(8,128)(2,1)S(1)} %broadcast_in_dim.40), channel_id=1, replica_groups=mesh['blk'=8,'rh'=8,'core'=2] {'core'}, dimensions={0} | all-to-all | bytes 8388608 | tf_op jit(solution)/shard_map/all_to_all | solution.py:101
  243.9 3.8 all-to-all-start.10
  247.7 16.5 %shard_map.112 = bf16[4096,256]{1,0:T(8,128)(2,1)} custom-call(s32[16,6]{1,0:T(8,128)} %fusion.3.rows_ref, bf16[16,6,256,256]{3,2,1,0:T(8,128)(2,1)} %bitcast.50, bf16[32,256,256]{2,1,0:T(8,128)(2,1)} %bitcast.55), custom_call_target="tpu_custom_call" | custom-call | tf_op jit(solution)/shard_map/pallas_call | solution.py:88
  264.3 9.4 %all-to-all-done.10 = bf16[8,512,256]{2,1,0:T(8,128)(2,1)S(1)} async-done(((bf16[8,512,256]{2,1,0:T(8,128)(2,1)}), bf16[8,512,256]{2,1,0:T(8,128)(2,1)S(1)}, u32[]{:S(2)}, u32[]{:S(2)}) %all-to-all-start.10) | async-done | bytes 2097184 | tf_op jit(solution)/shard_map/all_to_all | solution.py:101
  273.9 9.0 %all_to_all.78 = bf16[2,4096,256]{2,1,0:T(8,128)(2,1)} all-to-all(bf16[2,4096,256]{2,1,0:T(8,128)(2,1)S(1)} %broadcast_in_dim.43), channel_id=1, replica_groups=mesh['blk'=8,'rh'=8,'core'=2] {'core'}, dimensions={0} | all-to-all | bytes 8388608 | tf_op jit(solution)/shard_map/all_to_all | solution.py:101
  282.9 3.6 all-to-all-start.9
  286.5 16.6 %shard_map.113 = bf16[4096,256]{1,0:T(8,128)(2,1)} custom-call(s32[16,6]{1,0:T(8,128)} %fusion.3.rows_ref, bf16[16,6,256,256]{3,2,1,0:T(8,128)(2,1)} %bitcast.51, bf16[32,256,256]{2,1,0:T(8,128)(2,1)} %bitcast.56), custom_call_target="tpu_custom_call" | custom-call | tf_op jit(solution)/shard_map/pallas_call | solution.py:88
  303.1 10.1 %all-to-all-done.9 = bf16[8,512,256]{2,1,0:T(8,128)(2,1)S(1)} async-done(((bf16[8,512,256]{2,1,0:T(8,128)(2,1)}), bf16[8,512,256]{2,1,0:T(8,128)(2,1)S(1)}, u32[]{:S(2)}, u32[]{:S(2)}) %all-to-all-start.9) | async-done | bytes 2097184 | tf_op jit(solution)/shard_map/all_to_all | solution.py:106
  313.2 4.3 %all-to-all-start.12 = ((bf16[8,512,256]{2,1,0:T(8,128)(2,1)}), bf16[8,512,256]{2,1,0:T(8,128)(2,1)}, u32[]{:S(2)}, u32[]{:S(2)}) async-start(bf16[8,512,256]{2,1,0:T(8,128)(2,1)} %bitcast.57), calls=%async_computation.12 | async-start | bytes 4194304 | tf_op jit(solution)/shard_map/all_to_all | solution.py:106
  318.0 25.4 %all-to-all-done.12 = bf16[8,512,256]{2,1,0:T(8,128)(2,1)} async-done(((bf16[8,512,256]{2,1,0:T(8,128)(2,1)}), bf16[8,512,256]{2,1,0:T(8,128)(2,1)}, u32[]{:S(2)}, u32[]{:S(2)}) %all-to-all-start.12) | async-done | bytes 2097184 | tf_op jit(solution)/shard_map/all_to_all | solution.py:106
  347.6 37.1 %all_to_all.79 = f32[128,5,512]{2,1,0:T(8,128)S(1)} all-to-all(f32[128,5,512]{2,1,0:T(8,128)} %reshape.206), channel_id=1, replica_groups=mesh['blk'=8,'rh'=8,'core'=2] {'blk','rh','core'}, dimensions={0} | all-to-all | bytes 2621440 | tf_op jit(solution)/shard_map/all_to_all | solution.py:106
  386.6 4.9 %all-to-all-start.14 = ((f32[128,5,512]{2,1,0:T(8,128)}), f32[128,5,512]{2,1,0:T(8,128)S(1)}, u32[]{:S(2)}, u32[]{:S(2)}) async-start(f32[128,5,512]{2,1,0:T(8,128)} %broadcast_in_dim.46), calls=%async_computation.14 | async-start | bytes 4194304 | tf_op jit(solution)/shard_map/all_to_all | solution.py:101
  392.4 2.6 convolution_convert_fusion
  394.9 26.6 %all-to-all-done.14 = f32[128,5,512]{2,1,0:T(8,128)S(1)} async-done(((f32[128,5,512]{2,1,0:T(8,128)}), f32[128,5,512]{2,1,0:T(8,128)S(1)}, u32[]{:S(2)}, u32[]{:S(2)}) %all-to-all-start.14) | async-done | bytes 1310752 | tf_op jit(solution)/shard_map/all_to_all | solution.py:101
  422.8 2.3 slice_multiply_fusion
  (75 shorter events, 24.2 us)
Async XLA Ops:
  0.6 1.9 copy-start
  7.6 8.6 %copy-start.11 = (s32[1,16,16]{2,1,0:T(8,128)S(1)}, s32[1,16,16]{2,1,0:T(8,128)}, u32[]{:S(2)}) copy-start(s32[1,16,16]{2,1,0:T(8,128)} %param.8) | copy-start | bytes 3076
  7.6 25.6 %all-to-all-start = ((bf16[16,64,512]{2,1,0:T(8,128)(2,1)}), bf16[16,64,512]{2,1,0:T(8,128)(2,1)S(1)}, u32[]{:S(2)}, u32[]{:S(2)}) async-start(bf16[16,64,512]{2,1,0:T(8,128)(2,1)} %bitcast.2), calls=%async_computation | async-start | bytes 2097152 | tf_op jit(solution)/shard_map/all_to_all | solution.py:128
  33.3 2.0 copy-start.8
  35.2 0.8 copy-start.3
  35.7 31.0 %copy-start.5 = (bf16[512,512]{1,0:T(8,128)(2,1)}, bf16[512,512]{1,0:T(8,128)(2,1)S(1)}, u32[]{:S(2)}) copy-start(bf16[512,512]{1,0:T(8,128)(2,1)S(1)} %convolution_convert_fusion.1) | copy-start | bytes 1572868
  68.1 3.7 copy-start.12
  68.1 28.5 %all-to-all-start.1 = ((bf16[8,512,256]{2,1,0:T(8,128)(2,1)}), bf16[8,512,256]{2,1,0:T(8,128)(2,1)S(1)}, u32[]{:S(2)}, u32[]{:S(2)}) async-start(bf16[8,512,256]{2,1,0:T(8,128)(2,1)} %broadcast_in_dim.36), calls=%async_computation.1 | async-start | bytes 4194304 | tf_op jit(solution)/shard_map/all_to_all | solution.py:101
  96.6 1.4 copy-start.2
  98.0 25.7 %all-to-all-start.5 = ((bf16[2,4096,256]{2,1,0:T(8,128)(2,1)}), bf16[2,4096,256]{2,1,0:T(8,128)(2,1)}, u32[]{:S(2)}, u32[]{:S(2)}) async-start(bf16[2,4096,256]{2,1,0:T(8,128)(2,1)} %bitcast.53), calls=%async_computation.5 | async-start | bytes 8388608 | tf_op jit(solution)/shard_map/all_to_all | solution.py:106
  123.7 10.6 %all-to-all-start.2 = ((bf16[2,4096,256]{2,1,0:T(8,128)(2,1)}), bf16[2,4096,256]{2,1,0:T(8,128)(2,1)}, u32[]{:S(2)}, u32[]{:S(2)}) async-start(bf16[2,4096,256]{2,1,0:T(8,128)(2,1)} %bitcast.54), calls=%async_computation.2 | async-start | bytes 8388608 | tf_op jit(solution)/shard_map/all_to_all | solution.py:106
  134.3 30.9 %all-to-all-start.6 = ((bf16[8,512,256]{2,1,0:T(8,128)(2,1)}), bf16[8,512,256]{2,1,0:T(8,128)(2,1)S(1)}, u32[]{:S(2)}, u32[]{:S(2)}) async-start(bf16[8,512,256]{2,1,0:T(8,128)(2,1)} %bitcast.14), calls=%async_computation.6 | async-start | bytes 4194304 | tf_op jit(solution)/shard_map/all_to_all | solution.py:106
  165.2 5.3 %copy-start.13 = (f32[512]{0:T(512)S(1)}, f32[512]{0:T(512)}, u32[]{:S(2)}) copy-start(f32[512]{0:T(512)} %param.10) | copy-start | bytes 6148
  165.2 31.6 %all-to-all-start.3 = ((bf16[8,512,256]{2,1,0:T(8,128)(2,1)}), bf16[8,512,256]{2,1,0:T(8,128)(2,1)}, u32[]{:S(2)}, u32[]{:S(2)}) async-start(bf16[8,512,256]{2,1,0:T(8,128)(2,1)} %bitcast.11), calls=%async_computation.3 | async-start | bytes 4194304 | tf_op jit(solution)/shard_map/all_to_all | solution.py:106
  170.8 27.9 %copy-start.7 = (bf16[512,512]{1,0:T(8,128)(2,1)S(1)}, bf16[512,512]{1,0:T(8,128)(2,1)}, u32[]{:S(2)}) copy-start(bf16[512,512]{1,0:T(8,128)(2,1)} %param.13) | copy-start | bytes 1572868
  243.9 29.7 %all-to-all-start.10 = ((bf16[8,512,256]{2,1,0:T(8,128)(2,1)}), bf16[8,512,256]{2,1,0:T(8,128)(2,1)S(1)}, u32[]{:S(2)}, u32[]{:S(2)}) async-start(bf16[8,512,256]{2,1,0:T(8,128)(2,1)} %broadcast_in_dim.41), calls=%async_computation.10 | async-start | bytes 4194304 | tf_op jit(solution)/shard_map/all_to_all | solution.py:101
  282.9 30.3 %all-to-all-start.9 = ((bf16[8,512,256]{2,1,0:T(8,128)(2,1)}), bf16[8,512,256]{2,1,0:T(8,128)(2,1)S(1)}, u32[]{:S(2)}, u32[]{:S(2)}) async-start(bf16[8,512,256]{2,1,0:T(8,128)(2,1)} %bitcast.17), calls=%async_computation.9 | async-start | bytes 4194304 | tf_op jit(solution)/shard_map/all_to_all | solution.py:106
  313.2 30.2 %all-to-all-start.12 = ((bf16[8,512,256]{2,1,0:T(8,128)(2,1)}), bf16[8,512,256]{2,1,0:T(8,128)(2,1)}, u32[]{:S(2)}, u32[]{:S(2)}) async-start(bf16[8,512,256]{2,1,0:T(8,128)(2,1)} %bitcast.57), calls=%async_computation.12 | async-start | bytes 4194304 | tf_op jit(solution)/shard_map/all_to_all | solution.py:106
  317.6 27.7 %copy-start.4 = (bf16[512,512]{1,0:T(8,128)(2,1)S(1)}, bf16[512,512]{1,0:T(8,128)(2,1)}, u32[]{:S(2)}) copy-start(bf16[512,512]{1,0:T(8,128)(2,1)} %copy-done.3) | copy-start | bytes 1572868
  318.0 27.8 %copy-start.9 = (bf16[512,256]{1,0:T(8,128)(2,1)}, bf16[512,256]{1,0:T(8,128)(2,1)S(1)}, u32[]{:S(2)}) copy-start(bf16[512,256]{1,0:T(8,128)(2,1)S(1)} %reduce_sum.120) | copy-start | bytes 786436
  345.3 0.7 copy-start.10
  386.6 5.0 %copy-start.6 = (bf16[512,256]{1,0:T(8,128)(2,1)S(1)}, bf16[512,256]{1,0:T(8,128)(2,1)}, u32[]{:S(2)}) copy-start(bf16[512,256]{1,0:T(8,128)(2,1)} %get-tuple-element.11) | copy-start | bytes 786436
  386.6 34.9 %all-to-all-start.14 = ((f32[128,5,512]{2,1,0:T(8,128)}), f32[128,5,512]{2,1,0:T(8,128)S(1)}, u32[]{:S(2)}, u32[]{:S(2)}) async-start(f32[128,5,512]{2,1,0:T(8,128)} %broadcast_in_dim.46), calls=%async_computation.14 | async-start | bytes 4194304 | tf_op jit(solution)/shard_map/all_to_all | solution.py:101
  392.4 34.0 %copy-start.1 = (bf16[1024,512]{1,0:T(8,128)(2,1)S(1)}, bf16[1024,512]{1,0:T(8,128)(2,1)}, u32[]{:S(2)}) copy-start(bf16[1024,512]{1,0:T(8,128)(2,1)} %param.7) | copy-start | bytes 3145732

commit v6 on v5

--- a/solution.py
+++ b/solution.py
@@ -181,8 +181,10 @@
     stacked = jnp.concatenate([local_weight, local_bias[None, :], pad_rows], axis=0)
     every = ("blk", "rh", "core")
     reduced = reduce_by_exchange(stacked, every, device_count)
-    stacked_sum = gather_by_exchange(reduced, every, device_count).reshape(
-        -1, feature_width
+    stacked_sum = (
+        gather_by_exchange(reduced.astype(jnp.bfloat16), every, device_count)
+        .reshape(-1, feature_width)
+        .astype(jnp.float32)
     )
     weight_sum = stacked_sum[:feature_width]
     bias_sum = stacked_sum[feature_width]

time: 429 us -> 415 us (0.967)
  waiting for transfers between devices: 142 us -> 133 us
    all_to_all x3, waiting for transfers between devices: 43.1 us -> 33.6 us  [gather_by_exchange(): return lax.all_to_all(stacked, axis, 0, 0, tiled=True)]
  transfers between devices with their start and end apart: 10 -> 10, of which waited for: 8 -> 8; matrix products, arithmetic and copies ran while one was open for 4% -> 3% of each run, Pallas kernels for 16% -> 16%
where the time goes in v6:
time: 415 us; the launch traced here: 412 us
  waiting for transfers between devices  133 us (32%)
  blocking collectives  119 us (29%)
  Pallas kernels  67 us (16%)
  starting transfers between devices  53.2 us (13%)
  other arithmetic  20.5 us (5%)
  local copies, waits for them, and re-layouts  16.6 us (4%)
    all_to_all x6, waiting for transfers between devices, reduce_by_exchange(): received = lax.all_to_all(chunks, axis, 0, 0, tiled=True)  82.7 us
    all_to_all x4, blocking collectives, gather_by_exchange(): return lax.all_to_all(stacked, axis, 0, 0, tiled=True)  81.7 us
    all_to_all x1, blocking collectives, reduce_by_exchange(): received = lax.all_to_all(chunks, axis, 0, 0, tiled=True)  37.1 us
    pallas_call x2, Pallas kernels, forward_spmm(): pl.pallas_call(_forward_kernel, grid_spec=grid_spec, out_shape=jax.ShapeD...  33.9 us
    all_to_all x3, waiting for transfers between devices, gather_by_exchange(): return lax.all_to_all(stacked, axis, 0, 0, tiled=True)  33.6 us
    pallas_call x2, Pallas kernels, backward_spmm(): pl.pallas_call(_backward_kernel, grid_spec=grid_spec, out_shape=jax.Shape...  33.1 us
    all_to_all x6, starting transfers between devices, reduce_by_exchange(): received = lax.all_to_all(chunks, axis, 0, 0, tiled=True)  32.3 us
    all_to_all x1, waiting for transfers between devices, per_device(): lax.all_to_all(outgoing, ('rh', 'core'), split_axis=0, concat_axis=0, til...  16.5 us
  transfers between devices with their start and end apart: 10, of which 8 were waited for; matrix products, arithmetic and copies ran while one was open for 3% of the time, Pallas kernels for 16%

profile of v6, /device:TPU:1, one launch (start us, length us, event | category | flops | bytes accessed | tf_op | source)
XLA Modules:
  0.0 412.1 jit_solution(17037263743959283308)
XLA Ops:
  2.5 5.1 %gather_fusion = bf16[1024,512]{1,0:T(8,128)(2,1)} fusion(bf16[1024,512]{1,0:T(8,128)(2,1)S(1)} %copy-done, s32[1024]{0:T(1024)S(1)} %broadcast_clamp_fusion), kind=kCustom, calls=%fused_computation | custom fusion | bytes 2101248 | tf_op jit(solution)/shard_map/gather | solution.py:127
  7.6 8.6 %all-to-all-start = ((bf16[16,64,512]{2,1,0:T(8,128)(2,1)}), bf16[16,64,512]{2,1,0:T(8,128)(2,1)S(1)}, u32[]{:S(2)}, u32[]{:S(2)}) async-start(bf16[16,64,512]{2,1,0:T(8,128)(2,1)} %bitcast.2), calls=%async_computation | async-start | bytes 2097152 | tf_op jit(solution)/shard_map/all_to_all | solution.py:128
  16.7 16.5 %all-to-all-done = bf16[16,64,512]{2,1,0:T(8,128)(2,1)S(1)} async-done(((bf16[16,64,512]{2,1,0:T(8,128)(2,1)}), bf16[16,64,512]{2,1,0:T(8,128)(2,1)S(1)}, u32[]{:S(2)}, u32[]{:S(2)}) %all-to-all-start) | async-done | bytes 1048608 | tf_op jit(solution)/shard_map/all_to_all | solution.py:128
  33.3 2.0 gather_fusion.1
  36.0 30.6 %all_to_all.75 = bf16[8,512,256]{2,1,0:T(8,128)(2,1)} all-to-all(bf16[8,512,256]{2,1,0:T(8,128)(2,1)S(1)} %broadcast_in_dim.37), channel_id=1, replica_groups=mesh['blk'=8,'rh'=8,'core'=2] {'blk'}, dimensions={0} | all-to-all | bytes 4194304 | tf_op jit(solution)/shard_map/all_to_all | solution.py:101
  68.1 3.7 all-to-all-start.1
  72.6 16.9 %shard_map.111 = bf16[32,256,256]{2,1,0:T(8,128)(2,1)} custom-call(s32[16,6]{1,0:T(8,128)} %fusion.3.rows_ref, bf16[16,6,256,256]{3,2,1,0:T(8,128)(2,1)} %bitcast.48, bf16[4096,256]{1,0:T(8,128)(2,1)} %bitcast.59), custom_call_target="tpu_custom_call" | custom-call | tf_op jit(solution)/shard_map/pallas_call | solution.py:49
  89.5 7.1 %all-to-all-done.1 = bf16[8,512,256]{2,1,0:T(8,128)(2,1)S(1)} async-done(((bf16[8,512,256]{2,1,0:T(8,128)(2,1)}), bf16[8,512,256]{2,1,0:T(8,128)(2,1)S(1)}, u32[]{:S(2)}, u32[]{:S(2)}) %all-to-all-start.1) | async-done | bytes 2097184 | tf_op jit(solution)/shard_map/all_to_all | solution.py:101
  98.0 8.7 %all-to-all-start.5 = ((bf16[2,4096,256]{2,1,0:T(8,128)(2,1)}), bf16[2,4096,256]{2,1,0:T(8,128)(2,1)}, u32[]{:S(2)}, u32[]{:S(2)}) async-start(bf16[2,4096,256]{2,1,0:T(8,128)(2,1)} %bitcast.53), calls=%async_computation.5 | async-start | bytes 8388608 | tf_op jit(solution)/shard_map/all_to_all | solution.py:106
  106.7 17.0 %shard_map.110 = bf16[32,256,256]{2,1,0:T(8,128)(2,1)} custom-call(s32[16,6]{1,0:T(8,128)} %fusion.3.rows_ref, bf16[16,6,256,256]{3,2,1,0:T(8,128)(2,1)} %bitcast.49, bf16[4096,256]{1,0:T(8,128)(2,1)} %bitcast.58), custom_call_target="tpu_custom_call" | custom-call | tf_op jit(solution)/shard_map/pallas_call | solution.py:49
  123.7 5.6 %all-to-all-start.2 = ((bf16[2,4096,256]{2,1,0:T(8,128)(2,1)}), bf16[2,4096,256]{2,1,0:T(8,128)(2,1)}, u32[]{:S(2)}, u32[]{:S(2)}) async-start(bf16[2,4096,256]{2,1,0:T(8,128)(2,1)} %bitcast.54), calls=%async_computation.2 | async-start | bytes 8388608 | tf_op jit(solution)/shard_map/all_to_all | solution.py:106
  129.3 4.9 %reduce_sum.118 = bf16[4096,256]{1,0:T(8,128)(2,1)} reduce(bf16[2,4096,256]{2,1,0:T(8,128)(2,1)} %all-to-all-done.5, bf16[]{:T(256)} %constant.87.clone.1), dimensions={0}, to_apply=%region_6.7 | reduce | flops 1048576 | bytes 6291458 | tf_op jit(solution)/shard_map/reduce_sum | solution.py:107
  134.3 4.7 %all-to-all-start.6 = ((bf16[8,512,256]{2,1,0:T(8,128)(2,1)}), bf16[8,512,256]{2,1,0:T(8,128)(2,1)S(1)}, u32[]{:S(2)}, u32[]{:S(2)}) async-start(bf16[8,512,256]{2,1,0:T(8,128)(2,1)} %bitcast.14), calls=%async_computation.6 | async-start | bytes 4194304 | tf_op jit(solution)/shard_map/all_to_all | solution.py:106
  139.0 4.9 %reduce_sum.116 = bf16[4096,256]{1,0:T(8,128)(2,1)} reduce(bf16[2,4096,256]{2,1,0:T(8,128)(2,1)} %all-to-all-done.2, bf16[]{:T(256)} %constant.87.clone.1), dimensions={0}, to_apply=%region_4.5 | reduce | flops 1048576 | bytes 6291458 | tf_op jit(solution)/shard_map/reduce_sum | solution.py:107
  143.9 21.3 %all-to-all-done.6 = bf16[8,512,256]{2,1,0:T(8,128)(2,1)S(1)} async-done(((bf16[8,512,256]{2,1,0:T(8,128)(2,1)}), bf16[8,512,256]{2,1,0:T(8,128)(2,1)S(1)}, u32[]{:S(2)}, u32[]{:S(2)}) %all-to-all-start.6) | async-done | bytes 2097184 | tf_op jit(solution)/shard_map/all_to_all | solution.py:106
  165.2 5.3 %all-to-all-start.3 = ((bf16[8,512,256]{2,1,0:T(8,128)(2,1)}), bf16[8,512,256]{2,1,0:T(8,128)(2,1)}, u32[]{:S(2)}, u32[]{:S(2)}) async-start(bf16[8,512,256]{2,1,0:T(8,128)(2,1)} %bitcast.11), calls=%async_computation.3 | async-start | bytes 4194304 | tf_op jit(solution)/shard_map/all_to_all | solution.py:106
  170.8 26.0 %all-to-all-done.3 = bf16[8,512,256]{2,1,0:T(8,128)(2,1)} async-done(((bf16[8,512,256]{2,1,0:T(8,128)(2,1)}), bf16[8,512,256]{2,1,0:T(8,128)(2,1)}, u32[]{:S(2)}, u32[]{:S(2)}) %all-to-all-start.3) | async-done | bytes 2097184 | tf_op jit(solution)/shard_map/all_to_all | solution.py:106
  200.2 31.8 %all_to_all.76 = bf16[8,512,256]{2,1,0:T(8,128)(2,1)S(1)} all-to-all(bf16[8,512,256]{2,1,0:T(8,128)(2,1)S(1)} %broadcast_in_dim.38), channel_id=1, replica_groups=mesh['blk'=8,'rh'=8,'core'=2] {'rh'}, dimensions={0} | all-to-all | bytes 4194304 | tf_op jit(solution)/shard_map/all_to_all | solution.py:101
  232.3 10.2 %all_to_all.77 = bf16[2,4096,256]{2,1,0:T(8,128)(2,1)} all-to-all(bf16[2,4096,256]{2,1,0:T(8,128)(2,1)S(1)} %broadcast_in_dim.40), channel_id=1, replica_groups=mesh['blk'=8,'rh'=8,'core'=2] {'core'}, dimensions={0} | all-to-all | bytes 8388608 | tf_op jit(solution)/shard_map/all_to_all | solution.py:101
  244.0 3.8 all-to-all-start.10
  247.8 16.5 %shard_map.112 = bf16[4096,256]{1,0:T(8,128)(2,1)} custom-call(s32[16,6]{1,0:T(8,128)} %fusion.3.rows_ref, bf16[16,6,256,256]{3,2,1,0:T(8,128)(2,1)} %bitcast.50, bf16[32,256,256]{2,1,0:T(8,128)(2,1)} %bitcast.55), custom_call_target="tpu_custom_call" | custom-call | tf_op jit(solution)/shard_map/pallas_call | solution.py:88
  264.4 9.4 %all-to-all-done.10 = bf16[8,512,256]{2,1,0:T(8,128)(2,1)S(1)} async-done(((bf16[8,512,256]{2,1,0:T(8,128)(2,1)}), bf16[8,512,256]{2,1,0:T(8,128)(2,1)S(1)}, u32[]{:S(2)}, u32[]{:S(2)}) %all-to-all-start.10) | async-done | bytes 2097184 | tf_op jit(solution)/shard_map/all_to_all | solution.py:101
  274.0 9.0 %all_to_all.78 = bf16[2,4096,256]{2,1,0:T(8,128)(2,1)} all-to-all(bf16[2,4096,256]{2,1,0:T(8,128)(2,1)S(1)} %broadcast_in_dim.43), channel_id=1, replica_groups=mesh['blk'=8,'rh'=8,'core'=2] {'core'}, dimensions={0} | all-to-all | bytes 8388608 | tf_op jit(solution)/shard_map/all_to_all | solution.py:101
  283.0 3.6 all-to-all-start.9
  286.6 16.6 %shard_map.113 = bf16[4096,256]{1,0:T(8,128)(2,1)} custom-call(s32[16,6]{1,0:T(8,128)} %fusion.3.rows_ref, bf16[16,6,256,256]{3,2,1,0:T(8,128)(2,1)} %bitcast.51, bf16[32,256,256]{2,1,0:T(8,128)(2,1)} %bitcast.56), custom_call_target="tpu_custom_call" | custom-call | tf_op jit(solution)/shard_map/pallas_call | solution.py:88
  303.2 10.1 %all-to-all-done.9 = bf16[8,512,256]{2,1,0:T(8,128)(2,1)S(1)} async-done(((bf16[8,512,256]{2,1,0:T(8,128)(2,1)}), bf16[8,512,256]{2,1,0:T(8,128)(2,1)S(1)}, u32[]{:S(2)}, u32[]{:S(2)}) %all-to-all-start.9) | async-done | bytes 2097184 | tf_op jit(solution)/shard_map/all_to_all | solution.py:106
  313.2 4.3 %all-to-all-start.12 = ((bf16[8,512,256]{2,1,0:T(8,128)(2,1)}), bf16[8,512,256]{2,1,0:T(8,128)(2,1)}, u32[]{:S(2)}, u32[]{:S(2)}) async-start(bf16[8,512,256]{2,1,0:T(8,128)(2,1)} %bitcast.57), calls=%async_computation.12 | async-start | bytes 4194304 | tf_op jit(solution)/shard_map/all_to_all | solution.py:106
  318.1 25.4 %all-to-all-done.12 = bf16[8,512,256]{2,1,0:T(8,128)(2,1)} async-done(((bf16[8,512,256]{2,1,0:T(8,128)(2,1)}), bf16[8,512,256]{2,1,0:T(8,128)(2,1)}, u32[]{:S(2)}, u32[]{:S(2)}) %all-to-all-start.12) | async-done | bytes 2097184 | tf_op jit(solution)/shard_map/all_to_all | solution.py:106
  343.5 2.0 reduce_sum.121
  347.7 37.1 %all_to_all.79 = f32[128,5,512]{2,1,0:T(8,128)S(1)} all-to-all(f32[128,5,512]{2,1,0:T(8,128)} %reshape.208), channel_id=1, replica_groups=mesh['blk'=8,'rh'=8,'core'=2] {'blk','rh','core'}, dimensions={0} | all-to-all | bytes 2621440 | tf_op jit(solution)/shard_map/all_to_all | solution.py:106
  386.1 4.8 %all-to-all-start.14 = ((bf16[128,5,512]{2,1,0:T(8,128)(2,1)}), bf16[128,5,512]{2,1,0:T(8,128)(2,1)S(1)}, u32[]{:S(2)}, u32[]{:S(2)}) async-start(bf16[128,5,512]{2,1,0:T(8,128)(2,1)} %broadcast_in_dim.46), calls=%async_computation.14 | async-start | bytes 2097152 | tf_op jit(solution)/shard_map/all_to_all | solution.py:101
  393.1 17.1 %all-to-all-done.14 = bf16[128,5,512]{2,1,0:T(8,128)(2,1)S(1)} async-done(((bf16[128,5,512]{2,1,0:T(8,128)(2,1)}), bf16[128,5,512]{2,1,0:T(8,128)(2,1)S(1)}, u32[]{:S(2)}, u32[]{:S(2)}) %all-to-all-start.14) | async-done | bytes 655392 | tf_op jit(solution)/shard_map/all_to_all | solution.py:101
  (83 shorter events, 20.4 us)
Async XLA Ops:
  0.6 1.9 copy-start
  7.6 8.6 %copy-start.15 = (s32[1,16,16]{2,1,0:T(8,128)S(1)}, s32[1,16,16]{2,1,0:T(8,128)}, u32[]{:S(2)}) copy-start(s32[1,16,16]{2,1,0:T(8,128)} %param.8) | copy-start | bytes 3076
  7.6 25.6 %all-to-all-start = ((bf16[16,64,512]{2,1,0:T(8,128)(2,1)}), bf16[16,64,512]{2,1,0:T(8,128)(2,1)S(1)}, u32[]{:S(2)}, u32[]{:S(2)}) async-start(bf16[16,64,512]{2,1,0:T(8,128)(2,1)} %bitcast.2), calls=%async_computation | async-start | bytes 2097152 | tf_op jit(solution)/shard_map/all_to_all | solution.py:128
  33.3 2.0 copy-start.9
  35.2 0.8 copy-start.3
  35.7 31.0 %copy-start.5 = (bf16[512,512]{1,0:T(8,128)(2,1)}, bf16[512,512]{1,0:T(8,128)(2,1)S(1)}, u32[]{:S(2)}) copy-start(bf16[512,512]{1,0:T(8,128)(2,1)S(1)} %convolution_convert_fusion.1) | copy-start | bytes 1572868
  68.1 3.7 copy-start.16
  68.1 28.5 %all-to-all-start.1 = ((bf16[8,512,256]{2,1,0:T(8,128)(2,1)}), bf16[8,512,256]{2,1,0:T(8,128)(2,1)S(1)}, u32[]{:S(2)}, u32[]{:S(2)}) async-start(bf16[8,512,256]{2,1,0:T(8,128)(2,1)} %broadcast_in_dim.36), calls=%async_computation.1 | async-start | bytes 4194304 | tf_op jit(solution)/shard_map/all_to_all | solution.py:101
  96.6 1.4 copy-start.2
  98.0 25.7 %all-to-all-start.5 = ((bf16[2,4096,256]{2,1,0:T(8,128)(2,1)}), bf16[2,4096,256]{2,1,0:T(8,128)(2,1)}, u32[]{:S(2)}, u32[]{:S(2)}) async-start(bf16[2,4096,256]{2,1,0:T(8,128)(2,1)} %bitcast.53), calls=%async_computation.5 | async-start | bytes 8388608 | tf_op jit(solution)/shard_map/all_to_all | solution.py:106
  123.7 10.6 %all-to-all-start.2 = ((bf16[2,4096,256]{2,1,0:T(8,128)(2,1)}), bf16[2,4096,256]{2,1,0:T(8,128)(2,1)}, u32[]{:S(2)}, u32[]{:S(2)}) async-start(bf16[2,4096,256]{2,1,0:T(8,128)(2,1)} %bitcast.54), calls=%async_computation.2 | async-start | bytes 8388608 | tf_op jit(solution)/shard_map/all_to_all | solution.py:106
  134.3 30.9 %all-to-all-start.6 = ((bf16[8,512,256]{2,1,0:T(8,128)(2,1)}), bf16[8,512,256]{2,1,0:T(8,128)(2,1)S(1)}, u32[]{:S(2)}, u32[]{:S(2)}) async-start(bf16[8,512,256]{2,1,0:T(8,128)(2,1)} %bitcast.14), calls=%async_computation.6 | async-start | bytes 4194304 | tf_op jit(solution)/shard_map/all_to_all | solution.py:106
  165.2 5.3 %copy-start.17 = (f32[512]{0:T(512)S(1)}, f32[512]{0:T(512)}, u32[]{:S(2)}) copy-start(f32[512]{0:T(512)} %param.10) | copy-start | bytes 6148
  165.2 31.6 %all-to-all-start.3 = ((bf16[8,512,256]{2,1,0:T(8,128)(2,1)}), bf16[8,512,256]{2,1,0:T(8,128)(2,1)}, u32[]{:S(2)}, u32[]{:S(2)}) async-start(bf16[8,512,256]{2,1,0:T(8,128)(2,1)} %bitcast.11), calls=%async_computation.3 | async-start | bytes 4194304 | tf_op jit(solution)/shard_map/all_to_all | solution.py:106
  170.8 27.9 %copy-start.8 = (bf16[512,512]{1,0:T(8,128)(2,1)S(1)}, bf16[512,512]{1,0:T(8,128)(2,1)}, u32[]{:S(2)}) copy-start(bf16[512,512]{1,0:T(8,128)(2,1)} %param.13) | copy-start | bytes 1572868
  244.0 29.7 %all-to-all-start.10 = ((bf16[8,512,256]{2,1,0:T(8,128)(2,1)}), bf16[8,512,256]{2,1,0:T(8,128)(2,1)S(1)}, u32[]{:S(2)}, u32[]{:S(2)}) async-start(bf16[8,512,256]{2,1,0:T(8,128)(2,1)} %broadcast_in_dim.41), calls=%async_computation.10 | async-start | bytes 4194304 | tf_op jit(solution)/shard_map/all_to_all | solution.py:101
  283.0 30.3 %all-to-all-start.9 = ((bf16[8,512,256]{2,1,0:T(8,128)(2,1)}), bf16[8,512,256]{2,1,0:T(8,128)(2,1)S(1)}, u32[]{:S(2)}, u32[]{:S(2)}) async-start(bf16[8,512,256]{2,1,0:T(8,128)(2,1)} %bitcast.17), calls=%async_computation.9 | async-start | bytes 4194304 | tf_op jit(solution)/shard_map/all_to_all | solution.py:106
  313.2 30.2 %all-to-all-start.12 = ((bf16[8,512,256]{2,1,0:T(8,128)(2,1)}), bf16[8,512,256]{2,1,0:T(8,128)(2,1)}, u32[]{:S(2)}, u32[]{:S(2)}) async-start(bf16[8,512,256]{2,1,0:T(8,128)(2,1)} %bitcast.57), calls=%async_computation.12 | async-start | bytes 4194304 | tf_op jit(solution)/shard_map/all_to_all | solution.py:106
  317.7 27.7 %copy-start.4 = (bf16[512,512]{1,0:T(8,128)(2,1)S(1)}, bf16[512,512]{1,0:T(8,128)(2,1)}, u32[]{:S(2)}) copy-start(bf16[512,512]{1,0:T(8,128)(2,1)} %copy-done.3) | copy-start | bytes 1572868
  318.1 27.8 %copy-start.11 = (bf16[512,256]{1,0:T(8,128)(2,1)}, bf16[512,256]{1,0:T(8,128)(2,1)S(1)}, u32[]{:S(2)}) copy-start(bf16[512,256]{1,0:T(8,128)(2,1)S(1)} %reduce_sum.120) | copy-start | bytes 786436
  345.4 0.7 copy-start.13
  385.1 5.9 %copy-start.6 = (bf16[512,256]{1,0:T(8,128)(2,1)S(1)}, bf16[512,256]{1,0:T(8,128)(2,1)}, u32[]{:S(2)}) copy-start(bf16[512,256]{1,0:T(8,128)(2,1)} %get-tuple-element.9) | copy-start | bytes 786436
  385.1 5.9 %copy-start.7 = (bf16[512,256]{1,0:T(8,128)(2,1)S(1)}, bf16[512,256]{1,0:T(8,128)(2,1)}, u32[]{:S(2)}) copy-start(bf16[512,256]{1,0:T(8,128)(2,1)} %get-tuple-element.11) | copy-start | bytes 786436
  385.1 6.7 %copy-start.10 = (bf16[512,512]{1,0:T(8,128)(2,1)S(1)}, bf16[512,512]{1,0:T(8,128)(2,1)}, u32[]{:S(2)}) copy-start(bf16[512,512]{1,0:T(8,128)(2,1)} %param.9) | copy-start | bytes 1572868
  385.1 6.7 %copy-start.12 = (bf16[512,256]{1,0:T(8,128)(2,1)S(1)}, bf16[512,256]{1,0:T(8,128)(2,1)}, u32[]{:S(2)}) copy-start(bf16[512,256]{1,0:T(8,128)(2,1)} %copy-done.11) | copy-start | bytes 786436
  385.1 6.7 %copy-start.14 = (bf16[512,256]{1,0:T(8,128)(2,1)S(1)}, bf16[512,256]{1,0:T(8,128)(2,1)}, u32[]{:S(2)}) copy-start(bf16[512,256]{1,0:T(8,128)(2,1)} %copy-done.13) | copy-start | bytes 786436
  386.1 24.0 %all-to-all-start.14 = ((bf16[128,5,512]{2,1,0:T(8,128)(2,1)}), bf16[128,5,512]{2,1,0:T(8,128)(2,1)S(1)}, u32[]{:S(2)}, u32[]{:S(2)}) async-start(bf16[128,5,512]{2,1,0:T(8,128)(2,1)} %broadcast_in_dim.46), calls=%async_computation.14 | async-start | bytes 2097152 | tf_op jit(solution)/shard_map/all_to_all | solution.py:101
  391.8 20.3 %copy-start.1 = (bf16[1024,512]{1,0:T(8,128)(2,1)S(1)}, bf16[1024,512]{1,0:T(8,128)(2,1)}, u32[]{:S(2)}) copy-start(bf16[1024,512]{1,0:T(8,128)(2,1)} %param.7) | copy-start | bytes 3145732

commit v7 on v6

--- a/solution.py
+++ b/solution.py
@@ -123,8 +123,10 @@
     root_count = math.sqrt(dev_rows * lax.axis_size("blk") * rep_size)
     sent_counts = lax.dynamic_index_in_dim(counts, own_index, 0, keepdims=False)
     first_rows = jnp.cumsum(sent_counts) - sent_counts
-    slot_rows = first_rows[:, None] + jnp.arange(capacity, dtype=jnp.int32)[None, :]
-    outgoing = raw_features[jnp.minimum(slot_rows, raw_rows - 1)]
+    window_starts = jnp.minimum(first_rows, raw_rows - capacity)
+    outgoing = jax.vmap(lambda start: lax.dynamic_slice_in_dim(raw_features, start, capacity))(
+        window_starts
+    )
     incoming = lax.all_to_all(outgoing, ("rh", "core"), split_axis=0, concat_axis=0, tiled=True)
     block_tiles = dev_rows // tile_size
     block_of = tile_lists // block_tiles
@@ -139,7 +141,10 @@
     positions = jnp.arange(dev_rows, dtype=jnp.int32)
     sources = jnp.sum((inclusive[None, :] <= positions[:, None]).astype(jnp.int32), axis=1)
     selector = sources[:, None] == jnp.arange(rep_size, dtype=jnp.int32)[None, :]
-    offsets = jnp.sum(jnp.where(selector, exclusive[None, :], 0), axis=1)
+    plan_starts = jnp.cumsum(counts, axis=1) - counts
+    window_shift = plan_starts - jnp.minimum(plan_starts, raw_rows - capacity)
+    recv_shift = lax.dynamic_index_in_dim(window_shift, own_index, 1, keepdims=False)
+    offsets = jnp.sum(jnp.where(selector, exclusive[None, :] - recv_shift[None, :], 0), axis=1)
     features = incoming.reshape(rep_size * capacity, feature_width)[
         sources * capacity + positions - offsets
     ]

time: 415 us -> 435 us (1.048)
  local copies, waits for them, and re-layouts: 16.6 us -> 37.4 us
    gather x1 -> x32, local copies, waits for them, and re-layouts: 5.08 us -> 25.3 us  [per_device(): outgoing = raw_features[jnp.minimum(slot_rows, raw_rows - 1)]]
  transfers between devices with their start and end apart: 10 -> 10, of which waited for: 8 -> 8; matrix products, arithmetic and copies ran while one was open for 3% -> 4% of each run, Pallas kernels for 16% -> 16%
where the time goes in v7:
time: 435 us; the launch traced here: 432 us
  waiting for transfers between devices  131 us (30%)
  blocking collectives  119 us (27%)
  Pallas kernels  67 us (15%)
  starting transfers between devices  53.1 us (12%)
  local copies, waits for them, and re-layouts  37.4 us (9%)
  other arithmetic  21.3 us (5%)
    all_to_all x4, blocking collectives, gather_by_exchange(): return lax.all_to_all(stacked, axis, 0, 0, tiled=True)  81.7 us
    all_to_all x6, waiting for transfers between devices, reduce_by_exchange(): received = lax.all_to_all(chunks, axis, 0, 0, tiled=True)  81.3 us
    all_to_all x1, blocking collectives, reduce_by_exchange(): received = lax.all_to_all(chunks, axis, 0, 0, tiled=True)  37.1 us
    pallas_call x2, Pallas kernels, forward_spmm(): pl.pallas_call(_forward_kernel, grid_spec=grid_spec, out_shape=jax.ShapeD...  33.9 us
    all_to_all x3, waiting for transfers between devices, gather_by_exchange(): return lax.all_to_all(stacked, axis, 0, 0, tiled=True)  33.8 us
    pallas_call x2, Pallas kernels, backward_spmm(): pl.pallas_call(_backward_kernel, grid_spec=grid_spec, out_shape=jax.Shape...  33.1 us
    all_to_all x6, starting transfers between devices, reduce_by_exchange(): received = lax.all_to_all(chunks, axis, 0, 0, tiled=True)  32.5 us
    gather x32, local copies, waits for them, and re-layouts  25.3 us
  transfers between devices with their start and end apart: 10, of which 8 were waited for; matrix products, arithmetic and copies ran while one was open for 4% of the time, Pallas kernels for 16%

profile of v7, /device:TPU:1, one launch (start us, length us, event | category | flops | bytes accessed | tf_op | source)
XLA Modules:
  0.0 432.0 jit_solution(3586607616111676134)
XLA Ops:
  1.6 25.3 %while.1 = (s32[]{:T(128)}, bf16[1024,512]{1,0:T(8,128)(2,1)}, s32[16,2]{1,0:T(8,128)S(1)}, bf16[16,64,512]{2,1,0:T(8,128)(2,1)}, s32[]{:T(128)}) while((s32[]{:T(128)}, bf16[1024,512]{1,0:T(8,128)(2,1)}, s32[16,2]{1,0:T(8,128)S(1)}, bf16[16,64,512]{2,1,0:T(8,128)(2,1)}, s32[]{:T(128)}) %tuple.33), condition=%wide.while_cond, body=%wide.while_body.sunk | while | flops 2 | bytes 131669 | solution.py:127
  26.9 8.5 %all-to-all-start = ((bf16[16,64,512]{2,1,0:T(8,128)(2,1)}), bf16[16,64,512]{2,1,0:T(8,128)(2,1)S(1)}, u32[]{:S(2)}, u32[]{:S(2)}) async-start(bf16[16,64,512]{2,1,0:T(8,128)(2,1)} %get-tuple-element.12), calls=%async_computation | async-start | bytes 2097152 | tf_op jit(solution)/shard_map/all_to_all | solution.py:130
  36.3 16.2 %all-to-all-done = bf16[16,64,512]{2,1,0:T(8,128)(2,1)S(1)} async-done(((bf16[16,64,512]{2,1,0:T(8,128)(2,1)}), bf16[16,64,512]{2,1,0:T(8,128)(2,1)S(1)}, u32[]{:S(2)}, u32[]{:S(2)}) %all-to-all-start) | async-done | bytes 1048608 | tf_op jit(solution)/shard_map/all_to_all | solution.py:130
  52.4 2.0 gather_fusion
  55.8 30.6 %all_to_all.75 = bf16[8,512,256]{2,1,0:T(8,128)(2,1)} all-to-all(bf16[8,512,256]{2,1,0:T(8,128)(2,1)S(1)} %broadcast_in_dim.40), channel_id=1, replica_groups=mesh['blk'=8,'rh'=8,'core'=2] {'blk'}, dimensions={0} | all-to-all | bytes 4194304 | tf_op jit(solution)/shard_map/all_to_all | solution.py:101
  87.9 3.7 all-to-all-start.1
  92.4 16.9 %shard_map.111 = bf16[32,256,256]{2,1,0:T(8,128)(2,1)} custom-call(s32[16,6]{1,0:T(8,128)} %fusion.4.rows_ref, bf16[16,6,256,256]{3,2,1,0:T(8,128)(2,1)} %bitcast.56, bf16[4096,256]{1,0:T(8,128)(2,1)} %bitcast.67), custom_call_target="tpu_custom_call" | custom-call | tf_op jit(solution)/shard_map/pallas_call | solution.py:49
  109.3 7.1 %all-to-all-done.1 = bf16[8,512,256]{2,1,0:T(8,128)(2,1)S(1)} async-done(((bf16[8,512,256]{2,1,0:T(8,128)(2,1)}), bf16[8,512,256]{2,1,0:T(8,128)(2,1)S(1)}, u32[]{:S(2)}, u32[]{:S(2)}) %all-to-all-start.1) | async-done | bytes 2097184 | tf_op jit(solution)/shard_map/all_to_all | solution.py:101
  117.8 8.7 %all-to-all-start.5 = ((bf16[2,4096,256]{2,1,0:T(8,128)(2,1)}), bf16[2,4096,256]{2,1,0:T(8,128)(2,1)}, u32[]{:S(2)}, u32[]{:S(2)}) async-start(bf16[2,4096,256]{2,1,0:T(8,128)(2,1)} %bitcast.61), calls=%async_computation.5 | async-start | bytes 8388608 | tf_op jit(solution)/shard_map/all_to_all | solution.py:106
  126.5 17.0 %shard_map.110 = bf16[32,256,256]{2,1,0:T(8,128)(2,1)} custom-call(s32[16,6]{1,0:T(8,128)} %fusion.4.rows_ref, bf16[16,6,256,256]{3,2,1,0:T(8,128)(2,1)} %bitcast.57, bf16[4096,256]{1,0:T(8,128)(2,1)} %bitcast.66), custom_call_target="tpu_custom_call" | custom-call | tf_op jit(solution)/shard_map/pallas_call | solution.py:49
  143.5 5.6 %all-to-all-start.2 = ((bf16[2,4096,256]{2,1,0:T(8,128)(2,1)}), bf16[2,4096,256]{2,1,0:T(8,128)(2,1)}, u32[]{:S(2)}, u32[]{:S(2)}) async-start(bf16[2,4096,256]{2,1,0:T(8,128)(2,1)} %bitcast.62), calls=%async_computation.2 | async-start | bytes 8388608 | tf_op jit(solution)/shard_map/all_to_all | solution.py:106
  149.1 4.9 %reduce_sum.118 = bf16[4096,256]{1,0:T(8,128)(2,1)} reduce(bf16[2,4096,256]{2,1,0:T(8,128)(2,1)} %all-to-all-done.5, bf16[]{:T(256)} %constant.94.clone.1), dimensions={0}, to_apply=%region_7.8 | reduce | flops 1048576 | bytes 6291458 | tf_op jit(solution)/shard_map/reduce_sum | solution.py:107
  154.0 4.7 %all-to-all-start.6 = ((bf16[8,512,256]{2,1,0:T(8,128)(2,1)}), bf16[8,512,256]{2,1,0:T(8,128)(2,1)S(1)}, u32[]{:S(2)}, u32[]{:S(2)}) async-start(bf16[8,512,256]{2,1,0:T(8,128)(2,1)} %bitcast.13), calls=%async_computation.6 | async-start | bytes 4194304 | tf_op jit(solution)/shard_map/all_to_all | solution.py:106
  158.7 4.9 %reduce_sum.116 = bf16[4096,256]{1,0:T(8,128)(2,1)} reduce(bf16[2,4096,256]{2,1,0:T(8,128)(2,1)} %all-to-all-done.2, bf16[]{:T(256)} %constant.94.clone.1), dimensions={0}, to_apply=%region_5.6 | reduce | flops 1048576 | bytes 6291458 | tf_op jit(solution)/shard_map/reduce_sum | solution.py:107
  163.7 21.3 %all-to-all-done.6 = bf16[8,512,256]{2,1,0:T(8,128)(2,1)S(1)} async-done(((bf16[8,512,256]{2,1,0:T(8,128)(2,1)}), bf16[8,512,256]{2,1,0:T(8,128)(2,1)S(1)}, u32[]{:S(2)}, u32[]{:S(2)}) %all-to-all-start.6) | async-done | bytes 2097184 | tf_op jit(solution)/shard_map/all_to_all | solution.py:106
  184.9 5.3 %all-to-all-start.3 = ((bf16[8,512,256]{2,1,0:T(8,128)(2,1)}), bf16[8,512,256]{2,1,0:T(8,128)(2,1)}, u32[]{:S(2)}, u32[]{:S(2)}) async-start(bf16[8,512,256]{2,1,0:T(8,128)(2,1)} %bitcast.10), calls=%async_computation.3 | async-start | bytes 4194304 | tf_op jit(solution)/shard_map/all_to_all | solution.py:106
  191.4 25.2 %all-to-all-done.3 = bf16[8,512,256]{2,1,0:T(8,128)(2,1)} async-done(((bf16[8,512,256]{2,1,0:T(8,128)(2,1)}), bf16[8,512,256]{2,1,0:T(8,128)(2,1)}, u32[]{:S(2)}, u32[]{:S(2)}) %all-to-all-start.3) | async-done | bytes 2097184 | tf_op jit(solution)/shard_map/all_to_all | solution.py:106
  219.9 31.8 %all_to_all.76 = bf16[8,512,256]{2,1,0:T(8,128)(2,1)S(1)} all-to-all(bf16[8,512,256]{2,1,0:T(8,128)(2,1)S(1)} %broadcast_in_dim.41), channel_id=1, replica_groups=mesh['blk'=8,'rh'=8,'core'=2] {'rh'}, dimensions={0} | all-to-all | bytes 4194304 | tf_op jit(solution)/shard_map/all_to_all | solution.py:101
  252.0 10.2 %all_to_all.77 = bf16[2,4096,256]{2,1,0:T(8,128)(2,1)} all-to-all(bf16[2,4096,256]{2,1,0:T(8,128)(2,1)S(1)} %broadcast_in_dim.43), channel_id=1, replica_groups=mesh['blk'=8,'rh'=8,'core'=2] {'core'}, dimensions={0} | all-to-all | bytes 8388608 | tf_op jit(solution)/shard_map/all_to_all | solution.py:101
  263.7 3.6 all-to-all-start.10
  267.3 16.5 %shard_map.112 = bf16[4096,256]{1,0:T(8,128)(2,1)} custom-call(s32[16,6]{1,0:T(8,128)} %fusion.4.rows_ref, bf16[16,6,256,256]{3,2,1,0:T(8,128)(2,1)} %bitcast.58, bf16[32,256,256]{2,1,0:T(8,128)(2,1)} %bitcast.63), custom_call_target="tpu_custom_call" | custom-call | tf_op jit(solution)/shard_map/pallas_call | solution.py:88
  283.8 9.6 %all-to-all-done.10 = bf16[8,512,256]{2,1,0:T(8,128)(2,1)S(1)} async-done(((bf16[8,512,256]{2,1,0:T(8,128)(2,1)}), bf16[8,512,256]{2,1,0:T(8,128)(2,1)S(1)}, u32[]{:S(2)}, u32[]{:S(2)}) %all-to-all-start.10) | async-done | bytes 2097184 | tf_op jit(solution)/shard_map/all_to_all | solution.py:101
  293.7 9.0 %all_to_all.78 = bf16[2,4096,256]{2,1,0:T(8,128)(2,1)} all-to-all(bf16[2,4096,256]{2,1,0:T(8,128)(2,1)S(1)} %broadcast_in_dim.84), channel_id=1, replica_groups=mesh['blk'=8,'rh'=8,'core'=2] {'core'}, dimensions={0} | all-to-all | bytes 8388608 | tf_op jit(solution)/shard_map/all_to_all | solution.py:101
  302.7 3.8 all-to-all-start.9
  306.5 16.6 %shard_map.113 = bf16[4096,256]{1,0:T(8,128)(2,1)} custom-call(s32[16,6]{1,0:T(8,128)} %fusion.4.rows_ref, bf16[16,6,256,256]{3,2,1,0:T(8,128)(2,1)} %bitcast.59, bf16[32,256,256]{2,1,0:T(8,128)(2,1)} %bitcast.64), custom_call_target="tpu_custom_call" | custom-call | tf_op jit(solution)/shard_map/pallas_call | solution.py:88
  323.0 10.1 %all-to-all-done.9 = bf16[8,512,256]{2,1,0:T(8,128)(2,1)S(1)} async-done(((bf16[8,512,256]{2,1,0:T(8,128)(2,1)}), bf16[8,512,256]{2,1,0:T(8,128)(2,1)S(1)}, u32[]{:S(2)}, u32[]{:S(2)}) %all-to-all-start.9) | async-done | bytes 2097184 | tf_op jit(solution)/shard_map/all_to_all | solution.py:106
  333.1 4.3 %all-to-all-start.12 = ((bf16[8,512,256]{2,1,0:T(8,128)(2,1)}), bf16[8,512,256]{2,1,0:T(8,128)(2,1)}, u32[]{:S(2)}, u32[]{:S(2)}) async-start(bf16[8,512,256]{2,1,0:T(8,128)(2,1)} %bitcast.65), calls=%async_computation.12 | async-start | bytes 4194304 | tf_op jit(solution)/shard_map/all_to_all | solution.py:106
  338.6 24.7 %all-to-all-done.12 = bf16[8,512,256]{2,1,0:T(8,128)(2,1)} async-done(((bf16[8,512,256]{2,1,0:T(8,128)(2,1)}), bf16[8,512,256]{2,1,0:T(8,128)(2,1)}, u32[]{:S(2)}, u32[]{:S(2)}) %all-to-all-start.12) | async-done | bytes 2097184 | tf_op jit(solution)/shard_map/all_to_all | solution.py:106
  363.3 2.0 reduce_sum.121
  367.7 37.1 %all_to_all.79 = f32[128,5,512]{2,1,0:T(8,128)S(1)} all-to-all(f32[128,5,512]{2,1,0:T(8,128)} %reshape.171), channel_id=1, replica_groups=mesh['blk'=8,'rh'=8,'core'=2] {'blk','rh','core'}, dimensions={0} | all-to-all | bytes 2621440 | tf_op jit(solution)/shard_map/all_to_all | solution.py:106
  406.1 4.8 %all-to-all-start.14 = ((bf16[128,5,512]{2,1,0:T(8,128)(2,1)}), bf16[128,5,512]{2,1,0:T(8,128)(2,1)S(1)}, u32[]{:S(2)}, u32[]{:S(2)}) async-start(bf16[128,5,512]{2,1,0:T(8,128)(2,1)} %broadcast_in_dim.87), calls=%async_computation.14 | async-start | bytes 2097152 | tf_op jit(solution)/shard_map/all_to_all | solution.py:101
  413.0 17.1 %all-to-all-done.14 = bf16[128,5,512]{2,1,0:T(8,128)(2,1)S(1)} async-done(((bf16[128,5,512]{2,1,0:T(8,128)(2,1)}), bf16[128,5,512]{2,1,0:T(8,128)(2,1)S(1)}, u32[]{:S(2)}, u32[]{:S(2)}) %all-to-all-start.14) | async-done | bytes 655392 | tf_op jit(solution)/shard_map/all_to_all | solution.py:101
  (105 shorter events, 47.1 us)
Async XLA Ops:
  0.6 53.8 %copy-start = (bf16[512,512]{1,0:T(8,128)(2,1)S(1)}, bf16[512,512]{1,0:T(8,128)(2,1)}, u32[]{:S(2)}) copy-start(bf16[512,512]{1,0:T(8,128)(2,1)} %param.9) | copy-start | bytes 1572868
  0.6 34.7 %copy-start.10 = (s32[1,16,16]{2,1,0:T(8,128)S(1)}, s32[1,16,16]{2,1,0:T(8,128)}, u32[]{:S(2)}) copy-start(s32[1,16,16]{2,1,0:T(8,128)} %param.8) | copy-start | bytes 3076
  26.9 25.6 %all-to-all-start = ((bf16[16,64,512]{2,1,0:T(8,128)(2,1)}), bf16[16,64,512]{2,1,0:T(8,128)(2,1)S(1)}, u32[]{:S(2)}, u32[]{:S(2)}) async-start(bf16[16,64,512]{2,1,0:T(8,128)(2,1)} %get-tuple-element.12), calls=%async_computation | async-start | bytes 2097152 | tf_op jit(solution)/shard_map/all_to_all | solution.py:130
  54.9 0.8 copy-start.3
  87.9 3.7 copy-start.11
  87.9 28.5 %all-to-all-start.1 = ((bf16[8,512,256]{2,1,0:T(8,128)(2,1)}), bf16[8,512,256]{2,1,0:T(8,128)(2,1)S(1)}, u32[]{:S(2)}, u32[]{:S(2)}) async-start(bf16[8,512,256]{2,1,0:T(8,128)(2,1)} %broadcast_in_dim.39), calls=%async_computation.1 | async-start | bytes 4194304 | tf_op jit(solution)/shard_map/all_to_all | solution.py:101
  116.4 1.4 copy-start.1
  117.8 25.7 %all-to-all-start.5 = ((bf16[2,4096,256]{2,1,0:T(8,128)(2,1)}), bf16[2,4096,256]{2,1,0:T(8,128)(2,1)}, u32[]{:S(2)}, u32[]{:S(2)}) async-start(bf16[2,4096,256]{2,1,0:T(8,128)(2,1)} %bitcast.61), calls=%async_computation.5 | async-start | bytes 8388608 | tf_op jit(solution)/shard_map/all_to_all | solution.py:106
  143.5 10.6 %all-to-all-start.2 = ((bf16[2,4096,256]{2,1,0:T(8,128)(2,1)}), bf16[2,4096,256]{2,1,0:T(8,128)(2,1)}, u32[]{:S(2)}, u32[]{:S(2)}) async-start(bf16[2,4096,256]{2,1,0:T(8,128)(2,1)} %bitcast.62), calls=%async_computation.2 | async-start | bytes 8388608 | tf_op jit(solution)/shard_map/all_to_all | solution.py:106
  154.0 30.9 %all-to-all-start.6 = ((bf16[8,512,256]{2,1,0:T(8,128)(2,1)}), bf16[8,512,256]{2,1,0:T(8,128)(2,1)S(1)}, u32[]{:S(2)}, u32[]{:S(2)}) async-start(bf16[8,512,256]{2,1,0:T(8,128)(2,1)} %bitcast.13), calls=%async_computation.6 | async-start | bytes 4194304 | tf_op jit(solution)/shard_map/all_to_all | solution.py:106
  184.9 5.3 %copy-start.12 = (f32[512]{0:T(512)S(1)}, f32[512]{0:T(512)}, u32[]{:S(2)}) copy-start(f32[512]{0:T(512)} %param.10) | copy-start | bytes 6148
  184.9 31.6 %all-to-all-start.3 = ((bf16[8,512,256]{2,1,0:T(8,128)(2,1)}), bf16[8,512,256]{2,1,0:T(8,128)(2,1)}, u32[]{:S(2)}, u32[]{:S(2)}) async-start(bf16[8,512,256]{2,1,0:T(8,128)(2,1)} %bitcast.10), calls=%async_computation.3 | async-start | bytes 4194304 | tf_op jit(solution)/shard_map/all_to_all | solution.py:106
  191.4 27.1 %copy-start.2 = (f32[512,256]{1,0:T(8,128)S(1)}, f32[512,256]{1,0:T(8,128)}, u32[]{:S(2)}) copy-start(f32[512,256]{1,0:T(8,128)} %convert_reduce_fusion) | copy-start | bytes 1572868
  191.4 27.1 %copy-start.5 = (bf16[512,512]{1,0:T(8,128)(2,1)S(1)}, bf16[512,512]{1,0:T(8,128)(2,1)}, u32[]{:S(2)}) copy-start(bf16[512,512]{1,0:T(8,128)(2,1)} %param.13) | copy-start | bytes 1572868
  263.7 29.7 %all-to-all-start.10 = ((bf16[8,512,256]{2,1,0:T(8,128)(2,1)}), bf16[8,512,256]{2,1,0:T(8,128)(2,1)S(1)}, u32[]{:S(2)}, u32[]{:S(2)}) async-start(bf16[8,512,256]{2,1,0:T(8,128)(2,1)} %broadcast_in_dim.44), calls=%async_computation.10 | async-start | bytes 4194304 | tf_op jit(solution)/shard_map/all_to_all | solution.py:101
  302.7 30.4 %all-to-all-start.9 = ((bf16[8,512,256]{2,1,0:T(8,128)(2,1)}), bf16[8,512,256]{2,1,0:T(8,128)(2,1)S(1)}, u32[]{:S(2)}, u32[]{:S(2)}) async-start(bf16[8,512,256]{2,1,0:T(8,128)(2,1)} %bitcast.16), calls=%async_computation.9 | async-start | bytes 4194304 | tf_op jit(solution)/shard_map/all_to_all | solution.py:106
  333.1 30.2 %all-to-all-start.12 = ((bf16[8,512,256]{2,1,0:T(8,128)(2,1)}), bf16[8,512,256]{2,1,0:T(8,128)(2,1)}, u32[]{:S(2)}, u32[]{:S(2)}) async-start(bf16[8,512,256]{2,1,0:T(8,128)(2,1)} %bitcast.65), calls=%async_computation.12 | async-start | bytes 4194304 | tf_op jit(solution)/shard_map/all_to_all | solution.py:106
  338.6 26.7 %copy-start.6 = (bf16[512,256]{1,0:T(8,128)(2,1)S(1)}, bf16[512,256]{1,0:T(8,128)(2,1)}, u32[]{:S(2)}) copy-start(bf16[512,256]{1,0:T(8,128)(2,1)} %reduce_sum.120) | copy-start | bytes 786436
  365.3 0.7 copy-start.8
  405.1 5.9 %copy-start.4 = (bf16[512,256]{1,0:T(8,128)(2,1)S(1)}, bf16[512,256]{1,0:T(8,128)(2,1)}, u32[]{:S(2)}) copy-start(bf16[512,256]{1,0:T(8,128)(2,1)} %get-tuple-element.39) | copy-start | bytes 786436
  405.1 6.7 %copy-start.7 = (bf16[512,256]{1,0:T(8,128)(2,1)S(1)}, bf16[512,256]{1,0:T(8,128)(2,1)}, u32[]{:S(2)}) copy-start(bf16[512,256]{1,0:T(8,128)(2,1)} %reduce_sum.120) | copy-start | bytes 786436
  405.1 6.7 %copy-start.9 = (bf16[512,256]{1,0:T(8,128)(2,1)S(1)}, bf16[512,256]{1,0:T(8,128)(2,1)}, u32[]{:S(2)}) copy-start(bf16[512,256]{1,0:T(8,128)(2,1)} %copy-done.8) | copy-start | bytes 786436
  406.1 24.0 %all-to-all-start.14 = ((bf16[128,5,512]{2,1,0:T(8,128)(2,1)}), bf16[128,5,512]{2,1,0:T(8,128)(2,1)S(1)}, u32[]{:S(2)}, u32[]{:S(2)}) async-start(bf16[128,5,512]{2,1,0:T(8,128)(2,1)} %broadcast_in_dim.87), calls=%async_computation.14 | async-start | bytes 2097152 | tf_op jit(solution)/shard_map/all_to_all | solution.py:101

commit v8 on v6

--- a/solution.py
+++ b/solution.py
@@ -15,35 +15,55 @@
     return sigma * (1.0 + values * (1.0 - sigma))
 
 
-def _forward_kernel(rows_ref, tiles_ref, cols_ref, out_ref, acc_ref):
+def _forward_kernel(rows_ref, first_ref, touched_ref, tiles_ref, cols_ref, out_ref, acc_ref):
     step = pl.program_id(0)
     fill = tiles_ref.shape[1]
-
-    @pl.when(step == 0)
-    def _():
-        acc_ref[...] = jnp.zeros_like(acc_ref)
-
     inputs = cols_ref[...]
     for j in range(fill):
         target = rows_ref[step, j]
-        acc_ref[target] += jnp.dot(tiles_ref[0, j], inputs, preferred_element_type=jnp.float32)
+        product = jnp.dot(tiles_ref[0, j], inputs, preferred_element_type=jnp.float32)
+
+        @pl.when(first_ref[step, j] == 1)
+        def _():
+            acc_ref[target] = product
+
+        @pl.when(first_ref[step, j] == 0)
+        def _():
+            acc_ref[target] += product
 
     @pl.when(step == pl.num_programs(0) - 1)
     def _():
-        out_ref[...] = acc_ref[...].astype(out_ref.dtype)
+        for tile in range(acc_ref.shape[0]):
+
+            @pl.when(touched_ref[tile] == 1)
+            def _():
+                out_ref[tile] = acc_ref[tile].astype(out_ref.dtype)
+
+            @pl.when(touched_ref[tile] == 0)
+            def _():
+                out_ref[tile] = jnp.zeros(out_ref.shape[1:], out_ref.dtype)
 
 
 def forward_spmm(row_lists, tile_stack, shard_rows, row_tiles, interpret=False):
     col_tiles, fill, tile_size, _ = tile_stack.shape
     width = shard_rows.shape[1]
+    flat = row_lists.reshape(-1)
+    order = jnp.arange(flat.shape[0], dtype=jnp.int32)
+    same = flat[:, None] == flat[None, :]
+    earlier = order[None, :] < order[:, None]
+    first_flags = (~jnp.any(same & earlier, axis=1)).astype(jnp.int32).reshape(row_lists.shape)
+    tiles = jnp.arange(row_tiles, dtype=jnp.int32)
+    touched = jnp.any(flat[None, :] == tiles[:, None], axis=1).astype(jnp.int32)
     grid_spec = pltpu.PrefetchScalarGridSpec(
-        num_scalar_prefetch=1,
+        num_scalar_prefetch=3,
         grid=(col_tiles,),
         in_specs=[
-            pl.BlockSpec((1, fill, tile_size, tile_size), lambda c, rows: (c, 0, 0, 0)),
-            pl.BlockSpec((tile_size, width), lambda c, rows: (c, 0)),
+            pl.BlockSpec((1, fill, tile_size, tile_size), lambda c, rows, first, hit: (c, 0, 0, 0)),
+            pl.BlockSpec((tile_size, width), lambda c, rows, first, hit: (c, 0)),
         ],
-        out_specs=pl.BlockSpec((row_tiles, tile_size, width), lambda c, rows: (0, 0, 0)),
+        out_specs=pl.BlockSpec(
+            (row_tiles, tile_size, width), lambda c, rows, first, hit: (0, 0, 0)
+        ),
         scratch_shapes=[pltpu.VMEM((row_tiles, tile_size, width), jnp.float32)],
     )
     return pl.pallas_call(
@@ -54,7 +74,7 @@
             dimension_semantics=("arbitrary",), vmem_limit_bytes=56 * 1024 * 1024
         ),
         interpret=interpret,
-    )(row_lists, tile_stack, shard_rows)
+    )(row_lists, first_flags, touched, tile_stack, shard_rows)
 
 
 def _backward_kernel(rows_ref, tiles_ref, grad_ref, out_ref):

time: 415 us -> 430 us (1.036)
  Pallas kernels: 67 us -> 87.4 us
  waiting for transfers between devices: 133 us -> 125 us
    pallas_call x2, Pallas kernels: 33.9 us -> 54.3 us  [forward_spmm(): pl.pallas_call(_forward_kernel, grid_spec=grid_spec, out_shape=jax.ShapeD...]
    all_to_all x3, waiting for transfers between devices: 33.6 us -> 26.7 us  [gather_by_exchange(): return lax.all_to_all(stacked, axis, 0, 0, tiled=True)]
  transfers between devices with their start and end apart: 10 -> 10, of which waited for: 8 -> 7; matrix products, arithmetic and copies ran while one was open for 3% -> 4% of each run, Pallas kernels for 16% -> 20%
where the time goes in v8:
time: 430 us; the launch traced here: 427 us
  waiting for transfers between devices  125 us (29%)
  blocking collectives  120 us (28%)
  Pallas kernels  87.4 us (20%)
  starting transfers between devices  53.1 us (12%)
  other arithmetic  21.3 us (5%)
  local copies, waits for them, and re-layouts  17.4 us (4%)
    all_to_all x6, waiting for transfers between devices, reduce_by_exchange(): received = lax.all_to_all(chunks, axis, 0, 0, tiled=True)  82.2 us
    all_to_all x4, blocking collectives, gather_by_exchange(): return lax.all_to_all(stacked, axis, 0, 0, tiled=True)  81.7 us
    pallas_call x2, Pallas kernels, forward_spmm(): pl.pallas_call(_forward_kernel, grid_spec=grid_spec, out_shape=jax.ShapeD...  54.3 us
    all_to_all x1, blocking collectives, reduce_by_exchange(): received = lax.all_to_all(chunks, axis, 0, 0, tiled=True)  38 us
    pallas_call x2, Pallas kernels, backward_spmm(): pl.pallas_call(_backward_kernel, grid_spec=grid_spec, out_shape=jax.Shape...  33.1 us
    all_to_all x6, starting transfers between devices, reduce_by_exchange(): received = lax.all_to_all(chunks, axis, 0, 0, tiled=True)  32.2 us
    all_to_all x3, waiting for transfers between devices, gather_by_exchange(): return lax.all_to_all(stacked, axis, 0, 0, tiled=True)  26.7 us
    all_to_all x1, waiting for transfers between devices, per_device(): lax.all_to_all(outgoing, ('rh', 'core'), split_axis=0, concat_axis=0, til...  16.5 us
  transfers between devices with their start and end apart: 10, of which 7 were waited for; matrix products, arithmetic and copies ran while one was open for 4% of the time, Pallas kernels for 20%

profile of v8, /device:TPU:1, one launch (start us, length us, event | category | flops | bytes accessed | tf_op | source)
XLA Modules:
  0.0 427.4 jit_solution(11209641526624407261)
XLA Ops:
  2.5 5.1 %gather_fusion = bf16[1024,512]{1,0:T(8,128)(2,1)} fusion(bf16[1024,512]{1,0:T(8,128)(2,1)S(1)} %copy-done, s32[1024]{0:T(1024)S(1)} %broadcast_clamp_fusion), kind=kCustom, calls=%fused_computation | custom fusion | bytes 2101248 | tf_op jit(solution)/shard_map/gather | solution.py:147
  7.6 8.6 %all-to-all-start = ((bf16[16,64,512]{2,1,0:T(8,128)(2,1)}), bf16[16,64,512]{2,1,0:T(8,128)(2,1)S(1)}, u32[]{:S(2)}, u32[]{:S(2)}) async-start(bf16[16,64,512]{2,1,0:T(8,128)(2,1)} %bitcast.2), calls=%async_computation | async-start | bytes 2097152 | tf_op jit(solution)/shard_map/all_to_all | solution.py:148
  16.7 16.5 %all-to-all-done = bf16[16,64,512]{2,1,0:T(8,128)(2,1)S(1)} async-done(((bf16[16,64,512]{2,1,0:T(8,128)(2,1)}), bf16[16,64,512]{2,1,0:T(8,128)(2,1)S(1)}, u32[]{:S(2)}, u32[]{:S(2)}) %all-to-all-start) | async-done | bytes 1048608 | tf_op jit(solution)/shard_map/all_to_all | solution.py:148
  33.3 2.0 gather_fusion.1
  36.0 30.6 %all_to_all.75 = bf16[8,512,256]{2,1,0:T(8,128)(2,1)} all-to-all(bf16[8,512,256]{2,1,0:T(8,128)(2,1)S(1)} %broadcast_in_dim.37), channel_id=1, replica_groups=mesh['blk'=8,'rh'=8,'core'=2] {'blk'}, dimensions={0} | all-to-all | bytes 4194304 | tf_op jit(solution)/shard_map/all_to_all | solution.py:121
  68.1 3.7 all-to-all-start.1
  74.2 27.1 %shard_map.111 = bf16[32,256,256]{2,1,0:T(8,128)(2,1)} custom-call(s32[16,6]{1,0:T(8,128)} %fusion.6.rows_ref, s32[16,6]{1,0:T(8,128)} %reshape.371.first_ref, s32[32]{0:T(128)} %convert_element_type.76.touched_ref, bf16[16,6,256,256]{3,2,1,0:T(8,128)(2,1)} %bitcast.50, bf16[4096,256]{1,0:T(8,128)(2,1)} %bitcast.60), custom_call_target="tpu_custom_call" | custom-call | tf_op jit(solution)/shard_map/pallas_call | solution.py:69
  102.7 7.8 %all-to-all-start.5 = ((bf16[2,4096,256]{2,1,0:T(8,128)(2,1)}), bf16[2,4096,256]{2,1,0:T(8,128)(2,1)}, u32[]{:S(2)}, u32[]{:S(2)}) async-start(bf16[2,4096,256]{2,1,0:T(8,128)(2,1)} %bitcast.55), calls=%async_computation.5 | async-start | bytes 8388608 | tf_op jit(solution)/shard_map/all_to_all | solution.py:126
  110.6 27.2 %shard_map.110 = bf16[32,256,256]{2,1,0:T(8,128)(2,1)} custom-call(s32[16,6]{1,0:T(8,128)} %fusion.6.rows_ref, s32[16,6]{1,0:T(8,128)} %reshape.371.first_ref, s32[32]{0:T(128)} %convert_element_type.76.touched_ref, bf16[16,6,256,256]{3,2,1,0:T(8,128)(2,1)} %bitcast.51, bf16[4096,256]{1,0:T(8,128)(2,1)} %bitcast.59), custom_call_target="tpu_custom_call" | custom-call | tf_op jit(solution)/shard_map/pallas_call | solution.py:69
  137.7 5.7 %all-to-all-start.2 = ((bf16[2,4096,256]{2,1,0:T(8,128)(2,1)}), bf16[2,4096,256]{2,1,0:T(8,128)(2,1)}, u32[]{:S(2)}, u32[]{:S(2)}) async-start(bf16[2,4096,256]{2,1,0:T(8,128)(2,1)} %bitcast.56), calls=%async_computation.2 | async-start | bytes 8388608 | tf_op jit(solution)/shard_map/all_to_all | solution.py:126
  143.4 4.9 %reduce_sum.118 = bf16[4096,256]{1,0:T(8,128)(2,1)} reduce(bf16[2,4096,256]{2,1,0:T(8,128)(2,1)} %all-to-all-done.5, bf16[]{:T(256)} %constant.97.clone.1), dimensions={0}, to_apply=%region_8.9 | reduce | flops 1048576 | bytes 6291458 | tf_op jit(solution)/shard_map/reduce_sum | solution.py:127
  148.3 3.7 all-to-all-start.6
  152.0 4.9 %reduce_sum.116 = bf16[4096,256]{1,0:T(8,128)(2,1)} reduce(bf16[2,4096,256]{2,1,0:T(8,128)(2,1)} %all-to-all-done.2, bf16[]{:T(256)} %constant.97.clone.1), dimensions={0}, to_apply=%region_6.7 | reduce | flops 1048576 | bytes 6291458 | tf_op jit(solution)/shard_map/reduce_sum | solution.py:127
  156.9 21.3 %all-to-all-done.6 = bf16[8,512,256]{2,1,0:T(8,128)(2,1)S(1)} async-done(((bf16[8,512,256]{2,1,0:T(8,128)(2,1)}), bf16[8,512,256]{2,1,0:T(8,128)(2,1)S(1)}, u32[]{:S(2)}, u32[]{:S(2)}) %all-to-all-start.6) | async-done | bytes 2097184 | tf_op jit(solution)/shard_map/all_to_all | solution.py:126
  178.2 5.3 %all-to-all-start.3 = ((bf16[8,512,256]{2,1,0:T(8,128)(2,1)}), bf16[8,512,256]{2,1,0:T(8,128)(2,1)}, u32[]{:S(2)}, u32[]{:S(2)}) async-start(bf16[8,512,256]{2,1,0:T(8,128)(2,1)} %bitcast.11), calls=%async_computation.3 | async-start | bytes 4194304 | tf_op jit(solution)/shard_map/all_to_all | solution.py:126
  183.9 26.0 %all-to-all-done.3 = bf16[8,512,256]{2,1,0:T(8,128)(2,1)} async-done(((bf16[8,512,256]{2,1,0:T(8,128)(2,1)}), bf16[8,512,256]{2,1,0:T(8,128)(2,1)}, u32[]{:S(2)}, u32[]{:S(2)}) %all-to-all-start.3) | async-done | bytes 2097184 | tf_op jit(solution)/shard_map/all_to_all | solution.py:126
  209.9 1.9 convert_reduce_fusion.1
  213.2 31.8 %all_to_all.76 = bf16[8,512,256]{2,1,0:T(8,128)(2,1)S(1)} all-to-all(bf16[8,512,256]{2,1,0:T(8,128)(2,1)S(1)} %broadcast_in_dim.38), channel_id=1, replica_groups=mesh['blk'=8,'rh'=8,'core'=2] {'rh'}, dimensions={0} | all-to-all | bytes 4194304 | tf_op jit(solution)/shard_map/all_to_all | solution.py:121
  245.3 10.2 %all_to_all.77 = bf16[2,4096,256]{2,1,0:T(8,128)(2,1)} all-to-all(bf16[2,4096,256]{2,1,0:T(8,128)(2,1)S(1)} %broadcast_in_dim.40), channel_id=1, replica_groups=mesh['blk'=8,'rh'=8,'core'=2] {'core'}, dimensions={0} | all-to-all | bytes 8388608 | tf_op jit(solution)/shard_map/all_to_all | solution.py:121
  257.1 3.8 all-to-all-start.10
  260.9 16.5 %shard_map.112 = bf16[4096,256]{1,0:T(8,128)(2,1)} custom-call(s32[16,6]{1,0:T(8,128)} %fusion.6.rows_ref, bf16[16,6,256,256]{3,2,1,0:T(8,128)(2,1)} %bitcast.52, bf16[32,256,256]{2,1,0:T(8,128)(2,1)} %bitcast.57), custom_call_target="tpu_custom_call" | custom-call | tf_op jit(solution)/shard_map/pallas_call | solution.py:108
  277.4 9.6 %all-to-all-done.10 = bf16[8,512,256]{2,1,0:T(8,128)(2,1)S(1)} async-done(((bf16[8,512,256]{2,1,0:T(8,128)(2,1)}), bf16[8,512,256]{2,1,0:T(8,128)(2,1)S(1)}, u32[]{:S(2)}, u32[]{:S(2)}) %all-to-all-start.10) | async-done | bytes 2097184 | tf_op jit(solution)/shard_map/all_to_all | solution.py:121
  287.3 9.0 %all_to_all.78 = bf16[2,4096,256]{2,1,0:T(8,128)(2,1)} all-to-all(bf16[2,4096,256]{2,1,0:T(8,128)(2,1)S(1)} %broadcast_in_dim.43), channel_id=1, replica_groups=mesh['blk'=8,'rh'=8,'core'=2] {'core'}, dimensions={0} | all-to-all | bytes 8388608 | tf_op jit(solution)/shard_map/all_to_all | solution.py:121
  296.2 5.4 %all-to-all-start.9 = ((bf16[8,512,256]{2,1,0:T(8,128)(2,1)}), bf16[8,512,256]{2,1,0:T(8,128)(2,1)S(1)}, u32[]{:S(2)}, u32[]{:S(2)}) async-start(bf16[8,512,256]{2,1,0:T(8,128)(2,1)} %bitcast.17), calls=%async_computation.9 | async-start | bytes 4194304 | tf_op jit(solution)/shard_map/all_to_all | solution.py:126
  301.6 16.6 %shard_map.113 = bf16[4096,256]{1,0:T(8,128)(2,1)} custom-call(s32[16,6]{1,0:T(8,128)} %fusion.6.rows_ref, bf16[16,6,256,256]{3,2,1,0:T(8,128)(2,1)} %bitcast.53, bf16[32,256,256]{2,1,0:T(8,128)(2,1)} %bitcast.58), custom_call_target="tpu_custom_call" | custom-call | tf_op jit(solution)/shard_map/pallas_call | solution.py:108
  318.2 9.9 %all-to-all-done.9 = bf16[8,512,256]{2,1,0:T(8,128)(2,1)S(1)} async-done(((bf16[8,512,256]{2,1,0:T(8,128)(2,1)}), bf16[8,512,256]{2,1,0:T(8,128)(2,1)S(1)}, u32[]{:S(2)}, u32[]{:S(2)}) %all-to-all-start.9) | async-done | bytes 2097184 | tf_op jit(solution)/shard_map/all_to_all | solution.py:126
  328.0 4.3 %all-to-all-start.12 = ((bf16[8,512,256]{2,1,0:T(8,128)(2,1)}), bf16[8,512,256]{2,1,0:T(8,128)(2,1)}, u32[]{:S(2)}, u32[]{:S(2)}) async-start(bf16[8,512,256]{2,1,0:T(8,128)(2,1)} %bitcast.61), calls=%async_computation.12 | async-start | bytes 4194304 | tf_op jit(solution)/shard_map/all_to_all | solution.py:126
  332.9 25.1 %all-to-all-done.12 = bf16[8,512,256]{2,1,0:T(8,128)(2,1)} async-done(((bf16[8,512,256]{2,1,0:T(8,128)(2,1)}), bf16[8,512,256]{2,1,0:T(8,128)(2,1)}, u32[]{:S(2)}, u32[]{:S(2)}) %all-to-all-start.12) | async-done | bytes 2097184 | tf_op jit(solution)/shard_map/all_to_all | solution.py:126
  357.9 2.0 reduce_sum.121
  362.2 38.0 %all_to_all.79 = f32[128,5,512]{2,1,0:T(8,128)S(1)} all-to-all(f32[128,5,512]{2,1,0:T(8,128)} %reshape.370), channel_id=1, replica_groups=mesh['blk'=8,'rh'=8,'core'=2] {'blk','rh','core'}, dimensions={0} | all-to-all | bytes 2621440 | tf_op jit(solution)/shard_map/all_to_all | solution.py:126
  401.5 4.8 %all-to-all-start.14 = ((bf16[128,5,512]{2,1,0:T(8,128)(2,1)}), bf16[128,5,512]{2,1,0:T(8,128)(2,1)S(1)}, u32[]{:S(2)}, u32[]{:S(2)}) async-start(bf16[128,5,512]{2,1,0:T(8,128)(2,1)} %broadcast_in_dim.46), calls=%async_computation.14 | async-start | bytes 2097152 | tf_op jit(solution)/shard_map/all_to_all | solution.py:121
  408.5 17.1 %all-to-all-done.14 = bf16[128,5,512]{2,1,0:T(8,128)(2,1)S(1)} async-done(((bf16[128,5,512]{2,1,0:T(8,128)(2,1)}), bf16[128,5,512]{2,1,0:T(8,128)(2,1)S(1)}, u32[]{:S(2)}, u32[]{:S(2)}) %all-to-all-start.14) | async-done | bytes 655392 | tf_op jit(solution)/shard_map/all_to_all | solution.py:121
  (90 shorter events, 20.1 us)
Async XLA Ops:
  0.6 1.9 copy-start
  7.6 8.6 %copy-start.15 = (s32[1,16,16]{2,1,0:T(8,128)S(1)}, s32[1,16,16]{2,1,0:T(8,128)}, u32[]{:S(2)}) copy-start(s32[1,16,16]{2,1,0:T(8,128)} %param.8) | copy-start | bytes 3076
  7.6 25.6 %all-to-all-start = ((bf16[16,64,512]{2,1,0:T(8,128)(2,1)}), bf16[16,64,512]{2,1,0:T(8,128)(2,1)S(1)}, u32[]{:S(2)}, u32[]{:S(2)}) async-start(bf16[16,64,512]{2,1,0:T(8,128)(2,1)} %bitcast.2), calls=%async_computation | async-start | bytes 2097152 | tf_op jit(solution)/shard_map/all_to_all | solution.py:148
  33.3 2.0 copy-start.9
  35.2 0.8 copy-start.3
  35.7 31.0 %copy-start.5 = (bf16[512,512]{1,0:T(8,128)(2,1)}, bf16[512,512]{1,0:T(8,128)(2,1)S(1)}, u32[]{:S(2)}) copy-start(bf16[512,512]{1,0:T(8,128)(2,1)S(1)} %convolution_convert_fusion.1) | copy-start | bytes 1572868
  68.1 3.7 copy-start.16
  68.1 33.2 %all-to-all-start.1 = ((bf16[8,512,256]{2,1,0:T(8,128)(2,1)}), bf16[8,512,256]{2,1,0:T(8,128)(2,1)S(1)}, u32[]{:S(2)}, u32[]{:S(2)}) async-start(bf16[8,512,256]{2,1,0:T(8,128)(2,1)} %broadcast_in_dim.36), calls=%async_computation.1 | async-start | bytes 4194304 | tf_op jit(solution)/shard_map/all_to_all | solution.py:121
  101.4 1.4 copy-start.2
  102.7 35.0 %all-to-all-start.5 = ((bf16[2,4096,256]{2,1,0:T(8,128)(2,1)}), bf16[2,4096,256]{2,1,0:T(8,128)(2,1)}, u32[]{:S(2)}, u32[]{:S(2)}) async-start(bf16[2,4096,256]{2,1,0:T(8,128)(2,1)} %bitcast.55), calls=%async_computation.5 | async-start | bytes 8388608 | tf_op jit(solution)/shard_map/all_to_all | solution.py:126
  137.7 10.6 %all-to-all-start.2 = ((bf16[2,4096,256]{2,1,0:T(8,128)(2,1)}), bf16[2,4096,256]{2,1,0:T(8,128)(2,1)}, u32[]{:S(2)}, u32[]{:S(2)}) async-start(bf16[2,4096,256]{2,1,0:T(8,128)(2,1)} %bitcast.56), calls=%async_computation.2 | async-start | bytes 8388608 | tf_op jit(solution)/shard_map/all_to_all | solution.py:126
  148.3 29.9 %all-to-all-start.6 = ((bf16[8,512,256]{2,1,0:T(8,128)(2,1)}), bf16[8,512,256]{2,1,0:T(8,128)(2,1)S(1)}, u32[]{:S(2)}, u32[]{:S(2)}) async-start(bf16[8,512,256]{2,1,0:T(8,128)(2,1)} %bitcast.14), calls=%async_computation.6 | async-start | bytes 4194304 | tf_op jit(solution)/shard_map/all_to_all | solution.py:126
  178.2 5.3 %copy-start.17 = (f32[512]{0:T(512)S(1)}, f32[512]{0:T(512)}, u32[]{:S(2)}) copy-start(f32[512]{0:T(512)} %param.10) | copy-start | bytes 6148
  178.2 31.6 %all-to-all-start.3 = ((bf16[8,512,256]{2,1,0:T(8,128)(2,1)}), bf16[8,512,256]{2,1,0:T(8,128)(2,1)}, u32[]{:S(2)}, u32[]{:S(2)}) async-start(bf16[8,512,256]{2,1,0:T(8,128)(2,1)} %bitcast.11), calls=%async_computation.3 | async-start | bytes 4194304 | tf_op jit(solution)/shard_map/all_to_all | solution.py:126
  183.9 27.9 %copy-start.8 = (bf16[512,512]{1,0:T(8,128)(2,1)S(1)}, bf16[512,512]{1,0:T(8,128)(2,1)}, u32[]{:S(2)}) copy-start(bf16[512,512]{1,0:T(8,128)(2,1)} %param.13) | copy-start | bytes 1572868
  257.1 29.9 %all-to-all-start.10 = ((bf16[8,512,256]{2,1,0:T(8,128)(2,1)}), bf16[8,512,256]{2,1,0:T(8,128)(2,1)S(1)}, u32[]{:S(2)}, u32[]{:S(2)}) async-start(bf16[8,512,256]{2,1,0:T(8,128)(2,1)} %broadcast_in_dim.41), calls=%async_computation.10 | async-start | bytes 4194304 | tf_op jit(solution)/shard_map/all_to_all | solution.py:121
  296.2 31.8 %all-to-all-start.9 = ((bf16[8,512,256]{2,1,0:T(8,128)(2,1)}), bf16[8,512,256]{2,1,0:T(8,128)(2,1)S(1)}, u32[]{:S(2)}, u32[]{:S(2)}) async-start(bf16[8,512,256]{2,1,0:T(8,128)(2,1)} %bitcast.17), calls=%async_computation.9 | async-start | bytes 4194304 | tf_op jit(solution)/shard_map/all_to_all | solution.py:126
  328.0 29.9 %all-to-all-start.12 = ((bf16[8,512,256]{2,1,0:T(8,128)(2,1)}), bf16[8,512,256]{2,1,0:T(8,128)(2,1)}, u32[]{:S(2)}, u32[]{:S(2)}) async-start(bf16[8,512,256]{2,1,0:T(8,128)(2,1)} %bitcast.61), calls=%async_computation.12 | async-start | bytes 4194304 | tf_op jit(solution)/shard_map/all_to_all | solution.py:126
  332.5 27.5 %copy-start.4 = (bf16[512,512]{1,0:T(8,128)(2,1)S(1)}, bf16[512,512]{1,0:T(8,128)(2,1)}, u32[]{:S(2)}) copy-start(bf16[512,512]{1,0:T(8,128)(2,1)} %copy-done.3) | copy-start | bytes 1572868
  332.9 27.6 %copy-start.11 = (bf16[512,256]{1,0:T(8,128)(2,1)}, bf16[512,256]{1,0:T(8,128)(2,1)S(1)}, u32[]{:S(2)}) copy-start(bf16[512,256]{1,0:T(8,128)(2,1)S(1)} %reduce_sum.120) | copy-start | bytes 786436
  359.9 0.7 copy-start.13
  400.4 5.9 %copy-start.6 = (bf16[512,256]{1,0:T(8,128)(2,1)S(1)}, bf16[512,256]{1,0:T(8,128)(2,1)}, u32[]{:S(2)}) copy-start(bf16[512,256]{1,0:T(8,128)(2,1)} %get-tuple-element.9) | copy-start | bytes 786436
  400.4 5.9 %copy-start.7 = (bf16[512,256]{1,0:T(8,128)(2,1)S(1)}, bf16[512,256]{1,0:T(8,128)(2,1)}, u32[]{:S(2)}) copy-start(bf16[512,256]{1,0:T(8,128)(2,1)} %get-tuple-element.11) | copy-start | bytes 786436
  400.4 6.7 %copy-start.10 = (bf16[512,512]{1,0:T(8,128)(2,1)S(1)}, bf16[512,512]{1,0:T(8,128)(2,1)}, u32[]{:S(2)}) copy-start(bf16[512,512]{1,0:T(8,128)(2,1)} %param.9) | copy-start | bytes 1572868
  400.5 6.7 %copy-start.12 = (bf16[512,256]{1,0:T(8,128)(2,1)S(1)}, bf16[512,256]{1,0:T(8,128)(2,1)}, u32[]{:S(2)}) copy-start(bf16[512,256]{1,0:T(8,128)(2,1)} %copy-done.11) | copy-start | bytes 786436
  400.5 6.7 %copy-start.14 = (bf16[512,256]{1,0:T(8,128)(2,1)S(1)}, bf16[512,256]{1,0:T(8,128)(2,1)}, u32[]{:S(2)}) copy-start(bf16[512,256]{1,0:T(8,128)(2,1)} %copy-done.13) | copy-start | bytes 786436
  401.5 24.0 %all-to-all-start.14 = ((bf16[128,5,512]{2,1,0:T(8,128)(2,1)}), bf16[128,5,512]{2,1,0:T(8,128)(2,1)S(1)}, u32[]{:S(2)}, u32[]{:S(2)}) async-start(bf16[128,5,512]{2,1,0:T(8,128)(2,1)} %broadcast_in_dim.46), calls=%async_computation.14 | async-start | bytes 2097152 | tf_op jit(solution)/shard_map/all_to_all | solution.py:121
  407.2 20.3 %copy-start.1 = (bf16[1024,512]{1,0:T(8,128)(2,1)S(1)}, bf16[1024,512]{1,0:T(8,128)(2,1)}, u32[]{:S(2)}) copy-start(bf16[1024,512]{1,0:T(8,128)(2,1)} %param.7) | copy-start | bytes 3145732

commit v9 on v8

--- a/solution.py
+++ b/solution.py
@@ -22,26 +22,14 @@
     for j in range(fill):
         target = rows_ref[step, j]
         product = jnp.dot(tiles_ref[0, j], inputs, preferred_element_type=jnp.float32)
-
-        @pl.when(first_ref[step, j] == 1)
-        def _():
-            acc_ref[target] = product
-
-        @pl.when(first_ref[step, j] == 0)
-        def _():
-            acc_ref[target] += product
+        acc_ref[target] = jnp.where(first_ref[step, j] == 1, product, acc_ref[target] + product)
 
     @pl.when(step == pl.num_programs(0) - 1)
     def _():
         for tile in range(acc_ref.shape[0]):
-
-            @pl.when(touched_ref[tile] == 1)
-            def _():
-                out_ref[tile] = acc_ref[tile].astype(out_ref.dtype)
-
-            @pl.when(touched_ref[tile] == 0)
-            def _():
-                out_ref[tile] = jnp.zeros(out_ref.shape[1:], out_ref.dtype)
+            out_ref[tile] = jnp.where(touched_ref[tile] == 1, acc_ref[tile], 0.0).astype(
+                out_ref.dtype
+            )
 
 
 def forward_spmm(row_lists, tile_stack, shard_rows, row_tiles, interpret=False):

time: 430 us -> 415 us (0.965)
  Pallas kernels: 87.4 us -> 66.5 us
  waiting for transfers between devices: 125 us -> 132 us
    pallas_call x2, Pallas kernels: 54.3 us -> 33.4 us  [forward_spmm(): pl.pallas_call(_forward_kernel, grid_spec=grid_spec, out_shape=jax.ShapeD...]
    all_to_all x3, waiting for transfers between devices: 26.7 us -> 32.4 us  [gather_by_exchange(): return lax.all_to_all(stacked, axis, 0, 0, tiled=True)]
  transfers between devices with their start and end apart: 10 -> 10, of which waited for: 7 -> 8; matrix products, arithmetic and copies ran while one was open for 4% -> 4% of each run, Pallas kernels for 20% -> 16%
where the time goes in v9:
time: 415 us; the launch traced here: 412 us
  waiting for transfers between devices  132 us (32%)
  blocking collectives  119 us (29%)
  Pallas kernels  66.5 us (16%)
  starting transfers between devices  53.2 us (13%)
  other arithmetic  21.3 us (5%)
  local copies, waits for them, and re-layouts  17.4 us (4%)
    all_to_all x6, waiting for transfers between devices, reduce_by_exchange(): received = lax.all_to_all(chunks, axis, 0, 0, tiled=True)  82.7 us
    all_to_all x4, blocking collectives, gather_by_exchange(): return lax.all_to_all(stacked, axis, 0, 0, tiled=True)  81.7 us
    all_to_all x1, blocking collectives, reduce_by_exchange(): received = lax.all_to_all(chunks, axis, 0, 0, tiled=True)  37.1 us
    pallas_call x2, Pallas kernels, forward_spmm(): pl.pallas_call(_forward_kernel, grid_spec=grid_spec, out_shape=jax.ShapeD...  33.4 us
    pallas_call x2, Pallas kernels, backward_spmm(): pl.pallas_call(_backward_kernel, grid_spec=grid_spec, out_shape=jax.Shape...  33.1 us
    all_to_all x6, starting transfers between devices, reduce_by_exchange(): received = lax.all_to_all(chunks, axis, 0, 0, tiled=True)  32.5 us
    all_to_all x3, waiting for transfers between devices, gather_by_exchange(): return lax.all_to_all(stacked, axis, 0, 0, tiled=True)  32.4 us
    all_to_all x1, waiting for transfers between devices, per_device(): lax.all_to_all(outgoing, ('rh', 'core'), split_axis=0, concat_axis=0, til...  16.5 us
  transfers between devices with their start and end apart: 10, of which 8 were waited for; matrix products, arithmetic and copies ran while one was open for 4% of the time, Pallas kernels for 16%

profile of v9, /device:TPU:1, one launch (start us, length us, event | category | flops | bytes accessed | tf_op | source)
XLA Modules:
  0.0 411.9 jit_solution(17826929239712954739)
XLA Ops:
  2.5 5.1 %gather_fusion = bf16[1024,512]{1,0:T(8,128)(2,1)} fusion(bf16[1024,512]{1,0:T(8,128)(2,1)S(1)} %copy-done, s32[1024]{0:T(1024)S(1)} %broadcast_clamp_fusion), kind=kCustom, calls=%fused_computation | custom fusion | bytes 2101248 | tf_op jit(solution)/shard_map/gather | solution.py:135
  7.6 8.6 %all-to-all-start = ((bf16[16,64,512]{2,1,0:T(8,128)(2,1)}), bf16[16,64,512]{2,1,0:T(8,128)(2,1)S(1)}, u32[]{:S(2)}, u32[]{:S(2)}) async-start(bf16[16,64,512]{2,1,0:T(8,128)(2,1)} %bitcast.2), calls=%async_computation | async-start | bytes 2097152 | tf_op jit(solution)/shard_map/all_to_all | solution.py:136
  16.7 16.5 %all-to-all-done = bf16[16,64,512]{2,1,0:T(8,128)(2,1)S(1)} async-done(((bf16[16,64,512]{2,1,0:T(8,128)(2,1)}), bf16[16,64,512]{2,1,0:T(8,128)(2,1)S(1)}, u32[]{:S(2)}, u32[]{:S(2)}) %all-to-all-start) | async-done | bytes 1048608 | tf_op jit(solution)/shard_map/all_to_all | solution.py:136
  33.3 2.0 gather_fusion.1
  36.0 30.6 %all_to_all.75 = bf16[8,512,256]{2,1,0:T(8,128)(2,1)} all-to-all(bf16[8,512,256]{2,1,0:T(8,128)(2,1)S(1)} %broadcast_in_dim.37), channel_id=1, replica_groups=mesh['blk'=8,'rh'=8,'core'=2] {'blk'}, dimensions={0} | all-to-all | bytes 4194304 | tf_op jit(solution)/shard_map/all_to_all | solution.py:109
  68.1 3.7 all-to-all-start.1
  74.2 16.7 %shard_map.111 = bf16[32,256,256]{2,1,0:T(8,128)(2,1)} custom-call(s32[16,6]{1,0:T(8,128)} %fusion.6.rows_ref, s32[16,6]{1,0:T(8,128)} %reshape.371.first_ref, s32[32]{0:T(128)} %convert_element_type.76.touched_ref, bf16[16,6,256,256]{3,2,1,0:T(8,128)(2,1)} %bitcast.50, bf16[4096,256]{1,0:T(8,128)(2,1)} %bitcast.60), custom_call_target="tpu_custom_call" | custom-call | tf_op jit(solution)/shard_map/pallas_call | solution.py:57
  90.9 5.7 %all-to-all-done.1 = bf16[8,512,256]{2,1,0:T(8,128)(2,1)S(1)} async-done(((bf16[8,512,256]{2,1,0:T(8,128)(2,1)}), bf16[8,512,256]{2,1,0:T(8,128)(2,1)S(1)}, u32[]{:S(2)}, u32[]{:S(2)}) %all-to-all-start.1) | async-done | bytes 2097184 | tf_op jit(solution)/shard_map/all_to_all | solution.py:109
  98.0 8.7 %all-to-all-start.5 = ((bf16[2,4096,256]{2,1,0:T(8,128)(2,1)}), bf16[2,4096,256]{2,1,0:T(8,128)(2,1)}, u32[]{:S(2)}, u32[]{:S(2)}) async-start(bf16[2,4096,256]{2,1,0:T(8,128)(2,1)} %bitcast.55), calls=%async_computation.5 | async-start | bytes 8388608 | tf_op jit(solution)/shard_map/all_to_all | solution.py:114
  106.7 16.7 %shard_map.110 = bf16[32,256,256]{2,1,0:T(8,128)(2,1)} custom-call(s32[16,6]{1,0:T(8,128)} %fusion.6.rows_ref, s32[16,6]{1,0:T(8,128)} %reshape.371.first_ref, s32[32]{0:T(128)} %convert_element_type.76.touched_ref, bf16[16,6,256,256]{3,2,1,0:T(8,128)(2,1)} %bitcast.51, bf16[4096,256]{1,0:T(8,128)(2,1)} %bitcast.59), custom_call_target="tpu_custom_call" | custom-call | tf_op jit(solution)/shard_map/pallas_call | solution.py:57
  123.4 5.6 %all-to-all-start.2 = ((bf16[2,4096,256]{2,1,0:T(8,128)(2,1)}), bf16[2,4096,256]{2,1,0:T(8,128)(2,1)}, u32[]{:S(2)}, u32[]{:S(2)}) async-start(bf16[2,4096,256]{2,1,0:T(8,128)(2,1)} %bitcast.56), calls=%async_computation.2 | async-start | bytes 8388608 | tf_op jit(solution)/shard_map/all_to_all | solution.py:114
  129.0 4.9 %reduce_sum.118 = bf16[4096,256]{1,0:T(8,128)(2,1)} reduce(bf16[2,4096,256]{2,1,0:T(8,128)(2,1)} %all-to-all-done.5, bf16[]{:T(256)} %constant.97.clone.1), dimensions={0}, to_apply=%region_8.9 | reduce | flops 1048576 | bytes 6291458 | tf_op jit(solution)/shard_map/reduce_sum | solution.py:115
  134.0 4.7 %all-to-all-start.6 = ((bf16[8,512,256]{2,1,0:T(8,128)(2,1)}), bf16[8,512,256]{2,1,0:T(8,128)(2,1)S(1)}, u32[]{:S(2)}, u32[]{:S(2)}) async-start(bf16[8,512,256]{2,1,0:T(8,128)(2,1)} %bitcast.14), calls=%async_computation.6 | async-start | bytes 4194304 | tf_op jit(solution)/shard_map/all_to_all | solution.py:114
  138.7 4.9 %reduce_sum.116 = bf16[4096,256]{1,0:T(8,128)(2,1)} reduce(bf16[2,4096,256]{2,1,0:T(8,128)(2,1)} %all-to-all-done.2, bf16[]{:T(256)} %constant.97.clone.1), dimensions={0}, to_apply=%region_6.7 | reduce | flops 1048576 | bytes 6291458 | tf_op jit(solution)/shard_map/reduce_sum | solution.py:115
  143.6 21.3 %all-to-all-done.6 = bf16[8,512,256]{2,1,0:T(8,128)(2,1)S(1)} async-done(((bf16[8,512,256]{2,1,0:T(8,128)(2,1)}), bf16[8,512,256]{2,1,0:T(8,128)(2,1)S(1)}, u32[]{:S(2)}, u32[]{:S(2)}) %all-to-all-start.6) | async-done | bytes 2097184 | tf_op jit(solution)/shard_map/all_to_all | solution.py:114
  164.9 5.3 %all-to-all-start.3 = ((bf16[8,512,256]{2,1,0:T(8,128)(2,1)}), bf16[8,512,256]{2,1,0:T(8,128)(2,1)}, u32[]{:S(2)}, u32[]{:S(2)}) async-start(bf16[8,512,256]{2,1,0:T(8,128)(2,1)} %bitcast.11), calls=%async_computation.3 | async-start | bytes 4194304 | tf_op jit(solution)/shard_map/all_to_all | solution.py:114
  170.5 26.0 %all-to-all-done.3 = bf16[8,512,256]{2,1,0:T(8,128)(2,1)} async-done(((bf16[8,512,256]{2,1,0:T(8,128)(2,1)}), bf16[8,512,256]{2,1,0:T(8,128)(2,1)}, u32[]{:S(2)}, u32[]{:S(2)}) %all-to-all-start.3) | async-done | bytes 2097184 | tf_op jit(solution)/shard_map/all_to_all | solution.py:114
  199.9 31.8 %all_to_all.76 = bf16[8,512,256]{2,1,0:T(8,128)(2,1)S(1)} all-to-all(bf16[8,512,256]{2,1,0:T(8,128)(2,1)S(1)} %broadcast_in_dim.38), channel_id=1, replica_groups=mesh['blk'=8,'rh'=8,'core'=2] {'rh'}, dimensions={0} | all-to-all | bytes 4194304 | tf_op jit(solution)/shard_map/all_to_all | solution.py:109
  232.0 10.2 %all_to_all.77 = bf16[2,4096,256]{2,1,0:T(8,128)(2,1)} all-to-all(bf16[2,4096,256]{2,1,0:T(8,128)(2,1)S(1)} %broadcast_in_dim.40), channel_id=1, replica_groups=mesh['blk'=8,'rh'=8,'core'=2] {'core'}, dimensions={0} | all-to-all | bytes 8388608 | tf_op jit(solution)/shard_map/all_to_all | solution.py:109
  243.7 3.6 all-to-all-start.10
  247.3 16.5 %shard_map.112 = bf16[4096,256]{1,0:T(8,128)(2,1)} custom-call(s32[16,6]{1,0:T(8,128)} %fusion.6.rows_ref, bf16[16,6,256,256]{3,2,1,0:T(8,128)(2,1)} %bitcast.52, bf16[32,256,256]{2,1,0:T(8,128)(2,1)} %bitcast.57), custom_call_target="tpu_custom_call" | custom-call | tf_op jit(solution)/shard_map/pallas_call | solution.py:96
  263.9 9.6 %all-to-all-done.10 = bf16[8,512,256]{2,1,0:T(8,128)(2,1)S(1)} async-done(((bf16[8,512,256]{2,1,0:T(8,128)(2,1)}), bf16[8,512,256]{2,1,0:T(8,128)(2,1)S(1)}, u32[]{:S(2)}, u32[]{:S(2)}) %all-to-all-start.10) | async-done | bytes 2097184 | tf_op jit(solution)/shard_map/all_to_all | solution.py:109
  273.7 9.0 %all_to_all.78 = bf16[2,4096,256]{2,1,0:T(8,128)(2,1)} all-to-all(bf16[2,4096,256]{2,1,0:T(8,128)(2,1)S(1)} %broadcast_in_dim.43), channel_id=1, replica_groups=mesh['blk'=8,'rh'=8,'core'=2] {'core'}, dimensions={0} | all-to-all | bytes 8388608 | tf_op jit(solution)/shard_map/all_to_all | solution.py:109
  282.7 3.6 all-to-all-start.9
  286.3 16.6 %shard_map.113 = bf16[4096,256]{1,0:T(8,128)(2,1)} custom-call(s32[16,6]{1,0:T(8,128)} %fusion.6.rows_ref, bf16[16,6,256,256]{3,2,1,0:T(8,128)(2,1)} %bitcast.53, bf16[32,256,256]{2,1,0:T(8,128)(2,1)} %bitcast.58), custom_call_target="tpu_custom_call" | custom-call | tf_op jit(solution)/shard_map/pallas_call | solution.py:96
  302.9 10.1 %all-to-all-done.9 = bf16[8,512,256]{2,1,0:T(8,128)(2,1)S(1)} async-done(((bf16[8,512,256]{2,1,0:T(8,128)(2,1)}), bf16[8,512,256]{2,1,0:T(8,128)(2,1)S(1)}, u32[]{:S(2)}, u32[]{:S(2)}) %all-to-all-start.9) | async-done | bytes 2097184 | tf_op jit(solution)/shard_map/all_to_all | solution.py:114
  313.0 4.5 %all-to-all-start.12 = ((bf16[8,512,256]{2,1,0:T(8,128)(2,1)}), bf16[8,512,256]{2,1,0:T(8,128)(2,1)}, u32[]{:S(2)}, u32[]{:S(2)}) async-start(bf16[8,512,256]{2,1,0:T(8,128)(2,1)} %bitcast.61), calls=%async_computation.12 | async-start | bytes 4194304 | tf_op jit(solution)/shard_map/all_to_all | solution.py:114
  318.0 25.4 %all-to-all-done.12 = bf16[8,512,256]{2,1,0:T(8,128)(2,1)} async-done(((bf16[8,512,256]{2,1,0:T(8,128)(2,1)}), bf16[8,512,256]{2,1,0:T(8,128)(2,1)}, u32[]{:S(2)}, u32[]{:S(2)}) %all-to-all-start.12) | async-done | bytes 2097184 | tf_op jit(solution)/shard_map/all_to_all | solution.py:114
  343.4 2.0 reduce_sum.121
  347.6 37.1 %all_to_all.79 = f32[128,5,512]{2,1,0:T(8,128)S(1)} all-to-all(f32[128,5,512]{2,1,0:T(8,128)} %reshape.370), channel_id=1, replica_groups=mesh['blk'=8,'rh'=8,'core'=2] {'blk','rh','core'}, dimensions={0} | all-to-all | bytes 2621440 | tf_op jit(solution)/shard_map/all_to_all | solution.py:114
  386.0 4.8 %all-to-all-start.14 = ((bf16[128,5,512]{2,1,0:T(8,128)(2,1)}), bf16[128,5,512]{2,1,0:T(8,128)(2,1)S(1)}, u32[]{:S(2)}, u32[]{:S(2)}) async-start(bf16[128,5,512]{2,1,0:T(8,128)(2,1)} %broadcast_in_dim.46), calls=%async_computation.14 | async-start | bytes 2097152 | tf_op jit(solution)/shard_map/all_to_all | solution.py:109
  393.0 17.1 %all-to-all-done.14 = bf16[128,5,512]{2,1,0:T(8,128)(2,1)S(1)} async-done(((bf16[128,5,512]{2,1,0:T(8,128)(2,1)}), bf16[128,5,512]{2,1,0:T(8,128)(2,1)S(1)}, u32[]{:S(2)}, u32[]{:S(2)}) %all-to-all-start.14) | async-done | bytes 655392 | tf_op jit(solution)/shard_map/all_to_all | solution.py:109
  (90 shorter events, 22.0 us)
Async XLA Ops:
  0.6 1.9 copy-start
  7.6 8.6 %copy-start.15 = (s32[1,16,16]{2,1,0:T(8,128)S(1)}, s32[1,16,16]{2,1,0:T(8,128)}, u32[]{:S(2)}) copy-start(s32[1,16,16]{2,1,0:T(8,128)} %param.8) | copy-start | bytes 3076
  7.6 25.6 %all-to-all-start = ((bf16[16,64,512]{2,1,0:T(8,128)(2,1)}), bf16[16,64,512]{2,1,0:T(8,128)(2,1)S(1)}, u32[]{:S(2)}, u32[]{:S(2)}) async-start(bf16[16,64,512]{2,1,0:T(8,128)(2,1)} %bitcast.2), calls=%async_computation | async-start | bytes 2097152 | tf_op jit(solution)/shard_map/all_to_all | solution.py:136
  33.3 2.0 copy-start.9
  35.2 0.8 copy-start.3
  35.7 31.0 %copy-start.5 = (bf16[512,512]{1,0:T(8,128)(2,1)}, bf16[512,512]{1,0:T(8,128)(2,1)S(1)}, u32[]{:S(2)}) copy-start(bf16[512,512]{1,0:T(8,128)(2,1)S(1)} %convolution_convert_fusion.1) | copy-start | bytes 1572868
  68.1 3.7 copy-start.16
  68.1 28.5 %all-to-all-start.1 = ((bf16[8,512,256]{2,1,0:T(8,128)(2,1)}), bf16[8,512,256]{2,1,0:T(8,128)(2,1)S(1)}, u32[]{:S(2)}, u32[]{:S(2)}) async-start(bf16[8,512,256]{2,1,0:T(8,128)(2,1)} %broadcast_in_dim.36), calls=%async_computation.1 | async-start | bytes 4194304 | tf_op jit(solution)/shard_map/all_to_all | solution.py:109
  96.6 1.4 copy-start.2
  98.0 25.4 %all-to-all-start.5 = ((bf16[2,4096,256]{2,1,0:T(8,128)(2,1)}), bf16[2,4096,256]{2,1,0:T(8,128)(2,1)}, u32[]{:S(2)}, u32[]{:S(2)}) async-start(bf16[2,4096,256]{2,1,0:T(8,128)(2,1)} %bitcast.55), calls=%async_computation.5 | async-start | bytes 8388608 | tf_op jit(solution)/shard_map/all_to_all | solution.py:114
  123.4 10.6 %all-to-all-start.2 = ((bf16[2,4096,256]{2,1,0:T(8,128)(2,1)}), bf16[2,4096,256]{2,1,0:T(8,128)(2,1)}, u32[]{:S(2)}, u32[]{:S(2)}) async-start(bf16[2,4096,256]{2,1,0:T(8,128)(2,1)} %bitcast.56), calls=%async_computation.2 | async-start | bytes 8388608 | tf_op jit(solution)/shard_map/all_to_all | solution.py:114
  134.0 30.9 %all-to-all-start.6 = ((bf16[8,512,256]{2,1,0:T(8,128)(2,1)}), bf16[8,512,256]{2,1,0:T(8,128)(2,1)S(1)}, u32[]{:S(2)}, u32[]{:S(2)}) async-start(bf16[8,512,256]{2,1,0:T(8,128)(2,1)} %bitcast.14), calls=%async_computation.6 | async-start | bytes 4194304 | tf_op jit(solution)/shard_map/all_to_all | solution.py:114
  164.9 5.3 %copy-start.17 = (f32[512]{0:T(512)S(1)}, f32[512]{0:T(512)}, u32[]{:S(2)}) copy-start(f32[512]{0:T(512)} %param.10) | copy-start | bytes 6148
  164.9 31.6 %all-to-all-start.3 = ((bf16[8,512,256]{2,1,0:T(8,128)(2,1)}), bf16[8,512,256]{2,1,0:T(8,128)(2,1)}, u32[]{:S(2)}, u32[]{:S(2)}) async-start(bf16[8,512,256]{2,1,0:T(8,128)(2,1)} %bitcast.11), calls=%async_computation.3 | async-start | bytes 4194304 | tf_op jit(solution)/shard_map/all_to_all | solution.py:114
  170.5 27.9 %copy-start.8 = (bf16[512,512]{1,0:T(8,128)(2,1)S(1)}, bf16[512,512]{1,0:T(8,128)(2,1)}, u32[]{:S(2)}) copy-start(bf16[512,512]{1,0:T(8,128)(2,1)} %param.13) | copy-start | bytes 1572868
  243.7 29.7 %all-to-all-start.10 = ((bf16[8,512,256]{2,1,0:T(8,128)(2,1)}), bf16[8,512,256]{2,1,0:T(8,128)(2,1)S(1)}, u32[]{:S(2)}, u32[]{:S(2)}) async-start(bf16[8,512,256]{2,1,0:T(8,128)(2,1)} %broadcast_in_dim.41), calls=%async_computation.10 | async-start | bytes 4194304 | tf_op jit(solution)/shard_map/all_to_all | solution.py:109
  282.7 30.3 %all-to-all-start.9 = ((bf16[8,512,256]{2,1,0:T(8,128)(2,1)}), bf16[8,512,256]{2,1,0:T(8,128)(2,1)S(1)}, u32[]{:S(2)}, u32[]{:S(2)}) async-start(bf16[8,512,256]{2,1,0:T(8,128)(2,1)} %bitcast.17), calls=%async_computation.9 | async-start | bytes 4194304 | tf_op jit(solution)/shard_map/all_to_all | solution.py:114
  313.0 30.4 %all-to-all-start.12 = ((bf16[8,512,256]{2,1,0:T(8,128)(2,1)}), bf16[8,512,256]{2,1,0:T(8,128)(2,1)}, u32[]{:S(2)}, u32[]{:S(2)}) async-start(bf16[8,512,256]{2,1,0:T(8,128)(2,1)} %bitcast.61), calls=%async_computation.12 | async-start | bytes 4194304 | tf_op jit(solution)/shard_map/all_to_all | solution.py:114
  317.6 27.7 %copy-start.4 = (bf16[512,512]{1,0:T(8,128)(2,1)S(1)}, bf16[512,512]{1,0:T(8,128)(2,1)}, u32[]{:S(2)}) copy-start(bf16[512,512]{1,0:T(8,128)(2,1)} %copy-done.3) | copy-start | bytes 1572868
  318.0 27.8 %copy-start.11 = (bf16[512,256]{1,0:T(8,128)(2,1)}, bf16[512,256]{1,0:T(8,128)(2,1)S(1)}, u32[]{:S(2)}) copy-start(bf16[512,256]{1,0:T(8,128)(2,1)S(1)} %reduce_sum.120) | copy-start | bytes 786436
  345.3 0.7 copy-start.13
  384.9 5.9 %copy-start.6 = (bf16[512,256]{1,0:T(8,128)(2,1)S(1)}, bf16[512,256]{1,0:T(8,128)(2,1)}, u32[]{:S(2)}) copy-start(bf16[512,256]{1,0:T(8,128)(2,1)} %get-tuple-element.9) | copy-start | bytes 786436
  385.0 5.9 %copy-start.7 = (bf16[512,256]{1,0:T(8,128)(2,1)S(1)}, bf16[512,256]{1,0:T(8,128)(2,1)}, u32[]{:S(2)}) copy-start(bf16[512,256]{1,0:T(8,128)(2,1)} %get-tuple-element.11) | copy-start | bytes 786436
  385.0 6.7 %copy-start.10 = (bf16[512,512]{1,0:T(8,128)(2,1)S(1)}, bf16[512,512]{1,0:T(8,128)(2,1)}, u32[]{:S(2)}) copy-start(bf16[512,512]{1,0:T(8,128)(2,1)} %param.9) | copy-start | bytes 1572868
  385.0 6.7 %copy-start.12 = (bf16[512,256]{1,0:T(8,128)(2,1)S(1)}, bf16[512,256]{1,0:T(8,128)(2,1)}, u32[]{:S(2)}) copy-start(bf16[512,256]{1,0:T(8,128)(2,1)} %copy-done.11) | copy-start | bytes 786436
  385.0 6.7 %copy-start.14 = (bf16[512,256]{1,0:T(8,128)(2,1)S(1)}, bf16[512,256]{1,0:T(8,128)(2,1)}, u32[]{:S(2)}) copy-start(bf16[512,256]{1,0:T(8,128)(2,1)} %copy-done.13) | copy-start | bytes 786436
  386.0 24.0 %all-to-all-start.14 = ((bf16[128,5,512]{2,1,0:T(8,128)(2,1)}), bf16[128,5,512]{2,1,0:T(8,128)(2,1)S(1)}, u32[]{:S(2)}, u32[]{:S(2)}) async-start(bf16[128,5,512]{2,1,0:T(8,128)(2,1)} %broadcast_in_dim.46), calls=%async_computation.14 | async-start | bytes 2097152 | tf_op jit(solution)/shard_map/all_to_all | solution.py:109
  391.7 20.3 %copy-start.1 = (bf16[1024,512]{1,0:T(8,128)(2,1)S(1)}, bf16[1024,512]{1,0:T(8,128)(2,1)}, u32[]{:S(2)}) copy-start(bf16[1024,512]{1,0:T(8,128)(2,1)} %param.7) | copy-start | bytes 3145732

commit v10 on v9

--- a/solution.py
+++ b/solution.py
@@ -171,31 +171,37 @@
             jnp.bfloat16
         )
         activated_parts.append(jax.nn.silu(preact).astype(jnp.bfloat16))
-        bias_parts.append(jnp.sum(own_grad.astype(jnp.float32), axis=0))
         chip_grad = gather_by_exchange(own_grad, "rh", chip_size).reshape(-1, chunk_width)
         pre_grad = gather_by_exchange(chip_grad, "core", core_size)
         grad_tiles = pre_grad.reshape(row_tiles, tile_size, chunk_width)
         column_contribution = backward_spmm(row_lists, tile_stack, grad_tiles)
-        grad_parts.append(
-            reduce_by_exchange(column_contribution, "blk", blk_size).astype(jnp.bfloat16)
-        )
+        partition_bias = jnp.sum(grad_tiles.astype(jnp.float32), axis=(0, 1))
+        bias_high = partition_bias.astype(jnp.bfloat16)
+        bias_low = (partition_bias - bias_high.astype(jnp.float32)).astype(jnp.bfloat16)
+        extra = jnp.zeros((16, chunk_width), jnp.bfloat16).at[0].set(bias_high).at[1].set(bias_low)
+        pieces = jnp.concatenate(
+            [
+                column_contribution.reshape(blk_size, dev_rows, chunk_width),
+                jnp.broadcast_to(extra[None], (blk_size, 16, chunk_width)),
+            ],
+            axis=1,
+        )
+        received = lax.all_to_all(pieces, "blk", 0, 0, tiled=True)
+        summed = jnp.sum(received.astype(jnp.float32), axis=0)
+        grad_parts.append(summed[:dev_rows].astype(jnp.bfloat16))
+        bias_parts.append(summed[dev_rows] + summed[dev_rows + 1])
     activated = jnp.concatenate(activated_parts, axis=1)
     proj_grad = jnp.concatenate(grad_parts, axis=1)
-    local_bias = jnp.concatenate(bias_parts, axis=0)
+    bias_sum = jnp.concatenate(bias_parts, axis=0)
     local_weight = jnp.einsum("nf,ng->fg", features, proj_grad, preferred_element_type=jnp.float32)
     device_count = blk_size * rep_size
-    chunk_rows = feature_width // device_count + 1
-    pad_rows = jnp.zeros((device_count * chunk_rows - feature_width - 1, feature_width), jnp.float32)
-    stacked = jnp.concatenate([local_weight, local_bias[None, :], pad_rows], axis=0)
     every = ("blk", "rh", "core")
-    reduced = reduce_by_exchange(stacked, every, device_count)
-    stacked_sum = (
+    reduced = reduce_by_exchange(local_weight, every, device_count)
+    weight_sum = (
         gather_by_exchange(reduced.astype(jnp.bfloat16), every, device_count)
         .reshape(-1, feature_width)
         .astype(jnp.float32)
     )
-    weight_sum = stacked_sum[:feature_width]
-    bias_sum = stacked_sum[feature_width]
     feature_grad = jnp.einsum(
         "ng,fg->nf", proj_grad, weight, preferred_element_type=jnp.float32
     ).astype(jnp.bfloat16)

time: 415 us -> 403 us (0.971)
  blocking collectives: 119 us -> 72.7 us
  starting transfers between devices: 53.2 us -> 66.6 us
  other arithmetic: 21.3 us -> 32 us
  local copies, waits for them, and re-layouts: 17.4 us -> 21.6 us
    all_to_all x1 -> x0, blocking collectives: 37.1 us -> none  [reduce_by_exchange(): received = lax.all_to_all(chunks, axis, 0, 0, tiled=True)]
    all_to_all x0 -> x2, waiting for transfers between devices: none -> 29.8 us  [per_device(): received = lax.all_to_all(pieces, 'blk', 0, 0, tiled=True)]
    all_to_all x6 -> x5, waiting for transfers between devices: 82.7 us -> 64.7 us  [reduce_by_exchange(): received = lax.all_to_all(chunks, axis, 0, 0, tiled=True)]
    all_to_all x4 -> x3, blocking collectives: 81.7 us -> 72.7 us  [gather_by_exchange(): return lax.all_to_all(stacked, axis, 0, 0, tiled=True)]
    all_to_all x0 -> x2, starting transfers between devices: none -> 7.97 us  [per_device(): received = lax.all_to_all(pieces, 'blk', 0, 0, tiled=True)]
    reduce_sum x1 -> x4, other arithmetic: 1.29 us -> 8.8 us  [the longest x2 6.57 us: per_device(): partition_bias = jnp.sum(grad_tiles.astype(jnp.float32), axis=(0, 1))]
    all_to_all x3 -> x4, waiting for transfers between devices: 32.4 us -> 25.3 us  [gather_by_exchange(): return lax.all_to_all(stacked, axis, 0, 0, tiled=True)]
    all_to_all x3 -> x4, starting transfers between devices: 12.1 us -> 18.7 us  [gather_by_exchange(): return lax.all_to_all(stacked, axis, 0, 0, tiled=True)]
  transfers between devices with their start and end apart: 10 -> 12, of which waited for: 8 -> 10; matrix products, arithmetic and copies ran while one was open for 4% -> 7% of each run, Pallas kernels for 16% -> 17%
where the time goes in v10:
time: 403 us; the launch traced here: 400 us
  waiting for transfers between devices  136 us (34%)
  blocking collectives  72.7 us (18%)
  starting transfers between devices  66.6 us (17%)
  Pallas kernels  66.5 us (17%)
  other arithmetic  32 us (8%)
  local copies, waits for them, and re-layouts  21.6 us (5%)
    all_to_all x3, blocking collectives, gather_by_exchange(): return lax.all_to_all(stacked, axis, 0, 0, tiled=True)  72.7 us
    all_to_all x5, waiting for transfers between devices, reduce_by_exchange(): received = lax.all_to_all(chunks, axis, 0, 0, tiled=True)  64.7 us
    pallas_call x2, Pallas kernels, forward_spmm(): pl.pallas_call(_forward_kernel, grid_spec=grid_spec, out_shape=jax.ShapeD...  33.4 us
    pallas_call x2, Pallas kernels, backward_spmm(): pl.pallas_call(_backward_kernel, grid_spec=grid_spec, out_shape=jax.Shape...  33.1 us
    all_to_all x5, starting transfers between devices, reduce_by_exchange(): received = lax.all_to_all(chunks, axis, 0, 0, tiled=True)  31.5 us
    all_to_all x2, waiting for transfers between devices, per_device(): received = lax.all_to_all(pieces, 'blk', 0, 0, tiled=True)  29.8 us
    all_to_all x4, waiting for transfers between devices, gather_by_exchange(): return lax.all_to_all(stacked, axis, 0, 0, tiled=True)  25.3 us
    all_to_all x4, starting transfers between devices, gather_by_exchange(): return lax.all_to_all(stacked, axis, 0, 0, tiled=True)  18.7 us
  transfers between devices with their start and end apart: 12, of which 10 were waited for; matrix products, arithmetic and copies ran while one was open for 7% of the time, Pallas kernels for 17%

profile of v10, /device:TPU:1, one launch (start us, length us, event | category | flops | bytes accessed | tf_op | source)
XLA Modules:
  0.0 400.0 jit_solution(12810865479201119838)
XLA Ops:
  2.5 5.1 %gather_fusion = bf16[1024,512]{1,0:T(8,128)(2,1)} fusion(bf16[1024,512]{1,0:T(8,128)(2,1)S(1)} %copy-done, s32[1024]{0:T(1024)S(1)} %broadcast_clamp_fusion), kind=kCustom, calls=%fused_computation | custom fusion | bytes 2101248 | tf_op jit(solution)/shard_map/gather | solution.py:135
  7.6 8.4 %all-to-all-start = ((bf16[16,64,512]{2,1,0:T(8,128)(2,1)}), bf16[16,64,512]{2,1,0:T(8,128)(2,1)S(1)}, u32[]{:S(2)}, u32[]{:S(2)}) async-start(bf16[16,64,512]{2,1,0:T(8,128)(2,1)} %bitcast.2), calls=%async_computation | async-start | bytes 2097152 | tf_op jit(solution)/shard_map/all_to_all | solution.py:136
  16.6 16.5 %all-to-all-done = bf16[16,64,512]{2,1,0:T(8,128)(2,1)S(1)} async-done(((bf16[16,64,512]{2,1,0:T(8,128)(2,1)}), bf16[16,64,512]{2,1,0:T(8,128)(2,1)S(1)}, u32[]{:S(2)}, u32[]{:S(2)}) %all-to-all-start) | async-done | bytes 1048608 | tf_op jit(solution)/shard_map/all_to_all | solution.py:136
  35.9 30.6 %all_to_all.75 = bf16[8,512,256]{2,1,0:T(8,128)(2,1)} all-to-all(bf16[8,512,256]{2,1,0:T(8,128)(2,1)S(1)} %broadcast_in_dim.36), channel_id=1, replica_groups=mesh['blk'=8,'rh'=8,'core'=2] {'blk'}, dimensions={0} | all-to-all | bytes 4194304 | tf_op jit(solution)/shard_map/all_to_all | solution.py:109
  68.0 3.7 all-to-all-start.4
  74.1 16.7 %shard_map.110 = bf16[32,256,256]{2,1,0:T(8,128)(2,1)} custom-call(s32[16,6]{1,0:T(8,128)} %fusion.6.rows_ref, s32[16,6]{1,0:T(8,128)} %reshape.505.first_ref, s32[32]{0:T(128)} %convert_element_type.134.touched_ref, bf16[16,6,256,256]{3,2,1,0:T(8,128)(2,1)} %bitcast.52, bf16[4096,256]{1,0:T(8,128)(2,1)} %bitcast.61), custom_call_target="tpu_custom_call" | custom-call | tf_op jit(solution)/shard_map/pallas_call | solution.py:57
  90.8 5.7 %all-to-all-done.4 = bf16[8,512,256]{2,1,0:T(8,128)(2,1)S(1)} async-done(((bf16[8,512,256]{2,1,0:T(8,128)(2,1)}), bf16[8,512,256]{2,1,0:T(8,128)(2,1)S(1)}, u32[]{:S(2)}, u32[]{:S(2)}) %all-to-all-start.4) | async-done | bytes 2097184 | tf_op jit(solution)/shard_map/all_to_all | solution.py:109
  97.9 8.7 %all-to-all-start.2 = ((bf16[2,4096,256]{2,1,0:T(8,128)(2,1)}), bf16[2,4096,256]{2,1,0:T(8,128)(2,1)}, u32[]{:S(2)}, u32[]{:S(2)}) async-start(bf16[2,4096,256]{2,1,0:T(8,128)(2,1)} %bitcast.58), calls=%async_computation.2 | async-start | bytes 8388608 | tf_op jit(solution)/shard_map/all_to_all | solution.py:114
  106.6 16.7 %shard_map.111 = bf16[32,256,256]{2,1,0:T(8,128)(2,1)} custom-call(s32[16,6]{1,0:T(8,128)} %fusion.6.rows_ref, s32[16,6]{1,0:T(8,128)} %reshape.505.first_ref, s32[32]{0:T(128)} %convert_element_type.134.touched_ref, bf16[16,6,256,256]{3,2,1,0:T(8,128)(2,1)} %bitcast.53, bf16[4096,256]{1,0:T(8,128)(2,1)} %bitcast.60), custom_call_target="tpu_custom_call" | custom-call | tf_op jit(solution)/shard_map/pallas_call | solution.py:57
  123.3 5.6 %all-to-all-start.5 = ((bf16[2,4096,256]{2,1,0:T(8,128)(2,1)}), bf16[2,4096,256]{2,1,0:T(8,128)(2,1)}, u32[]{:S(2)}, u32[]{:S(2)}) async-start(bf16[2,4096,256]{2,1,0:T(8,128)(2,1)} %bitcast.59), calls=%async_computation.5 | async-start | bytes 8388608 | tf_op jit(solution)/shard_map/all_to_all | solution.py:114
  128.9 4.9 %reduce_sum.114 = bf16[4096,256]{1,0:T(8,128)(2,1)} reduce(bf16[2,4096,256]{2,1,0:T(8,128)(2,1)} %all-to-all-done.2, bf16[]{:T(256)} %constant.191.clone.1), dimensions={0}, to_apply=%region_6.7 | reduce | flops 1048576 | bytes 6291458 | tf_op jit(solution)/shard_map/reduce_sum | solution.py:115
  133.9 4.7 %all-to-all-start.3 = ((bf16[8,512,256]{2,1,0:T(8,128)(2,1)}), bf16[8,512,256]{2,1,0:T(8,128)(2,1)S(1)}, u32[]{:S(2)}, u32[]{:S(2)}) async-start(bf16[8,512,256]{2,1,0:T(8,128)(2,1)} %bitcast.11), calls=%async_computation.3 | async-start | bytes 4194304 | tf_op jit(solution)/shard_map/all_to_all | solution.py:114
  138.6 4.9 %reduce_sum.116 = bf16[4096,256]{1,0:T(8,128)(2,1)} reduce(bf16[2,4096,256]{2,1,0:T(8,128)(2,1)} %all-to-all-done.5, bf16[]{:T(256)} %constant.191.clone.1), dimensions={0}, to_apply=%region_8.9 | reduce | flops 1048576 | bytes 6291458 | tf_op jit(solution)/shard_map/reduce_sum | solution.py:115
  143.5 21.3 %all-to-all-done.3 = bf16[8,512,256]{2,1,0:T(8,128)(2,1)S(1)} async-done(((bf16[8,512,256]{2,1,0:T(8,128)(2,1)}), bf16[8,512,256]{2,1,0:T(8,128)(2,1)S(1)}, u32[]{:S(2)}, u32[]{:S(2)}) %all-to-all-start.3) | async-done | bytes 2097184 | tf_op jit(solution)/shard_map/all_to_all | solution.py:114
  164.8 5.2 %all-to-all-start.6 = ((bf16[8,512,256]{2,1,0:T(8,128)(2,1)}), bf16[8,512,256]{2,1,0:T(8,128)(2,1)}, u32[]{:S(2)}, u32[]{:S(2)}) async-start(bf16[8,512,256]{2,1,0:T(8,128)(2,1)} %bitcast.14), calls=%async_computation.6 | async-start | bytes 4194304 | tf_op jit(solution)/shard_map/all_to_all | solution.py:114
  170.3 26.0 %all-to-all-done.6 = bf16[8,512,256]{2,1,0:T(8,128)(2,1)} async-done(((bf16[8,512,256]{2,1,0:T(8,128)(2,1)}), bf16[8,512,256]{2,1,0:T(8,128)(2,1)}, u32[]{:S(2)}, u32[]{:S(2)}) %all-to-all-start.6) | async-done | bytes 2097184 | tf_op jit(solution)/shard_map/all_to_all | solution.py:114
  199.5 31.8 %all_to_all.76 = bf16[8,512,256]{2,1,0:T(8,128)(2,1)S(1)} all-to-all(bf16[8,512,256]{2,1,0:T(8,128)(2,1)S(1)} %broadcast_in_dim.38), channel_id=1, replica_groups=mesh['blk'=8,'rh'=8,'core'=2] {'rh'}, dimensions={0} | all-to-all | bytes 4194304 | tf_op jit(solution)/shard_map/all_to_all | solution.py:109
  231.6 10.2 %all_to_all.77 = bf16[2,4096,256]{2,1,0:T(8,128)(2,1)} all-to-all(bf16[2,4096,256]{2,1,0:T(8,128)(2,1)S(1)} %broadcast_in_dim.40), channel_id=1, replica_groups=mesh['blk'=8,'rh'=8,'core'=2] {'core'}, dimensions={0} | all-to-all | bytes 8388608 | tf_op jit(solution)/shard_map/all_to_all | solution.py:109
  243.3 3.8 all-to-all-start.10
  250.4 16.6 %shard_map.112 = bf16[4096,256]{1,0:T(8,128)(2,1)} custom-call(s32[16,6]{1,0:T(8,128)} %fusion.6.rows_ref, bf16[16,6,256,256]{3,2,1,0:T(8,128)(2,1)} %bitcast.54, bf16[32,256,256]{2,1,0:T(8,128)(2,1)} %bitcast.56), custom_call_target="tpu_custom_call" | custom-call | tf_op jit(solution)/shard_map/pallas_call | solution.py:96
  267.0 6.1 %all-to-all-done.10 = bf16[8,512,256]{2,1,0:T(8,128)(2,1)S(1)} async-done(((bf16[8,512,256]{2,1,0:T(8,128)(2,1)}), bf16[8,512,256]{2,1,0:T(8,128)(2,1)S(1)}, u32[]{:S(2)}, u32[]{:S(2)}) %all-to-all-start.10) | async-done | bytes 2097184 | tf_op jit(solution)/shard_map/all_to_all | solution.py:109
  275.3 6.9 %all-to-all-start.11 = ((bf16[2,4096,256]{2,1,0:T(8,128)(2,1)}), bf16[2,4096,256]{2,1,0:T(8,128)(2,1)}, u32[]{:S(2)}, u32[]{:S(2)}) async-start(bf16[2,4096,256]{2,1,0:T(8,128)(2,1)} %broadcast_in_dim.44), calls=%async_computation.11 | async-start | bytes 8388608 | tf_op jit(solution)/shard_map/all_to_all | solution.py:109
  286.3 3.6 all-to-all-start.9
  290.0 3.3 convert_reduce_fusion
  293.3 16.5 %shard_map.113 = bf16[4096,256]{1,0:T(8,128)(2,1)} custom-call(s32[16,6]{1,0:T(8,128)} %fusion.6.rows_ref, bf16[16,6,256,256]{3,2,1,0:T(8,128)(2,1)} %bitcast.55, bf16[32,256,256]{2,1,0:T(8,128)(2,1)} %bitcast.20.grad_ref), custom_call_target="tpu_custom_call" | custom-call | tf_op jit(solution)/shard_map/pallas_call | solution.py:96
  312.9 4.4 %all-to-all-done.9 = bf16[8,528,256]{2,1,0:T(8,128)(2,1)S(1)} async-done(((bf16[8,528,256]{2,1,0:T(8,128)(2,1)}), bf16[8,528,256]{2,1,0:T(8,128)(2,1)S(1)}, u32[]{:S(2)}, u32[]{:S(2)}) %all-to-all-start.9) | async-done | bytes 2162720 | tf_op jit(solution)/shard_map/all_to_all | solution.py:189
  317.3 4.4 %all-to-all-start.12 = ((bf16[8,528,256]{2,1,0:T(8,128)(2,1)}), bf16[8,528,256]{2,1,0:T(8,128)(2,1)}, u32[]{:S(2)}, u32[]{:S(2)}) async-start(bf16[8,528,256]{2,1,0:T(8,128)(2,1)} %pad_maximum_fusion.1), calls=%async_computation.12 | async-start | bytes 4325376 | tf_op jit(solution)/shard_map/all_to_all | solution.py:189
  322.8 25.4 %all-to-all-done.12 = bf16[8,528,256]{2,1,0:T(8,128)(2,1)} async-done(((bf16[8,528,256]{2,1,0:T(8,128)(2,1)}), bf16[8,528,256]{2,1,0:T(8,128)(2,1)}, u32[]{:S(2)}, u32[]{:S(2)}) %all-to-all-start.12) | async-done | bytes 2162720 | tf_op jit(solution)/shard_map/all_to_all | solution.py:189
  352.7 7.3 %all-to-all-start.13 = ((f32[128,4,512]{2,1,0:T(4,128)}), f32[128,4,512]{2,1,0:T(4,128)S(1)}, u32[]{:S(2)}, u32[]{:S(2)}) async-start(f32[128,4,512]{2,1,0:T(4,128)} %reshape.504), calls=%async_computation.13 | async-start | bytes 2097152 | tf_op jit(solution)/shard_map/all_to_all | solution.py:114
  361.6 17.5 %all-to-all-done.13 = f32[128,4,512]{2,1,0:T(4,128)S(1)} async-done(((f32[128,4,512]{2,1,0:T(4,128)}), f32[128,4,512]{2,1,0:T(4,128)S(1)}, u32[]{:S(2)}, u32[]{:S(2)}) %all-to-all-start.13) | async-done | bytes 1048608 | tf_op jit(solution)/shard_map/all_to_all | solution.py:114
  380.2 4.3 %all-to-all-start.14 = ((bf16[128,4,512]{2,1,0:T(4,128)(2,1)}), bf16[128,4,512]{2,1,0:T(4,128)(2,1)S(1)}, u32[]{:S(2)}, u32[]{:S(2)}) async-start(bf16[128,4,512]{2,1,0:T(4,128)(2,1)} %broadcast_in_dim.46), calls=%async_computation.14 | async-start | bytes 1048576 | tf_op jit(solution)/shard_map/all_to_all | solution.py:109
  387.5 10.9 %all-to-all-done.14 = bf16[128,4,512]{2,1,0:T(4,128)(2,1)S(1)} async-done(((bf16[128,4,512]{2,1,0:T(4,128)(2,1)}), bf16[128,4,512]{2,1,0:T(4,128)(2,1)S(1)}, u32[]{:S(2)}, u32[]{:S(2)}) %all-to-all-start.14) | async-done | bytes 524320 | tf_op jit(solution)/shard_map/all_to_all | solution.py:109
  (102 shorter events, 41.2 us)
Async XLA Ops:
  0.6 1.9 copy-start
  2.5 13.5 %copy-start.13 = (s32[1,16,16]{2,1,0:T(8,128)S(1)}, s32[1,16,16]{2,1,0:T(8,128)}, u32[]{:S(2)}) copy-start(s32[1,16,16]{2,1,0:T(8,128)} %param.16) | copy-start | bytes 3076
  7.6 25.5 %all-to-all-start = ((bf16[16,64,512]{2,1,0:T(8,128)(2,1)}), bf16[16,64,512]{2,1,0:T(8,128)(2,1)S(1)}, u32[]{:S(2)}, u32[]{:S(2)}) async-start(bf16[16,64,512]{2,1,0:T(8,128)(2,1)} %bitcast.2), calls=%async_computation | async-start | bytes 2097152 | tf_op jit(solution)/shard_map/all_to_all | solution.py:136
  33.1 2.0 copy-start.9
  35.1 0.8 copy-start.4
  35.6 31.0 %copy-start.6 = (bf16[512,512]{1,0:T(8,128)(2,1)}, bf16[512,512]{1,0:T(8,128)(2,1)S(1)}, u32[]{:S(2)}) copy-start(bf16[512,512]{1,0:T(8,128)(2,1)S(1)} %convolution_convert_fusion.1) | copy-start | bytes 1572868
  68.0 3.7 copy-start.14
  68.0 28.5 %all-to-all-start.4 = ((bf16[8,512,256]{2,1,0:T(8,128)(2,1)}), bf16[8,512,256]{2,1,0:T(8,128)(2,1)S(1)}, u32[]{:S(2)}, u32[]{:S(2)}) async-start(bf16[8,512,256]{2,1,0:T(8,128)(2,1)} %broadcast_in_dim.37), calls=%async_computation.4 | async-start | bytes 4194304 | tf_op jit(solution)/shard_map/all_to_all | solution.py:109
  96.5 1.4 copy-start.2
  97.9 25.4 %all-to-all-start.2 = ((bf16[2,4096,256]{2,1,0:T(8,128)(2,1)}), bf16[2,4096,256]{2,1,0:T(8,128)(2,1)}, u32[]{:S(2)}, u32[]{:S(2)}) async-start(bf16[2,4096,256]{2,1,0:T(8,128)(2,1)} %bitcast.58), calls=%async_computation.2 | async-start | bytes 8388608 | tf_op jit(solution)/shard_map/all_to_all | solution.py:114
  123.3 10.6 %all-to-all-start.5 = ((bf16[2,4096,256]{2,1,0:T(8,128)(2,1)}), bf16[2,4096,256]{2,1,0:T(8,128)(2,1)}, u32[]{:S(2)}, u32[]{:S(2)}) async-start(bf16[2,4096,256]{2,1,0:T(8,128)(2,1)} %bitcast.59), calls=%async_computation.5 | async-start | bytes 8388608 | tf_op jit(solution)/shard_map/all_to_all | solution.py:114
  133.9 30.9 %all-to-all-start.3 = ((bf16[8,512,256]{2,1,0:T(8,128)(2,1)}), bf16[8,512,256]{2,1,0:T(8,128)(2,1)S(1)}, u32[]{:S(2)}, u32[]{:S(2)}) async-start(bf16[8,512,256]{2,1,0:T(8,128)(2,1)} %bitcast.11), calls=%async_computation.3 | async-start | bytes 4194304 | tf_op jit(solution)/shard_map/all_to_all | solution.py:114
  143.5 26.5 %copy-start.15 = (f32[512]{0:T(512)S(1)}, f32[512]{0:T(512)}, u32[]{:S(2)}) copy-start(f32[512]{0:T(512)} %param.18) | copy-start | bytes 6148
  164.8 31.5 %all-to-all-start.6 = ((bf16[8,512,256]{2,1,0:T(8,128)(2,1)}), bf16[8,512,256]{2,1,0:T(8,128)(2,1)}, u32[]{:S(2)}, u32[]{:S(2)}) async-start(bf16[8,512,256]{2,1,0:T(8,128)(2,1)} %bitcast.14), calls=%async_computation.6 | async-start | bytes 4194304 | tf_op jit(solution)/shard_map/all_to_all | solution.py:114
  170.3 27.9 %copy-start.10 = (bf16[512,512]{1,0:T(8,128)(2,1)S(1)}, bf16[512,512]{1,0:T(8,128)(2,1)}, u32[]{:S(2)}) copy-start(bf16[512,512]{1,0:T(8,128)(2,1)} %param.21) | copy-start | bytes 1572868
  243.3 29.7 %all-to-all-start.10 = ((bf16[8,512,256]{2,1,0:T(8,128)(2,1)}), bf16[8,512,256]{2,1,0:T(8,128)(2,1)S(1)}, u32[]{:S(2)}, u32[]{:S(2)}) async-start(bf16[8,512,256]{2,1,0:T(8,128)(2,1)} %broadcast_in_dim.42), calls=%async_computation.10 | async-start | bytes 4194304 | tf_op jit(solution)/shard_map/all_to_all | solution.py:109
  275.3 6.9 %copy-start.3 = (bf16[4096,256]{1,0:T(8,128)(2,1)S(1)}, bf16[4096,256]{1,0:T(8,128)(2,1)}, u32[]{:S(2)}) copy-start(bf16[4096,256]{1,0:T(8,128)(2,1)} %shard_map.112) | copy-start | bytes 6291460
  275.3 11.0 %all-to-all-start.11 = ((bf16[2,4096,256]{2,1,0:T(8,128)(2,1)}), bf16[2,4096,256]{2,1,0:T(8,128)(2,1)}, u32[]{:S(2)}, u32[]{:S(2)}) async-start(bf16[2,4096,256]{2,1,0:T(8,128)(2,1)} %broadcast_in_dim.44), calls=%async_computation.11 | async-start | bytes 8388608 | tf_op jit(solution)/shard_map/all_to_all | solution.py:109
  286.3 31.0 %all-to-all-start.9 = ((bf16[8,528,256]{2,1,0:T(8,128)(2,1)}), bf16[8,528,256]{2,1,0:T(8,128)(2,1)S(1)}, u32[]{:S(2)}, u32[]{:S(2)}) async-start(bf16[8,528,256]{2,1,0:T(8,128)(2,1)} %pad_maximum_fusion), calls=%async_computation.9 | async-start | bytes 4325376 | tf_op jit(solution)/shard_map/all_to_all | solution.py:189
  317.3 30.9 %all-to-all-start.12 = ((bf16[8,528,256]{2,1,0:T(8,128)(2,1)}), bf16[8,528,256]{2,1,0:T(8,128)(2,1)}, u32[]{:S(2)}, u32[]{:S(2)}) async-start(bf16[8,528,256]{2,1,0:T(8,128)(2,1)} %pad_maximum_fusion.1), calls=%async_computation.12 | async-start | bytes 4325376 | tf_op jit(solution)/shard_map/all_to_all | solution.py:189
  322.0 0.8 copy-start.7
  322.8 28.1 %copy-start.5 = (bf16[512,512]{1,0:T(8,128)(2,1)S(1)}, bf16[512,512]{1,0:T(8,128)(2,1)}, u32[]{:S(2)}) copy-start(bf16[512,512]{1,0:T(8,128)(2,1)} %copy-done.4) | copy-start | bytes 1572868
  350.2 0.7 copy-start.11
  351.4 8.6 %copy-start.8 = (bf16[512,256]{1,0:T(8,128)(2,1)S(1)}, bf16[512,256]{1,0:T(8,128)(2,1)}, u32[]{:S(2)}) copy-start(bf16[512,256]{1,0:T(8,128)(2,1)} %get-tuple-element.57) | copy-start | bytes 786436
  352.7 26.4 %all-to-all-start.13 = ((f32[128,4,512]{2,1,0:T(4,128)}), f32[128,4,512]{2,1,0:T(4,128)S(1)}, u32[]{:S(2)}, u32[]{:S(2)}) async-start(f32[128,4,512]{2,1,0:T(4,128)} %reshape.504), calls=%async_computation.13 | async-start | bytes 2097152 | tf_op jit(solution)/shard_map/all_to_all | solution.py:114
  360.0 25.1 %copy-start.12 = (bf16[512,256]{1,0:T(8,128)(2,1)S(1)}, bf16[512,256]{1,0:T(8,128)(2,1)}, u32[]{:S(2)}) copy-start(bf16[512,256]{1,0:T(8,128)(2,1)} %copy-done.11) | copy-start | bytes 786436
  380.2 18.2 %all-to-all-start.14 = ((bf16[128,4,512]{2,1,0:T(4,128)(2,1)}), bf16[128,4,512]{2,1,0:T(4,128)(2,1)S(1)}, u32[]{:S(2)}, u32[]{:S(2)}) async-start(bf16[128,4,512]{2,1,0:T(4,128)(2,1)} %broadcast_in_dim.46), calls=%async_computation.14 | async-start | bytes 1048576 | tf_op jit(solution)/shard_map/all_to_all | solution.py:109
  385.1 14.9 %copy-start.1 = (bf16[1024,512]{1,0:T(8,128)(2,1)S(1)}, bf16[1024,512]{1,0:T(8,128)(2,1)}, u32[]{:S(2)}) copy-start(bf16[1024,512]{1,0:T(8,128)(2,1)} %param.15) | copy-start | bytes 3145732

commit v11 on v10

--- a/solution.py
+++ b/solution.py
@@ -196,7 +196,7 @@
     local_weight = jnp.einsum("nf,ng->fg", features, proj_grad, preferred_element_type=jnp.float32)
     device_count = blk_size * rep_size
     every = ("blk", "rh", "core")
-    reduced = reduce_by_exchange(local_weight, every, device_count)
+    reduced = reduce_by_exchange(local_weight.reshape(-1, 128), every, device_count)
     weight_sum = (
         gather_by_exchange(reduced.astype(jnp.bfloat16), every, device_count)
         .reshape(-1, feature_width)

time: 403 us -> 402 us (level)
  no operation moved by 1% of the time
where the time goes in v11:
time: 402 us; the launch traced here: 399 us
  waiting for transfers between devices  136 us (34%)
  blocking collectives  72.7 us (18%)
  starting transfers between devices  66.6 us (17%)
  Pallas kernels  66.5 us (17%)
  other arithmetic  31.8 us (8%)
  local copies, waits for them, and re-layouts  21 us (5%)
    all_to_all x3, blocking collectives, gather_by_exchange(): return lax.all_to_all(stacked, axis, 0, 0, tiled=True)  72.7 us
    all_to_all x5, waiting for transfers between devices, reduce_by_exchange(): received = lax.all_to_all(chunks, axis, 0, 0, tiled=True)  64.7 us
    pallas_call x2, Pallas kernels, forward_spmm(): pl.pallas_call(_forward_kernel, grid_spec=grid_spec, out_shape=jax.ShapeD...  33.4 us
    pallas_call x2, Pallas kernels, backward_spmm(): pl.pallas_call(_backward_kernel, grid_spec=grid_spec, out_shape=jax.Shape...  33.1 us
    all_to_all x5, starting transfers between devices, reduce_by_exchange(): received = lax.all_to_all(chunks, axis, 0, 0, tiled=True)  31.5 us
    all_to_all x2, waiting for transfers between devices, per_device(): received = lax.all_to_all(pieces, 'blk', 0, 0, tiled=True)  29.8 us
    all_to_all x4, waiting for transfers between devices, gather_by_exchange(): return lax.all_to_all(stacked, axis, 0, 0, tiled=True)  25.3 us
    all_to_all x4, starting transfers between devices, gather_by_exchange(): return lax.all_to_all(stacked, axis, 0, 0, tiled=True)  18.7 us
  transfers between devices with their start and end apart: 12, of which 10 were waited for; matrix products, arithmetic and copies ran while one was open for 7% of the time, Pallas kernels for 17%

profile of v11, /device:TPU:1, one launch (start us, length us, event | category | flops | bytes accessed | tf_op | source)
XLA Modules:
  0.0 399.3 jit_solution(5838097333941314654)
XLA Ops:
  2.5 5.1 %gather_fusion = bf16[1024,512]{1,0:T(8,128)(2,1)} fusion(bf16[1024,512]{1,0:T(8,128)(2,1)S(1)} %copy-done, s32[1024]{0:T(1024)S(1)} %broadcast_clamp_fusion), kind=kCustom, calls=%fused_computation | custom fusion | bytes 2101248 | tf_op jit(solution)/shard_map/gather | solution.py:135
  7.6 8.4 %all-to-all-start = ((bf16[16,64,512]{2,1,0:T(8,128)(2,1)}), bf16[16,64,512]{2,1,0:T(8,128)(2,1)S(1)}, u32[]{:S(2)}, u32[]{:S(2)}) async-start(bf16[16,64,512]{2,1,0:T(8,128)(2,1)} %bitcast.2), calls=%async_computation | async-start | bytes 2097152 | tf_op jit(solution)/shard_map/all_to_all | solution.py:136
  16.6 16.5 %all-to-all-done = bf16[16,64,512]{2,1,0:T(8,128)(2,1)S(1)} async-done(((bf16[16,64,512]{2,1,0:T(8,128)(2,1)}), bf16[16,64,512]{2,1,0:T(8,128)(2,1)S(1)}, u32[]{:S(2)}, u32[]{:S(2)}) %all-to-all-start) | async-done | bytes 1048608 | tf_op jit(solution)/shard_map/all_to_all | solution.py:136
  35.9 30.6 %all_to_all.75 = bf16[8,512,256]{2,1,0:T(8,128)(2,1)} all-to-all(bf16[8,512,256]{2,1,0:T(8,128)(2,1)S(1)} %broadcast_in_dim.36), channel_id=1, replica_groups=mesh['blk'=8,'rh'=8,'core'=2] {'blk'}, dimensions={0} | all-to-all | bytes 4194304 | tf_op jit(solution)/shard_map/all_to_all | solution.py:109
  68.0 3.7 all-to-all-start.4
  74.1 16.7 %shard_map.110 = bf16[32,256,256]{2,1,0:T(8,128)(2,1)} custom-call(s32[16,6]{1,0:T(8,128)} %fusion.6.rows_ref, s32[16,6]{1,0:T(8,128)} %reshape.501.first_ref, s32[32]{0:T(128)} %convert_element_type.134.touched_ref, bf16[16,6,256,256]{3,2,1,0:T(8,128)(2,1)} %bitcast.52, bf16[4096,256]{1,0:T(8,128)(2,1)} %bitcast.61), custom_call_target="tpu_custom_call" | custom-call | tf_op jit(solution)/shard_map/pallas_call | solution.py:57
  90.8 5.7 %all-to-all-done.4 = bf16[8,512,256]{2,1,0:T(8,128)(2,1)S(1)} async-done(((bf16[8,512,256]{2,1,0:T(8,128)(2,1)}), bf16[8,512,256]{2,1,0:T(8,128)(2,1)S(1)}, u32[]{:S(2)}, u32[]{:S(2)}) %all-to-all-start.4) | async-done | bytes 2097184 | tf_op jit(solution)/shard_map/all_to_all | solution.py:109
  97.9 8.7 %all-to-all-start.2 = ((bf16[2,4096,256]{2,1,0:T(8,128)(2,1)}), bf16[2,4096,256]{2,1,0:T(8,128)(2,1)}, u32[]{:S(2)}, u32[]{:S(2)}) async-start(bf16[2,4096,256]{2,1,0:T(8,128)(2,1)} %bitcast.58), calls=%async_computation.2 | async-start | bytes 8388608 | tf_op jit(solution)/shard_map/all_to_all | solution.py:114
  106.6 16.7 %shard_map.111 = bf16[32,256,256]{2,1,0:T(8,128)(2,1)} custom-call(s32[16,6]{1,0:T(8,128)} %fusion.6.rows_ref, s32[16,6]{1,0:T(8,128)} %reshape.501.first_ref, s32[32]{0:T(128)} %convert_element_type.134.touched_ref, bf16[16,6,256,256]{3,2,1,0:T(8,128)(2,1)} %bitcast.53, bf16[4096,256]{1,0:T(8,128)(2,1)} %bitcast.60), custom_call_target="tpu_custom_call" | custom-call | tf_op jit(solution)/shard_map/pallas_call | solution.py:57
  123.3 5.6 %all-to-all-start.5 = ((bf16[2,4096,256]{2,1,0:T(8,128)(2,1)}), bf16[2,4096,256]{2,1,0:T(8,128)(2,1)}, u32[]{:S(2)}, u32[]{:S(2)}) async-start(bf16[2,4096,256]{2,1,0:T(8,128)(2,1)} %bitcast.59), calls=%async_computation.5 | async-start | bytes 8388608 | tf_op jit(solution)/shard_map/all_to_all | solution.py:114
  128.9 4.9 %reduce_sum.114 = bf16[4096,256]{1,0:T(8,128)(2,1)} reduce(bf16[2,4096,256]{2,1,0:T(8,128)(2,1)} %all-to-all-done.2, bf16[]{:T(256)} %constant.191.clone.1), dimensions={0}, to_apply=%region_6.7 | reduce | flops 1048576 | bytes 6291458 | tf_op jit(solution)/shard_map/reduce_sum | solution.py:115
  133.9 4.7 %all-to-all-start.3 = ((bf16[8,512,256]{2,1,0:T(8,128)(2,1)}), bf16[8,512,256]{2,1,0:T(8,128)(2,1)S(1)}, u32[]{:S(2)}, u32[]{:S(2)}) async-start(bf16[8,512,256]{2,1,0:T(8,128)(2,1)} %bitcast.11), calls=%async_computation.3 | async-start | bytes 4194304 | tf_op jit(solution)/shard_map/all_to_all | solution.py:114
  138.6 4.9 %reduce_sum.116 = bf16[4096,256]{1,0:T(8,128)(2,1)} reduce(bf16[2,4096,256]{2,1,0:T(8,128)(2,1)} %all-to-all-done.5, bf16[]{:T(256)} %constant.191.clone.1), dimensions={0}, to_apply=%region_8.9 | reduce | flops 1048576 | bytes 6291458 | tf_op jit(solution)/shard_map/reduce_sum | solution.py:115
  143.5 21.3 %all-to-all-done.3 = bf16[8,512,256]{2,1,0:T(8,128)(2,1)S(1)} async-done(((bf16[8,512,256]{2,1,0:T(8,128)(2,1)}), bf16[8,512,256]{2,1,0:T(8,128)(2,1)S(1)}, u32[]{:S(2)}, u32[]{:S(2)}) %all-to-all-start.3) | async-done | bytes 2097184 | tf_op jit(solution)/shard_map/all_to_all | solution.py:114
  164.8 5.2 %all-to-all-start.6 = ((bf16[8,512,256]{2,1,0:T(8,128)(2,1)}), bf16[8,512,256]{2,1,0:T(8,128)(2,1)}, u32[]{:S(2)}, u32[]{:S(2)}) async-start(bf16[8,512,256]{2,1,0:T(8,128)(2,1)} %bitcast.14), calls=%async_computation.6 | async-start | bytes 4194304 | tf_op jit(solution)/shard_map/all_to_all | solution.py:114
  170.3 26.0 %all-to-all-done.6 = bf16[8,512,256]{2,1,0:T(8,128)(2,1)} async-done(((bf16[8,512,256]{2,1,0:T(8,128)(2,1)}), bf16[8,512,256]{2,1,0:T(8,128)(2,1)}, u32[]{:S(2)}, u32[]{:S(2)}) %all-to-all-start.6) | async-done | bytes 2097184 | tf_op jit(solution)/shard_map/all_to_all | solution.py:114
  199.5 31.8 %all_to_all.76 = bf16[8,512,256]{2,1,0:T(8,128)(2,1)S(1)} all-to-all(bf16[8,512,256]{2,1,0:T(8,128)(2,1)S(1)} %broadcast_in_dim.38), channel_id=1, replica_groups=mesh['blk'=8,'rh'=8,'core'=2] {'rh'}, dimensions={0} | all-to-all | bytes 4194304 | tf_op jit(solution)/shard_map/all_to_all | solution.py:109
  231.6 10.2 %all_to_all.77 = bf16[2,4096,256]{2,1,0:T(8,128)(2,1)} all-to-all(bf16[2,4096,256]{2,1,0:T(8,128)(2,1)S(1)} %broadcast_in_dim.40), channel_id=1, replica_groups=mesh['blk'=8,'rh'=8,'core'=2] {'core'}, dimensions={0} | all-to-all | bytes 8388608 | tf_op jit(solution)/shard_map/all_to_all | solution.py:109
  243.3 3.8 all-to-all-start.10
  250.4 16.6 %shard_map.112 = bf16[4096,256]{1,0:T(8,128)(2,1)} custom-call(s32[16,6]{1,0:T(8,128)} %fusion.6.rows_ref, bf16[16,6,256,256]{3,2,1,0:T(8,128)(2,1)} %bitcast.54, bf16[32,256,256]{2,1,0:T(8,128)(2,1)} %bitcast.56), custom_call_target="tpu_custom_call" | custom-call | tf_op jit(solution)/shard_map/pallas_call | solution.py:96
  267.0 6.1 %all-to-all-done.10 = bf16[8,512,256]{2,1,0:T(8,128)(2,1)S(1)} async-done(((bf16[8,512,256]{2,1,0:T(8,128)(2,1)}), bf16[8,512,256]{2,1,0:T(8,128)(2,1)S(1)}, u32[]{:S(2)}, u32[]{:S(2)}) %all-to-all-start.10) | async-done | bytes 2097184 | tf_op jit(solution)/shard_map/all_to_all | solution.py:109
  275.3 6.9 %all-to-all-start.11 = ((bf16[2,4096,256]{2,1,0:T(8,128)(2,1)}), bf16[2,4096,256]{2,1,0:T(8,128)(2,1)}, u32[]{:S(2)}, u32[]{:S(2)}) async-start(bf16[2,4096,256]{2,1,0:T(8,128)(2,1)} %broadcast_in_dim.44), calls=%async_computation.11 | async-start | bytes 8388608 | tf_op jit(solution)/shard_map/all_to_all | solution.py:109
  286.3 3.6 all-to-all-start.9
  290.0 3.3 convert_reduce_fusion
  293.3 16.5 %shard_map.113 = bf16[4096,256]{1,0:T(8,128)(2,1)} custom-call(s32[16,6]{1,0:T(8,128)} %fusion.6.rows_ref, bf16[16,6,256,256]{3,2,1,0:T(8,128)(2,1)} %bitcast.55, bf16[32,256,256]{2,1,0:T(8,128)(2,1)} %bitcast.20.grad_ref), custom_call_target="tpu_custom_call" | custom-call | tf_op jit(solution)/shard_map/pallas_call | solution.py:96
  312.9 4.4 %all-to-all-done.9 = bf16[8,528,256]{2,1,0:T(8,128)(2,1)S(1)} async-done(((bf16[8,528,256]{2,1,0:T(8,128)(2,1)}), bf16[8,528,256]{2,1,0:T(8,128)(2,1)S(1)}, u32[]{:S(2)}, u32[]{:S(2)}) %all-to-all-start.9) | async-done | bytes 2162720 | tf_op jit(solution)/shard_map/all_to_all | solution.py:189
  317.3 4.4 %all-to-all-start.12 = ((bf16[8,528,256]{2,1,0:T(8,128)(2,1)}), bf16[8,528,256]{2,1,0:T(8,128)(2,1)}, u32[]{:S(2)}, u32[]{:S(2)}) async-start(bf16[8,528,256]{2,1,0:T(8,128)(2,1)} %pad_maximum_fusion.1), calls=%async_computation.12 | async-start | bytes 4325376 | tf_op jit(solution)/shard_map/all_to_all | solution.py:189
  322.8 25.4 %all-to-all-done.12 = bf16[8,528,256]{2,1,0:T(8,128)(2,1)} async-done(((bf16[8,528,256]{2,1,0:T(8,128)(2,1)}), bf16[8,528,256]{2,1,0:T(8,128)(2,1)}, u32[]{:S(2)}, u32[]{:S(2)}) %all-to-all-start.12) | async-done | bytes 2162720 | tf_op jit(solution)/shard_map/all_to_all | solution.py:189
  352.5 7.3 %all-to-all-start.13 = ((f32[128,16,128]{2,1,0:T(8,128)}), f32[128,16,128]{2,1,0:T(8,128)S(1)}, u32[]{:S(2)}, u32[]{:S(2)}) async-start(f32[128,16,128]{2,1,0:T(8,128)} %reshape_reshape.11), calls=%async_computation.13 | async-start | bytes 2097152 | tf_op jit(solution)/shard_map/all_to_all | solution.py:114
  361.4 17.5 %all-to-all-done.13 = f32[128,16,128]{2,1,0:T(8,128)S(1)} async-done(((f32[128,16,128]{2,1,0:T(8,128)}), f32[128,16,128]{2,1,0:T(8,128)S(1)}, u32[]{:S(2)}, u32[]{:S(2)}) %all-to-all-start.13) | async-done | bytes 1048608 | tf_op jit(solution)/shard_map/all_to_all | solution.py:114
  379.9 4.3 %all-to-all-start.14 = ((bf16[128,16,128]{2,1,0:T(8,128)(2,1)}), bf16[128,16,128]{2,1,0:T(8,128)(2,1)S(1)}, u32[]{:S(2)}, u32[]{:S(2)}) async-start(bf16[128,16,128]{2,1,0:T(8,128)(2,1)} %broadcast_in_dim.46), calls=%async_computation.14 | async-start | bytes 1048576 | tf_op jit(solution)/shard_map/all_to_all | solution.py:109
  387.1 10.9 %all-to-all-done.14 = bf16[128,16,128]{2,1,0:T(8,128)(2,1)S(1)} async-done(((bf16[128,16,128]{2,1,0:T(8,128)(2,1)}), bf16[128,16,128]{2,1,0:T(8,128)(2,1)S(1)}, u32[]{:S(2)}, u32[]{:S(2)}) %all-to-all-start.14) | async-done | bytes 524320 | tf_op jit(solution)/shard_map/all_to_all | solution.py:109
  (102 shorter events, 40.5 us)
Async XLA Ops:
  0.6 1.9 copy-start
  2.5 13.5 %copy-start.13 = (s32[1,16,16]{2,1,0:T(8,128)S(1)}, s32[1,16,16]{2,1,0:T(8,128)}, u32[]{:S(2)}) copy-start(s32[1,16,16]{2,1,0:T(8,128)} %param.16) | copy-start | bytes 3076
  7.6 25.5 %all-to-all-start = ((bf16[16,64,512]{2,1,0:T(8,128)(2,1)}), bf16[16,64,512]{2,1,0:T(8,128)(2,1)S(1)}, u32[]{:S(2)}, u32[]{:S(2)}) async-start(bf16[16,64,512]{2,1,0:T(8,128)(2,1)} %bitcast.2), calls=%async_computation | async-start | bytes 2097152 | tf_op jit(solution)/shard_map/all_to_all | solution.py:136
  33.1 2.0 copy-start.9
  35.1 0.8 copy-start.4
  35.6 31.0 %copy-start.6 = (bf16[512,512]{1,0:T(8,128)(2,1)}, bf16[512,512]{1,0:T(8,128)(2,1)S(1)}, u32[]{:S(2)}) copy-start(bf16[512,512]{1,0:T(8,128)(2,1)S(1)} %convolution_convert_fusion.1) | copy-start | bytes 1572868
  68.0 3.7 copy-start.14
  68.0 28.5 %all-to-all-start.4 = ((bf16[8,512,256]{2,1,0:T(8,128)(2,1)}), bf16[8,512,256]{2,1,0:T(8,128)(2,1)S(1)}, u32[]{:S(2)}, u32[]{:S(2)}) async-start(bf16[8,512,256]{2,1,0:T(8,128)(2,1)} %broadcast_in_dim.37), calls=%async_computation.4 | async-start | bytes 4194304 | tf_op jit(solution)/shard_map/all_to_all | solution.py:109
  96.5 1.4 copy-start.2
  97.9 25.4 %all-to-all-start.2 = ((bf16[2,4096,256]{2,1,0:T(8,128)(2,1)}), bf16[2,4096,256]{2,1,0:T(8,128)(2,1)}, u32[]{:S(2)}, u32[]{:S(2)}) async-start(bf16[2,4096,256]{2,1,0:T(8,128)(2,1)} %bitcast.58), calls=%async_computation.2 | async-start | bytes 8388608 | tf_op jit(solution)/shard_map/all_to_all | solution.py:114
  123.3 10.6 %all-to-all-start.5 = ((bf16[2,4096,256]{2,1,0:T(8,128)(2,1)}), bf16[2,4096,256]{2,1,0:T(8,128)(2,1)}, u32[]{:S(2)}, u32[]{:S(2)}) async-start(bf16[2,4096,256]{2,1,0:T(8,128)(2,1)} %bitcast.59), calls=%async_computation.5 | async-start | bytes 8388608 | tf_op jit(solution)/shard_map/all_to_all | solution.py:114
  133.9 30.9 %all-to-all-start.3 = ((bf16[8,512,256]{2,1,0:T(8,128)(2,1)}), bf16[8,512,256]{2,1,0:T(8,128)(2,1)S(1)}, u32[]{:S(2)}, u32[]{:S(2)}) async-start(bf16[8,512,256]{2,1,0:T(8,128)(2,1)} %bitcast.11), calls=%async_computation.3 | async-start | bytes 4194304 | tf_op jit(solution)/shard_map/all_to_all | solution.py:114
  143.5 26.5 %copy-start.15 = (f32[512]{0:T(512)S(1)}, f32[512]{0:T(512)}, u32[]{:S(2)}) copy-start(f32[512]{0:T(512)} %param.18) | copy-start | bytes 6148
  164.8 31.5 %all-to-all-start.6 = ((bf16[8,512,256]{2,1,0:T(8,128)(2,1)}), bf16[8,512,256]{2,1,0:T(8,128)(2,1)}, u32[]{:S(2)}, u32[]{:S(2)}) async-start(bf16[8,512,256]{2,1,0:T(8,128)(2,1)} %bitcast.14), calls=%async_computation.6 | async-start | bytes 4194304 | tf_op jit(solution)/shard_map/all_to_all | solution.py:114
  170.3 27.9 %copy-start.10 = (bf16[512,512]{1,0:T(8,128)(2,1)S(1)}, bf16[512,512]{1,0:T(8,128)(2,1)}, u32[]{:S(2)}) copy-start(bf16[512,512]{1,0:T(8,128)(2,1)} %param.21) | copy-start | bytes 1572868
  243.3 29.7 %all-to-all-start.10 = ((bf16[8,512,256]{2,1,0:T(8,128)(2,1)}), bf16[8,512,256]{2,1,0:T(8,128)(2,1)S(1)}, u32[]{:S(2)}, u32[]{:S(2)}) async-start(bf16[8,512,256]{2,1,0:T(8,128)(2,1)} %broadcast_in_dim.42), calls=%async_computation.10 | async-start | bytes 4194304 | tf_op jit(solution)/shard_map/all_to_all | solution.py:109
  275.3 6.9 %copy-start.3 = (bf16[4096,256]{1,0:T(8,128)(2,1)S(1)}, bf16[4096,256]{1,0:T(8,128)(2,1)}, u32[]{:S(2)}) copy-start(bf16[4096,256]{1,0:T(8,128)(2,1)} %shard_map.112) | copy-start | bytes 6291460
  275.3 11.0 %all-to-all-start.11 = ((bf16[2,4096,256]{2,1,0:T(8,128)(2,1)}), bf16[2,4096,256]{2,1,0:T(8,128)(2,1)}, u32[]{:S(2)}, u32[]{:S(2)}) async-start(bf16[2,4096,256]{2,1,0:T(8,128)(2,1)} %broadcast_in_dim.44), calls=%async_computation.11 | async-start | bytes 8388608 | tf_op jit(solution)/shard_map/all_to_all | solution.py:109
  286.3 31.0 %all-to-all-start.9 = ((bf16[8,528,256]{2,1,0:T(8,128)(2,1)}), bf16[8,528,256]{2,1,0:T(8,128)(2,1)S(1)}, u32[]{:S(2)}, u32[]{:S(2)}) async-start(bf16[8,528,256]{2,1,0:T(8,128)(2,1)} %pad_maximum_fusion), calls=%async_computation.9 | async-start | bytes 4325376 | tf_op jit(solution)/shard_map/all_to_all | solution.py:189
  317.3 30.9 %all-to-all-start.12 = ((bf16[8,528,256]{2,1,0:T(8,128)(2,1)}), bf16[8,528,256]{2,1,0:T(8,128)(2,1)}, u32[]{:S(2)}, u32[]{:S(2)}) async-start(bf16[8,528,256]{2,1,0:T(8,128)(2,1)} %pad_maximum_fusion.1), calls=%async_computation.12 | async-start | bytes 4325376 | tf_op jit(solution)/shard_map/all_to_all | solution.py:189
  322.0 0.8 copy-start.7
  322.8 28.1 %copy-start.5 = (bf16[512,512]{1,0:T(8,128)(2,1)S(1)}, bf16[512,512]{1,0:T(8,128)(2,1)}, u32[]{:S(2)}) copy-start(bf16[512,512]{1,0:T(8,128)(2,1)} %copy-done.4) | copy-start | bytes 1572868
  350.2 0.7 copy-start.11
  351.4 8.4 %copy-start.8 = (bf16[512,256]{1,0:T(8,128)(2,1)S(1)}, bf16[512,256]{1,0:T(8,128)(2,1)}, u32[]{:S(2)}) copy-start(bf16[512,256]{1,0:T(8,128)(2,1)} %get-tuple-element.57) | copy-start | bytes 786436
  352.5 26.4 %all-to-all-start.13 = ((f32[128,16,128]{2,1,0:T(8,128)}), f32[128,16,128]{2,1,0:T(8,128)S(1)}, u32[]{:S(2)}, u32[]{:S(2)}) async-start(f32[128,16,128]{2,1,0:T(8,128)} %reshape_reshape.11), calls=%async_computation.13 | async-start | bytes 2097152 | tf_op jit(solution)/shard_map/all_to_all | solution.py:114
  359.8 25.0 %copy-start.12 = (bf16[512,256]{1,0:T(8,128)(2,1)S(1)}, bf16[512,256]{1,0:T(8,128)(2,1)}, u32[]{:S(2)}) copy-start(bf16[512,256]{1,0:T(8,128)(2,1)} %copy-done.11) | copy-start | bytes 786436
  379.9 18.2 %all-to-all-start.14 = ((bf16[128,16,128]{2,1,0:T(8,128)(2,1)}), bf16[128,16,128]{2,1,0:T(8,128)(2,1)S(1)}, u32[]{:S(2)}, u32[]{:S(2)}) async-start(bf16[128,16,128]{2,1,0:T(8,128)(2,1)} %broadcast_in_dim.46), calls=%async_computation.14 | async-start | bytes 1048576 | tf_op jit(solution)/shard_map/all_to_all | solution.py:109
  384.7 14.5 %copy-start.1 = (bf16[1024,512]{1,0:T(8,128)(2,1)S(1)}, bf16[1024,512]{1,0:T(8,128)(2,1)}, u32[]{:S(2)}) copy-start(bf16[1024,512]{1,0:T(8,128)(2,1)} %param.15) | copy-start | bytes 3145732
